TPU v7x, 256 devices: a whole 4x4x8 slice. The times are simulated.
256 devices in a mesh: vocab: 32 (over x, z), fsdp: 8 (over y, core).
Axes of the slice: x: 4, y: 4, z: 8, core: 2. Of those that a mesh axis runs over, the one named last changes fastest.
Arguments:
- hidden: bfloat16 [131072, 2048], P(('vocab', 'fsdp')), may hold values from -100 to 100
- head_weight: bfloat16 [262144, 2048], P(('vocab', 'fsdp')), may hold values from -2.5 to 2.5
- language_blocks: int32 [256, 6], replicated, may hold values from 0 to 7, as said below
- language_owner: int32 [256], replicated, may hold values from 0 to 255, each once
- token_language: int32 [131072, 1], P(('vocab', 'fsdp')), may hold values from 0 to 255; in each aligned block of 512 rows (0 to 511, 512 to 1023, ...) at most 4 rows name the same one
- labels: int32 [131072], P(('vocab', 'fsdp')), may hold values from 0 to 767
- loss_weight: bfloat16 [131072], P(('vocab', 'fsdp')), may hold values from 1 to 16
Outputs:
- hidden_grad: bfloat16 [131072, 2048], P(('vocab', 'fsdp'))
- token_loss: bfloat16 [131072], P(('vocab', 'fsdp'))
- head_grad: bfloat16 [262144, 2048], P(('vocab', 'fsdp'))
Inputs may be any that keep to these rules, and one draw needn't show every extreme that they name: `language_blocks`: each row names 6 different blocks. `language_owner`: each language slot is named by exactly one language. `token_language`: in each aligned group of 512 tokens no language is named more than 4 times, a bound that some block reaches in some or all groups.
All inputs are finite; a program needn't handle non-finite values.
Results may differ from a plain program's by a relative error of at most 0.0049.
Values may be sent and summed in bfloat16 or wider, within the bound.
No kernel may reach another device: no remote copies, remote signals or barrier semaphores. Data moves between devices by JAX's collectives and lax.ppermute only.
A program may use at most 128 MiB of HBM per device.

v0:
```python
import jax
import jax.numpy as jnp
from jax import lax
from jax.sharding import PartitionSpec as P

D = 2048
BLOCK = 128
SB = 8
LB = 6
CAP = 4
EXTRA = 128
LABEL_SPLIT = 128

SMOOTH = 0.1
AXES = ("vocab", "fsdp")


def smoothed_loss(logits, targets, weights):
    columns = logits.shape[1]
    row_max = jnp.max(logits, axis=1, keepdims=True)
    shifted = logits - row_max
    log_probs = shifted - jnp.log(jnp.sum(jnp.exp(shifted), axis=1, keepdims=True))
    onehot = (lax.broadcasted_iota(jnp.int32, logits.shape, 1) == targets[:, None]).astype(
        jnp.float32
    )
    losses = -(1.0 - SMOOTH) * jnp.sum(onehot * log_probs, axis=1) - SMOOTH / columns * jnp.sum(
        log_probs, axis=1
    )
    grads = weights.astype(jnp.float32)[:, None] * (
        jnp.exp(log_probs) - (1.0 - SMOOTH) * onehot - SMOOTH / columns
    )
    return (losses.astype(jnp.bfloat16), grads.astype(jnp.bfloat16))


def place_tokens(token_language, language_owner):
    language = token_language[:, 0]
    languages = language_owner.shape[0]
    matches = language[:, None] == jnp.arange(languages, dtype=jnp.int32)[None, :]
    slot_ids = jnp.sum(jnp.where(matches, language_owner[None, :], 0), axis=1)
    positions = jnp.arange(language.shape[0], dtype=jnp.int32)
    earlier = (language[:, None] == language[None, :]) & (positions[None, :] < positions[:, None])
    rank_in_group = jnp.sum(earlier.astype(jnp.int32), axis=1)
    return slot_ids * CAP + rank_in_group


def shards(
    hidden, head_weight, language_blocks, language_owner, token_language, labels, loss_weight
):
    devices = lax.axis_size(AXES)
    tokens, features = hidden.shape
    places = devices * CAP
    width = features + EXTRA
    assert head_weight.shape[0] == SB * BLOCK

    target_place = place_tokens(token_language, language_owner)
    place_hot = (
        lax.broadcasted_iota(jnp.int32, (places, tokens), 0) == target_place[None, :]
    ).astype(jnp.bfloat16)

    extra_cols = lax.broadcasted_iota(jnp.int32, (tokens, EXTRA), 1)
    label_hi = (labels // LABEL_SPLIT).astype(jnp.bfloat16)
    label_lo = (labels % LABEL_SPLIT).astype(jnp.bfloat16)
    extras = jnp.where(
        extra_cols == 0,
        loss_weight[:, None],
        jnp.where(
            extra_cols == 1,
            label_hi[:, None],
            jnp.where(extra_cols == 2, label_lo[:, None], jnp.zeros((), jnp.bfloat16)),
        ),
    )
    packed = jnp.concatenate([hidden, extras], axis=1)
    send = jnp.dot(place_hot, packed, preferred_element_type=jnp.float32).astype(jnp.bfloat16)

    received = lax.all_to_all(
        send.reshape(devices, CAP, width), AXES, split_axis=0, concat_axis=0, tiled=True
    ).reshape(places, width)

    token_rows = received[:, :features]
    weights = received[:, features]
    targets = (
        received[:, features + 1].astype(jnp.int32) * LABEL_SPLIT
        + received[:, features + 2].astype(jnp.int32)
    )

    self_index = lax.axis_index(AXES)
    owned_mask = (language_owner == self_index).astype(jnp.int32)
    blocks = jnp.sum(owned_mask[:, None] * language_blocks, axis=0)
    slab = head_weight.reshape(SB, BLOCK, features)
    candidates = jnp.take(slab, blocks, axis=0).reshape(LB * BLOCK, features)

    logits = lax.dot_general(
        token_rows, candidates, (((1,), (1,)), ((), ())), preferred_element_type=jnp.float32
    )
    losses, grads = smoothed_loss(logits, targets, weights)
    row_grads = jnp.dot(grads, candidates, preferred_element_type=jnp.float32).astype(
        jnp.bfloat16
    )

    block_hot = blocks[None, :] == jnp.arange(SB, dtype=jnp.int32)[:, None]
    listed = jnp.any(block_hot, axis=1)
    list_index = jnp.sum(
        jnp.where(block_hot, jnp.arange(LB, dtype=jnp.int32)[None, :], 0), axis=1
    )
    grads_by_block = grads.reshape(places, LB, BLOCK)
    expanded = jnp.where(
        listed[None, :, None],
        jnp.take(grads_by_block, list_index, axis=1),
        jnp.zeros((), jnp.bfloat16),
    ).reshape(places, SB * BLOCK)
    head_grad = lax.dot_general(
        expanded, token_rows, (((0,), (0,)), ((), ())), preferred_element_type=jnp.float32
    ).astype(jnp.bfloat16)

    back_cols = lax.broadcasted_iota(jnp.int32, (places, EXTRA), 1)
    back_extras = jnp.where(back_cols == 0, losses[:, None], jnp.zeros((), jnp.bfloat16))
    back = jnp.concatenate([row_grads, back_extras], axis=1)
    returned = lax.all_to_all(
        back.reshape(devices, CAP, width), AXES, split_axis=0, concat_axis=0, tiled=True
    ).reshape(places, width)

    gathered = lax.dot_general(
        place_hot, returned, (((0,), (0,)), ((), ())), preferred_element_type=jnp.float32
    )
    hidden_grad = gathered[:, :features].astype(jnp.bfloat16)
    token_loss = gathered[:, features].astype(jnp.bfloat16)
    return (hidden_grad, token_loss, head_grad)


def solution(mesh):
    in_specs = (
        P(AXES, None),
        P(AXES, None),
        P(),
        P(),
        P(AXES, None),
        P(AXES),
        P(AXES),
    )
    out_specs = (P(AXES, None), P(AXES), P(AXES, None))
    return jax.shard_map(shards, mesh=mesh, in_specs=in_specs, out_specs=out_specs, check_vma=False)
```

profile of v0, /device:TPU:1, one launch (start us, length us, event | category | flops | bytes accessed | tf_op | source)
XLA Modules:
  0.0 292.8 jit_solution(13144603630878875125)
XLA Ops:
  1.3 1.0 convert_reduce_fusion
  3.3 0.9 select_select_fusion
  4.3 5.9 %convolution_convert_fusion = bf16[1024,2176]{1,0:T(8,128)(2,1)} fusion(bf16[512,128]{1,0:T(8,128)(2,1)S(1)} %select_select_fusion, bf16[512,2048]{1,0:T(8,128)(2,1)} %param.7, s32[512]{0:T(512)S(1)} %multiply_add_fusion), kind=kOutput, calls=%fused_computation.2 | convolution fusion | flops 2288910336 | bytes 6686720 | tf_op jit(solution)/shard_map/dot_general | solution.py:73
  10.2 7.1 %reshape.95 = bf16[256,4,2176]{2,1,0:T(4,128)(2,1)} reshape(bf16[1024,2176]{1,0:T(8,128)(2,1)} %convolution_convert_fusion) | data formatting | bytes 8912896 | tf_op jit(solution)/shard_map/reshape | solution.py:76
  17.2 16.5 %all-to-all-start = ((bf16[256,4,2176]{2,1,0:T(4,128)(2,1)}), bf16[256,4,2176]{2,1,0:T(4,128)(2,1)}, u32[]{:S(2)}, u32[]{:S(2)}) async-start(bf16[256,4,2176]{2,1,0:T(4,128)(2,1)} %reshape.95), calls=%async_computation | async-start | bytes 8912896 | tf_op jit(solution)/shard_map/all_to_all | solution.py:75
  33.9 2.9 %gather_fusion = bf16[6,128,2048]{2,1,0:T(8,128)(2,1)S(1)} fusion(bf16[8,128,2048]{2,1,0:T(8,128)(2,1)} %bitcast.31, s32[1024]{0:T(1024)S(1)} %pad_clamp_fusion.1), kind=kCustom, calls=%fused_computation | custom fusion | bytes 6291480 | tf_op jit(solution)/shard_map/jit(_take)/gather | solution.py:90
  37.0 2.2 bitcast_select_fusion
  39.2 97.7 %all-to-all-done = bf16[256,4,2176]{2,1,0:T(4,128)(2,1)} async-done(((bf16[256,4,2176]{2,1,0:T(4,128)(2,1)}), bf16[256,4,2176]{2,1,0:T(4,128)(2,1)}, u32[]{:S(2)}, u32[]{:S(2)}) %all-to-all-start) | async-done | bytes 4456480 | tf_op jit(solution)/shard_map/all_to_all | solution.py:75
  136.9 7.0 %reshape.96 = bf16[1024,2176]{1,0:T(8,128)(2,1)} reshape(bf16[256,4,2176]{2,1,0:T(4,128)(2,1)} %all-to-all-done) | data formatting | bytes 8912896 | tf_op jit(solution)/shard_map/reshape | solution.py:77
  143.9 1.4 add_reduce_fusion
  145.3 1.1 convert_reduce_fusion.1
  146.5 5.3 %fusion.18 = (f32[1024]{0:T(1024)S(1)}, f32[1024,768]{0,1:T(8,128)S(1)}) fusion(bf16[768,2048]{1,0:T(8,128)(2,1)S(1)} %copy-done, bf16[1024,2176]{1,0:T(8,128)(2,1)} %reshape.96), kind=kOutput, calls=%fused_computation.69 | convolution fusion | flops 3222010880 | bytes 10489856 | tf_op jit(solution)/shard_map/dot_general | solution.py:92
  152.3 1.4 select_reduce_fusion
  154.1 3.7 %convolution_convert_fusion.2 = bf16[1024,2048]{1,0:T(8,128)(2,1)S(1)} fusion(bf16[1024,768]{0,1:T(8,128)(2,1)S(1)} %get-tuple-element.5, bf16[768,2048]{1,0:T(8,128)(2,1)S(1)} %copy-done.1), kind=kOutput, calls=%fused_computation.5 | convolution fusion | flops 3223322624 | bytes 8912896 | tf_op jit(solution)/shard_map/dot_general | solution.py:96
  157.8 2.5 pad_maximum_fusion
  160.3 7.1 %reshape.98 = bf16[256,4,2176]{2,1,0:T(4,128)(2,1)} reshape(bf16[1024,2176]{1,0:T(8,128)(2,1)} %pad_maximum_fusion) | data formatting | bytes 8912896 | tf_op jit(solution)/shard_map/reshape | solution.py:119
  167.4 7.7 %all-to-all-start.1 = ((bf16[256,4,2176]{2,1,0:T(4,128)(2,1)}), bf16[256,4,2176]{2,1,0:T(4,128)(2,1)}, u32[]{:S(2)}, u32[]{:S(2)}) async-start(bf16[256,4,2176]{2,1,0:T(4,128)(2,1)} %reshape.98), calls=%async_computation.1 | async-start | bytes 8912896 | tf_op jit(solution)/shard_map/all_to_all | solution.py:118
  175.5 2.0 gather_fusion.1
  177.5 2.1 fusion.7
  179.6 8.2 %convolution_convert_fusion.3 = bf16[1024,2048]{1,0:T(8,128)(2,1)} fusion(bf16[1024,1024]{0,1:T(8,128)(2,1)S(1)} %fusion.7, bf16[1024,2176]{1,0:T(8,128)(2,1)} %reshape.96), kind=kOutput, calls=%fused_computation.6 | convolution fusion | flops 4297064448 | bytes 10485760 | tf_op jit(solution)/shard_map/dot_general | solution.py:111
  187.8 90.5 %all-to-all-done.1 = bf16[256,4,2176]{2,1,0:T(4,128)(2,1)} async-done(((bf16[256,4,2176]{2,1,0:T(4,128)(2,1)}), bf16[256,4,2176]{2,1,0:T(4,128)(2,1)}, u32[]{:S(2)}, u32[]{:S(2)}) %all-to-all-start.1) | async-done | bytes 4456480 | tf_op jit(solution)/shard_map/all_to_all | solution.py:118
  278.3 7.0 %reshape.99 = bf16[1024,2176]{1,0:T(8,128)(2,1)} reshape(bf16[256,4,2176]{2,1,0:T(4,128)(2,1)} %all-to-all-done.1) | data formatting | bytes 8912896 | tf_op jit(solution)/shard_map/reshape | solution.py:120
  285.4 5.2 %convolution_convert_fusion.1 = bf16[512,2176]{1,0:T(8,128)(2,1)S(1)} fusion(bf16[1024,2176]{1,0:T(8,128)(2,1)} %reshape.99, s32[512]{0:T(512)S(1)} %multiply_add_fusion), kind=kOutput, calls=%fused_computation.3 | convolution fusion | flops 2283339776 | bytes 6686720 | tf_op jit(solution)/shard_map/dot_general | solution.py:122
  290.5 1.6 slice.34
  (30 shorter events, 3.8 us)
Async XLA Ops:
  17.2 16.6 %copy-start.3 = (s32[256]{0:T(256)S(1)}, s32[256]{0:T(256)}, u32[]{:S(2)}) copy-start(s32[256]{0:T(256)} %param.10) | copy-start | bytes 3076
  17.2 16.6 %copy-start.2 = (s32[256,6]{0,1:T(8,128)S(1)}, s32[256,6]{0,1:T(8,128)}, u32[]{:S(2)}) copy-start(s32[256,6]{0,1:T(8,128)} %param.9) | copy-start | bytes 18436
  17.2 119.7 %all-to-all-start = ((bf16[256,4,2176]{2,1,0:T(4,128)(2,1)}), bf16[256,4,2176]{2,1,0:T(4,128)(2,1)}, u32[]{:S(2)}, u32[]{:S(2)}) async-start(bf16[256,4,2176]{2,1,0:T(4,128)(2,1)} %reshape.95), calls=%async_computation | async-start | bytes 8912896 | tf_op jit(solution)/shard_map/all_to_all | solution.py:75
  39.2 107.3 %copy-start = (bf16[768,2048]{1,0:T(8,128)(2,1)S(1)}, bf16[768,2048]{1,0:T(8,128)(2,1)}, u32[]{:S(2)}) copy-start(bf16[768,2048]{1,0:T(8,128)(2,1)} %bitcast_select_fusion) | copy-start | bytes 9437188
  152.2 1.9 copy-start.1
  167.4 110.9 %all-to-all-start.1 = ((bf16[256,4,2176]{2,1,0:T(4,128)(2,1)}), bf16[256,4,2176]{2,1,0:T(4,128)(2,1)}, u32[]{:S(2)}, u32[]{:S(2)}) async-start(bf16[256,4,2176]{2,1,0:T(4,128)(2,1)} %reshape.98), calls=%async_computation.1 | async-start | bytes 8912896 | tf_op jit(solution)/shard_map/all_to_all | solution.py:118
where the time goes:
time: 294 us; the launch traced here: 293 us
  waiting for transfers between devices  188 us (64%)
  local copies, waits for them, and re-layouts  35.8 us (12%)
  matrix products  28.3 us (10%)
  starting transfers between devices  24.2 us (8%)
  other arithmetic  15.4 us (5%)
    all_to_all x1, waiting for transfers between devices, shards(): lax.all_to_all(send.reshape(devices, CAP, width), AXES, split_axis=0, con...  97.7 us
    all_to_all x1, waiting for transfers between devices, shards(): lax.all_to_all(back.reshape(devices, CAP, width), AXES, split_axis=0, con...  90.5 us
    all_to_all x1, starting transfers between devices, shards(): lax.all_to_all(send.reshape(devices, CAP, width), AXES, split_axis=0, con...  16.5 us
    dot_general x1, matrix products, shards(): lax.dot_general(expanded, token_rows, (((0,), (0,)), ((), ())), preferred...  8.23 us
    all_to_all x1, starting transfers between devices, shards(): lax.all_to_all(back.reshape(devices, CAP, width), AXES, split_axis=0, con...  7.7 us
    reshape x1, local copies, waits for them, and re-layouts, shards(): back.reshape(devices, CAP, width)  7.07 us
    reshape x1, local copies, waits for them, and re-layouts, shards(): send.reshape(devices, CAP, width)  7.05 us
    reshape x1, local copies, waits for them, and re-layouts, shards(): received = lax.all_to_all(send.reshape(devices, CAP, width), AXES, split_...  7.05 us
  transfers between devices with their start and end apart: 2, of which 2 were waited for; matrix products, arithmetic and copies ran while one was open for 6% of the time, Pallas kernels for 0%

commit v1 on v0

--- a/solution.py
+++ b/solution.py
@@ -10,6 +10,7 @@
 CAP = 4
 EXTRA = 128
 LABEL_SPLIT = 128
+SPLIT = 1024
 
 SMOOTH = 0.1
 AXES = ("vocab", "fsdp")
@@ -70,17 +71,23 @@
         ),
     )
     packed = jnp.concatenate([hidden, extras], axis=1)
-    send = jnp.dot(place_hot, packed, preferred_element_type=jnp.float32).astype(jnp.bfloat16)
+    bounds = [(0, SPLIT), (SPLIT, width)]
 
-    received = lax.all_to_all(
-        send.reshape(devices, CAP, width), AXES, split_axis=0, concat_axis=0, tiled=True
-    ).reshape(places, width)
+    def exchange(values):
+        return lax.all_to_all(
+            values.reshape(devices, CAP, values.shape[1]), AXES, split_axis=0, concat_axis=0,
+            tiled=True,
+        ).reshape(places, values.shape[1])
 
-    token_rows = received[:, :features]
-    weights = received[:, features]
+    received = []
+    for lo, hi in bounds:
+        send = jnp.dot(place_hot, packed[:, lo:hi], preferred_element_type=jnp.float32)
+        received.append(exchange(send.astype(jnp.bfloat16)))
+    tail = received[-1]
+    weights = tail[:, features - SPLIT]
     targets = (
-        received[:, features + 1].astype(jnp.int32) * LABEL_SPLIT
-        + received[:, features + 2].astype(jnp.int32)
+        tail[:, features - SPLIT + 1].astype(jnp.int32) * LABEL_SPLIT
+        + tail[:, features - SPLIT + 2].astype(jnp.int32)
     )
 
     self_index = lax.axis_index(AXES)
@@ -88,14 +95,31 @@
     blocks = jnp.sum(owned_mask[:, None] * language_blocks, axis=0)
     slab = head_weight.reshape(SB, BLOCK, features)
     candidates = jnp.take(slab, blocks, axis=0).reshape(LB * BLOCK, features)
+    cand_padded = jnp.concatenate(
+        [candidates, jnp.zeros((LB * BLOCK, EXTRA), jnp.bfloat16)], axis=1
+    )
 
-    logits = lax.dot_general(
-        token_rows, candidates, (((1,), (1,)), ((), ())), preferred_element_type=jnp.float32
-    )
+    logits = None
+    for (lo, hi), part in zip(bounds, received):
+        piece = lax.dot_general(
+            part, cand_padded[:, lo:hi], (((1,), (1,)), ((), ())),
+            preferred_element_type=jnp.float32,
+        )
+        logits = piece if logits is None else logits + piece
     losses, grads = smoothed_loss(logits, targets, weights)
-    row_grads = jnp.dot(grads, candidates, preferred_element_type=jnp.float32).astype(
-        jnp.bfloat16
-    )
+
+    back_cols = lax.broadcasted_iota(jnp.int32, (places, EXTRA), 1)
+    returned = []
+    for lo, hi in bounds:
+        part = jnp.dot(grads, cand_padded[:, lo:hi], preferred_element_type=jnp.float32)
+        part = part.astype(jnp.bfloat16)
+        if hi == width:
+            part = jnp.where(
+                (lax.broadcasted_iota(jnp.int32, part.shape, 1) == features - lo),
+                losses[:, None],
+                part,
+            )
+        returned.append(exchange(part))
 
     block_hot = blocks[None, :] == jnp.arange(SB, dtype=jnp.int32)[:, None]
     listed = jnp.any(block_hot, axis=1)
@@ -108,22 +132,21 @@
         jnp.take(grads_by_block, list_index, axis=1),
         jnp.zeros((), jnp.bfloat16),
     ).reshape(places, SB * BLOCK)
+    token_rows = jnp.concatenate([received[0], received[1][:, : features - SPLIT]], axis=1)
     head_grad = lax.dot_general(
         expanded, token_rows, (((0,), (0,)), ((), ())), preferred_element_type=jnp.float32
     ).astype(jnp.bfloat16)
 
-    back_cols = lax.broadcasted_iota(jnp.int32, (places, EXTRA), 1)
-    back_extras = jnp.where(back_cols == 0, losses[:, None], jnp.zeros((), jnp.bfloat16))
-    back = jnp.concatenate([row_grads, back_extras], axis=1)
-    returned = lax.all_to_all(
-        back.reshape(devices, CAP, width), AXES, split_axis=0, concat_axis=0, tiled=True
-    ).reshape(places, width)
-
-    gathered = lax.dot_general(
-        place_hot, returned, (((0,), (0,)), ((), ())), preferred_element_type=jnp.float32
-    )
-    hidden_grad = gathered[:, :features].astype(jnp.bfloat16)
-    token_loss = gathered[:, features].astype(jnp.bfloat16)
+    gathered = [
+        lax.dot_general(
+            place_hot, part, (((0,), (0,)), ((), ())), preferred_element_type=jnp.float32
+        )
+        for part in returned
+    ]
+    hidden_grad = jnp.concatenate(
+        [gathered[0], gathered[1][:, : features - SPLIT]], axis=1
+    ).astype(jnp.bfloat16)
+    token_loss = gathered[1][:, features - SPLIT].astype(jnp.bfloat16)
     return (hidden_grad, token_loss, head_grad)
 
 

time: 294 us -> 298 us (1.014)
  starting transfers between devices: 24.2 us -> 37.7 us
  waiting for transfers between devices: 188 us -> 178 us
  other arithmetic: 15.4 us -> 9.76 us
  local copies, waits for them, and re-layouts: 35.8 us -> 40.6 us
    all_to_all x2 -> x4, starting transfers between devices: 24.2 us -> 37.7 us  [exchange(): lax.all_to_all(values.reshape(devices, CAP, values.shape[1]), AXES, split...]
    all_to_all x2 -> x4, waiting for transfers between devices: 188 us -> 178 us  [exchange(): lax.all_to_all(values.reshape(devices, CAP, values.shape[1]), AXES, split...]
    dot_general x4 -> x8, matrix products: 20.1 us -> 24.1 us  [the longest x2 8.77 us: shards(): jnp.dot(grads, cand_padded[:, lo:hi], preferred_element_type=jnp.float32)]
    reshape x4 -> x8, local copies, waits for them, and re-layouts: 28.2 us -> 30.8 us  [the longest x4 16.6 us: exchange(): values.reshape(devices, CAP, values.shape[1])]
  transfers between devices with their start and end apart: 2 -> 4, of which waited for: 2 -> 4; matrix products, arithmetic and copies ran while one was open for 6% -> 14% of each run, Pallas kernels for 0% -> 0%
where the time goes in v1:
time: 298 us; the launch traced here: 297 us
  waiting for transfers between devices  178 us (60%)
  local copies, waits for them, and re-layouts  40.6 us (14%)
  starting transfers between devices  37.7 us (13%)
  matrix products  30.3 us (10%)
  other arithmetic  9.76 us (3%)
    all_to_all x4, waiting for transfers between devices, exchange(): lax.all_to_all(values.reshape(devices, CAP, values.shape[1]), AXES, split...  178 us
    all_to_all x4, starting transfers between devices, exchange(): lax.all_to_all(values.reshape(devices, CAP, values.shape[1]), AXES, split...  37.7 us
    reshape x4, local copies, waits for them, and re-layouts, exchange(): values.reshape(devices, CAP, values.shape[1])  16.6 us
    reshape x4, local copies, waits for them, and re-layouts, exchange(): return lax.all_to_all(values.reshape(devices, CAP, values.shape[1]), AXES...  14.2 us
    dot_general x2, matrix products, shards(): jnp.dot(grads, cand_padded[:, lo:hi], preferred_element_type=jnp.float32)  8.77 us
    dot_general x2, matrix products, shards(): jnp.dot(place_hot, packed[:, lo:hi], preferred_element_type=jnp.float32)  6.71 us
    dot_general x1, matrix products, shards(): lax.dot_general(expanded, token_rows, (((0,), (0,)), ((), ())), preferred...  6.17 us
  transfers between devices with their start and end apart: 4, of which 4 were waited for; matrix products, arithmetic and copies ran while one was open for 14% of the time, Pallas kernels for 0%

profile of v1, /device:TPU:1, one launch (start us, length us, event | category | flops | bytes accessed | tf_op | source)
XLA Modules:
  0.0 297.4 jit_solution(2978154190079244162)
XLA Ops:
  2.6 2.5 fusion.12
  5.1 2.2 reshape.109
  7.3 15.7 %all-to-all-start.1 = ((bf16[256,4,1024]{2,1,0:T(4,128)(2,1)}), bf16[256,4,1024]{2,1,0:T(4,128)(2,1)S(1)}, u32[]{:S(2)}, u32[]{:S(2)}) async-start(bf16[256,4,1024]{2,1,0:T(4,128)(2,1)} %reshape.109), calls=%async_computation.1 | async-start | bytes 4194304 | tf_op jit(solution)/shard_map/all_to_all | solution.py:77
  23.3 4.2 %convolution_convert_fusion = bf16[1024,1152]{1,0:T(8,128)(2,1)} fusion(bf16[512,128]{1,0:T(8,128)(2,1)S(1)} %select_select_fusion, bf16[512,2048]{1,0:T(8,128)(2,1)} %param.7, s32[512]{0:T(512)S(1)} %multiply_add_fusion), kind=kOutput, calls=%fused_computation.7 | convolution fusion | flops 1212022784 | bytes 4589568 | tf_op jit(solution)/shard_map/dot_general | solution.py:84
  27.5 5.1 %reshape.107 = bf16[256,4,1152]{2,1,0:T(4,128)(2,1)} reshape(bf16[1024,1152]{1,0:T(8,128)(2,1)} %convolution_convert_fusion) | data formatting | bytes 4718592 | tf_op jit(solution)/shard_map/reshape | solution.py:78
  32.6 43.7 %all-to-all-done.1 = bf16[256,4,1024]{2,1,0:T(4,128)(2,1)S(1)} async-done(((bf16[256,4,1024]{2,1,0:T(4,128)(2,1)}), bf16[256,4,1024]{2,1,0:T(4,128)(2,1)S(1)}, u32[]{:S(2)}, u32[]{:S(2)}) %all-to-all-start.1) | async-done | bytes 2097184 | tf_op jit(solution)/shard_map/all_to_all | solution.py:77
  77.7 7.3 %all-to-all-start = ((bf16[256,4,1152]{2,1,0:T(4,128)(2,1)}), bf16[256,4,1152]{2,1,0:T(4,128)(2,1)}, u32[]{:S(2)}, u32[]{:S(2)}) async-start(bf16[256,4,1152]{2,1,0:T(4,128)(2,1)} %reshape.107), calls=%async_computation | async-start | bytes 4718592 | tf_op jit(solution)/shard_map/all_to_all | solution.py:77
  85.1 2.9 gather_fusion
  88.2 2.2 bitcast_select_fusion
  90.4 4.0 %reshape.110 = bf16[1024,1024]{1,0:T(8,128)(2,1)} reshape(bf16[256,4,1024]{2,1,0:T(4,128)(2,1)} %copy-done.2) | data formatting | bytes 4194304 | tf_op jit(solution)/shard_map/reshape | solution.py:80
  94.4 48.9 %all-to-all-done = bf16[256,4,1152]{2,1,0:T(4,128)(2,1)} async-done(((bf16[256,4,1152]{2,1,0:T(4,128)(2,1)}), bf16[256,4,1152]{2,1,0:T(4,128)(2,1)}, u32[]{:S(2)}, u32[]{:S(2)}) %all-to-all-start) | async-done | bytes 2359328 | tf_op jit(solution)/shard_map/all_to_all | solution.py:77
  143.2 3.9 %reshape.108 = bf16[1024,1152]{1,0:T(8,128)(2,1)S(1)} reshape(bf16[256,4,1152]{2,1,0:T(4,128)(2,1)} %all-to-all-done) | data formatting | bytes 4718592 | tf_op jit(solution)/shard_map/reshape | solution.py:80
  147.7 3.9 %fusion.17 = f32[1024,768]{0,1:T(8,128)S(1)} fusion(bf16[1024,1152]{1,0:T(8,128)(2,1)S(1)} %reshape.108, bf16[768,2048]{1,0:T(8,128)(2,1)} %bitcast_select_fusion), kind=kOutput, calls=%fused_computation.33 | convolution fusion | flops 1811939328 | bytes 8650752 | tf_op jit(solution)/shard_map/dot_general | solution.py:104
  156.6 3.2 %convolution_convert_fusion.3 = bf16[1024,1024]{1,0:T(8,128)(2,1)} fusion(bf16[1024,768]{0,1:T(8,128)(2,1)S(1)} %get-tuple-element.5, bf16[768,2048]{1,0:T(8,128)(2,1)S(1)} %copy-done.3), kind=kOutput, calls=%fused_computation.26 | convolution fusion | flops 1611661312 | bytes 5242880 | tf_op jit(solution)/shard_map/dot_general | solution.py:114
  159.7 4.1 %reshape.112 = bf16[256,4,1024]{2,1,0:T(4,128)(2,1)} reshape(bf16[1024,1024]{1,0:T(8,128)(2,1)} %convolution_convert_fusion.3) | data formatting | bytes 4194304 | tf_op jit(solution)/shard_map/reshape | solution.py:78
  163.9 7.5 %all-to-all-start.2 = ((bf16[256,4,1024]{2,1,0:T(4,128)(2,1)}), bf16[256,4,1024]{2,1,0:T(4,128)(2,1)}, u32[]{:S(2)}, u32[]{:S(2)}) async-start(bf16[256,4,1024]{2,1,0:T(4,128)(2,1)} %reshape.112), calls=%async_computation.2 | async-start | bytes 4194304 | tf_op jit(solution)/shard_map/all_to_all | solution.py:77
  171.4 5.6 %fusion.7 = bf16[1024,1152]{1,0:T(8,128)(2,1)} fusion(bf16[1024,768]{0,1:T(8,128)(2,1)} %copy-done.1, pred[1152]{0:T(1024)(128)(4,1)S(1)} %iota_compare_fusion.12, bf16[1024]{0:T(1024)(128)(2,1)S(1)} %subtract_convert_fusion, bf16[768,2048]{1,0:T(8,128)(2,1)} %bitcast_select_fusion), kind=kOutput, calls=%fused_computation.10 | convolution fusion | flops 1814298624 | bytes 7081088 | tf_op jit(solution)/shard_map/dot_general | solution.py:114
  177.0 5.1 %reshape.114 = bf16[256,4,1152]{2,1,0:T(4,128)(2,1)} reshape(bf16[1024,1152]{1,0:T(8,128)(2,1)} %fusion.7) | data formatting | bytes 4718592 | tf_op jit(solution)/shard_map/reshape | solution.py:78
  182.1 41.9 %all-to-all-done.2 = bf16[256,4,1024]{2,1,0:T(4,128)(2,1)} async-done(((bf16[256,4,1024]{2,1,0:T(4,128)(2,1)}), bf16[256,4,1024]{2,1,0:T(4,128)(2,1)}, u32[]{:S(2)}, u32[]{:S(2)}) %all-to-all-start.2) | async-done | bytes 2097184 | tf_op jit(solution)/shard_map/all_to_all | solution.py:77
  224.0 7.3 %all-to-all-start.3 = ((bf16[256,4,1152]{2,1,0:T(4,128)(2,1)}), bf16[256,4,1152]{2,1,0:T(4,128)(2,1)}, u32[]{:S(2)}, u32[]{:S(2)}) async-start(bf16[256,4,1152]{2,1,0:T(4,128)(2,1)} %reshape.114), calls=%async_computation.3 | async-start | bytes 4718592 | tf_op jit(solution)/shard_map/all_to_all | solution.py:77
  236.0 6.2 %fusion.4 = bf16[1024,2048]{1,0:T(8,128)(2,1)} fusion(bf16[1024,1024]{0,1:T(8,128)(2,1)S(1)} %fusion.9, bf16[1024,1024]{1,0:T(8,128)(2,1)S(1)} %slice-done, bf16[1024,1024]{1,0:T(8,128)(2,1)S(1)} %copy-done.5), kind=kOutput, calls=%fused_computation.6 | convolution fusion | flops 4305453056 | bytes 10485760 | tf_op jit(solution)/shard_map/dot_general | solution.py:136
  242.1 2.5 reshape.113
  246.0 43.6 %all-to-all-done.3 = bf16[256,4,1152]{2,1,0:T(4,128)(2,1)} async-done(((bf16[256,4,1152]{2,1,0:T(4,128)(2,1)}), bf16[256,4,1152]{2,1,0:T(4,128)(2,1)}, u32[]{:S(2)}, u32[]{:S(2)}) %all-to-all-start.3) | async-done | bytes 2359328 | tf_op jit(solution)/shard_map/all_to_all | solution.py:77
  289.6 3.9 %reshape.115 = bf16[1024,1152]{1,0:T(8,128)(2,1)S(1)} reshape(bf16[256,4,1152]{2,1,0:T(4,128)(2,1)} %all-to-all-done.3) | data formatting | bytes 4718592 | tf_op jit(solution)/shard_map/reshape | solution.py:80
  (56 shorter events, 19.1 us)
Async XLA Ops:
  7.3 15.7 %copy-start.8 = (s32[512]{0:T(512)S(1)}, s32[512]{0:T(512)}, u32[]{:S(2)}) copy-start(s32[512]{0:T(512)} %param.12) | copy-start | bytes 6148
  7.3 15.7 %copy-start.9 = (bf16[512]{0:T(512)(128)(2,1)S(1)}, bf16[512]{0:T(512)(128)(2,1)}, u32[]{:S(2)}) copy-start(bf16[512]{0:T(512)(128)(2,1)} %param.13) | copy-start | bytes 3076
  7.3 69.1 %all-to-all-start.1 = ((bf16[256,4,1024]{2,1,0:T(4,128)(2,1)}), bf16[256,4,1024]{2,1,0:T(4,128)(2,1)S(1)}, u32[]{:S(2)}, u32[]{:S(2)}) async-start(bf16[256,4,1024]{2,1,0:T(4,128)(2,1)} %reshape.109), calls=%async_computation.1 | async-start | bytes 4194304 | tf_op jit(solution)/shard_map/all_to_all | solution.py:77
  32.6 52.3 %copy-start.7 = (s32[256]{0:T(256)S(1)}, s32[256]{0:T(256)}, u32[]{:S(2)}) copy-start(s32[256]{0:T(256)} %param.10) | copy-start | bytes 3076
  32.6 52.3 %copy-start.6 = (s32[256,6]{0,1:T(8,128)S(1)}, s32[256,6]{0,1:T(8,128)}, u32[]{:S(2)}) copy-start(s32[256,6]{0,1:T(8,128)} %param.9) | copy-start | bytes 18436
  76.3 1.3 copy-start.2
  77.7 65.6 %all-to-all-start = ((bf16[256,4,1152]{2,1,0:T(4,128)(2,1)}), bf16[256,4,1152]{2,1,0:T(4,128)(2,1)}, u32[]{:S(2)}, u32[]{:S(2)}) async-start(bf16[256,4,1152]{2,1,0:T(4,128)(2,1)} %reshape.107), calls=%async_computation | async-start | bytes 4718592 | tf_op jit(solution)/shard_map/all_to_all | solution.py:77
  147.1 84.5 %copy-start = (bf16[1024,1152]{1,0:T(8,128)(2,1)}, bf16[1024,1152]{1,0:T(8,128)(2,1)S(1)}, u32[]{:S(2)}) copy-start(bf16[1024,1152]{1,0:T(8,128)(2,1)S(1)} %reshape.108) | copy-start | bytes 7077892
  147.7 3.9 %copy-start.3 = (bf16[768,2048]{1,0:T(8,128)(2,1)S(1)}, bf16[768,2048]{1,0:T(8,128)(2,1)}, u32[]{:S(2)}) copy-start(bf16[768,2048]{1,0:T(8,128)(2,1)} %bitcast_select_fusion) | copy-start | bytes 9437188
  147.7 3.9 %copy-start.4 = (bf16[1024,1024]{1,0:T(8,128)(2,1)S(1)}, bf16[1024,1024]{1,0:T(8,128)(2,1)}, u32[]{:S(2)}) copy-start(bf16[1024,1024]{1,0:T(8,128)(2,1)} %reshape.110) | copy-start | bytes 6291460
  155.4 1.2 copy-start.1
  163.9 60.1 %all-to-all-start.2 = ((bf16[256,4,1024]{2,1,0:T(4,128)(2,1)}), bf16[256,4,1024]{2,1,0:T(4,128)(2,1)}, u32[]{:S(2)}, u32[]{:S(2)}) async-start(bf16[256,4,1024]{2,1,0:T(4,128)(2,1)} %reshape.112), calls=%async_computation.2 | async-start | bytes 4194304 | tf_op jit(solution)/shard_map/all_to_all | solution.py:77
  224.0 65.6 %all-to-all-start.3 = ((bf16[256,4,1152]{2,1,0:T(4,128)(2,1)}), bf16[256,4,1152]{2,1,0:T(4,128)(2,1)}, u32[]{:S(2)}, u32[]{:S(2)}) async-start(bf16[256,4,1152]{2,1,0:T(4,128)(2,1)} %reshape.114), calls=%async_computation.3 | async-start | bytes 4718592 | tf_op jit(solution)/shard_map/all_to_all | solution.py:77
  233.7 1.6 slice-start
  233.7 2.2 copy-start.5

commit v2 on v0

--- a/solution.py
+++ b/solution.py
@@ -1,6 +1,7 @@
 import jax
 import jax.numpy as jnp
 from jax import lax
+from jax.experimental import pallas as pl
 from jax.sharding import PartitionSpec as P
 
 D = 2048
@@ -13,6 +14,42 @@
 
 SMOOTH = 0.1
 AXES = ("vocab", "fsdp")
+GROUPS_PER_STEP = 64
+
+
+def _split_rows(x_ref, o_ref):
+    x = x_ref[...]
+    o_ref[...] = x.reshape(o_ref.shape)
+
+
+def _join_rows(x_ref, o_ref):
+    x = x_ref[...]
+    o_ref[...] = x.reshape(o_ref.shape)
+
+
+def to_groups(x):
+    rows, width = x.shape
+    groups = rows // CAP
+    step = min(GROUPS_PER_STEP, groups)
+    return pl.pallas_call(
+        _split_rows,
+        grid=(groups // step,),
+        in_specs=[pl.BlockSpec((step * CAP, width), lambda i: (i, 0))],
+        out_specs=pl.BlockSpec((step, CAP, width), lambda i: (i, 0, 0)),
+        out_shape=jax.ShapeDtypeStruct((groups, CAP, width), x.dtype),
+    )(x)
+
+
+def from_groups(x):
+    groups, cap, width = x.shape
+    step = min(GROUPS_PER_STEP, groups)
+    return pl.pallas_call(
+        _join_rows,
+        grid=(groups // step,),
+        in_specs=[pl.BlockSpec((step, cap, width), lambda i: (i, 0, 0))],
+        out_specs=pl.BlockSpec((step * cap, width), lambda i: (i, 0)),
+        out_shape=jax.ShapeDtypeStruct((groups * cap, width), x.dtype),
+    )(x)
 
 
 def smoothed_loss(logits, targets, weights):
@@ -72,9 +109,9 @@
     packed = jnp.concatenate([hidden, extras], axis=1)
     send = jnp.dot(place_hot, packed, preferred_element_type=jnp.float32).astype(jnp.bfloat16)
 
-    received = lax.all_to_all(
-        send.reshape(devices, CAP, width), AXES, split_axis=0, concat_axis=0, tiled=True
-    ).reshape(places, width)
+    received = from_groups(
+        lax.all_to_all(to_groups(send), AXES, split_axis=0, concat_axis=0, tiled=True)
+    )
 
     token_rows = received[:, :features]
     weights = received[:, features]
@@ -93,8 +130,14 @@
         token_rows, candidates, (((1,), (1,)), ((), ())), preferred_element_type=jnp.float32
     )
     losses, grads = smoothed_loss(logits, targets, weights)
-    row_grads = jnp.dot(grads, candidates, preferred_element_type=jnp.float32).astype(
+    cand_padded = jnp.concatenate(
+        [candidates, jnp.zeros((LB * BLOCK, EXTRA), jnp.bfloat16)], axis=1
+    )
+    row_grads = jnp.dot(grads, cand_padded, preferred_element_type=jnp.float32).astype(
         jnp.bfloat16
+    )
+    back = jnp.where(
+        lax.broadcasted_iota(jnp.int32, row_grads.shape, 1) == features, losses[:, None], row_grads
     )
 
     block_hot = blocks[None, :] == jnp.arange(SB, dtype=jnp.int32)[:, None]
@@ -112,18 +155,18 @@
         expanded, token_rows, (((0,), (0,)), ((), ())), preferred_element_type=jnp.float32
     ).astype(jnp.bfloat16)
 
-    back_cols = lax.broadcasted_iota(jnp.int32, (places, EXTRA), 1)
-    back_extras = jnp.where(back_cols == 0, losses[:, None], jnp.zeros((), jnp.bfloat16))
-    back = jnp.concatenate([row_grads, back_extras], axis=1)
-    returned = lax.all_to_all(
-        back.reshape(devices, CAP, width), AXES, split_axis=0, concat_axis=0, tiled=True
-    ).reshape(places, width)
+    returned = from_groups(
+        lax.all_to_all(to_groups(back), AXES, split_axis=0, concat_axis=0, tiled=True)
+    )
 
-    gathered = lax.dot_general(
-        place_hot, returned, (((0,), (0,)), ((), ())), preferred_element_type=jnp.float32
-    )
-    hidden_grad = gathered[:, :features].astype(jnp.bfloat16)
-    token_loss = gathered[:, features].astype(jnp.bfloat16)
+    hidden_grad = lax.dot_general(
+        place_hot, returned[:, :features], (((0,), (0,)), ((), ())),
+        preferred_element_type=jnp.float32,
+    ).astype(jnp.bfloat16)
+    token_loss = lax.dot_general(
+        place_hot, returned[:, features:], (((0,), (0,)), ((), ())),
+        preferred_element_type=jnp.float32,
+    )[:, 0].astype(jnp.bfloat16)
     return (hidden_grad, token_loss, head_grad)
 
 

time: 294 us -> 285 us (0.969)
  local copies, waits for them, and re-layouts: 35.8 us -> 6.13 us
  Pallas kernels: 0 us -> 19.9 us
  matrix products: 28.3 us -> 32.5 us
    reshape x4 -> x0, local copies, waits for them, and re-layouts: 28.2 us -> none  [the longest x1 7.07 us: shards(): back.reshape(devices, CAP, width)]
    pallas_call x0 -> x4, Pallas kernels: none -> 19.9 us  [the longest x2 10 us: to_groups(): pl.pallas_call(_split_rows, grid=(groups // step,), in_specs=[pl.BlockSpe...]
    dot_general x2 -> x3, matrix products: 8.85 us -> 13 us  [the longest x1 5.91 us: shards(): lax.dot_general(place_hot, returned[:, :features], (((0,), (0,)), ((), ()...]
where the time goes in v2:
time: 285 us; the launch traced here: 284 us
  waiting for transfers between devices  188 us (66%)
  matrix products  32.5 us (11%)
  starting transfers between devices  24.2 us (8%)
  Pallas kernels  19.9 us (7%)
  other arithmetic  12.7 us (4%)
  local copies, waits for them, and re-layouts  6.13 us (2%)
    all_to_all x1, waiting for transfers between devices, shards(): lax.all_to_all(to_groups(send), AXES, split_axis=0, concat_axis=0, tiled=...  97.7 us
    all_to_all x1, waiting for transfers between devices, shards(): lax.all_to_all(to_groups(back), AXES, split_axis=0, concat_axis=0, tiled=...  90.5 us
    all_to_all x1, starting transfers between devices, shards(): lax.all_to_all(to_groups(send), AXES, split_axis=0, concat_axis=0, tiled=...  16.5 us
    pallas_call x2, Pallas kernels, to_groups(): pl.pallas_call(_split_rows, grid=(groups // step,), in_specs=[pl.BlockSpe...  10 us
    pallas_call x2, Pallas kernels, from_groups(): pl.pallas_call(_join_rows, grid=(groups // step,), in_specs=[pl.BlockSpec...  9.9 us
    dot_general x1, matrix products, shards(): lax.dot_general(expanded, token_rows, (((0,), (0,)), ((), ())), preferred...  8.23 us
    all_to_all x1, starting transfers between devices, shards(): lax.all_to_all(to_groups(back), AXES, split_axis=0, concat_axis=0, tiled=...  7.7 us
    dot_general x1, matrix products, shards(): lax.dot_general(place_hot, returned[:, :features], (((0,), (0,)), ((), ()...  5.91 us
  transfers between devices with their start and end apart: 2, of which 2 were waited for; matrix products, arithmetic and copies ran while one was open for 6% of the time, Pallas kernels for 0%

profile of v2, /device:TPU:1, one launch (start us, length us, event | category | flops | bytes accessed | tf_op | source)
XLA Modules:
  0.0 284.5 jit_solution(12854460723459365233)
XLA Ops:
  1.3 1.0 convert_reduce_fusion
  2.4 0.9 select_reduce_fusion.1
  3.3 0.9 select_select_fusion
  4.3 5.9 %convolution_convert_fusion.1.x_ref = bf16[1024,2176]{1,0:T(8,128)(2,1)} fusion(bf16[512,128]{1,0:T(8,128)(2,1)S(1)} %select_select_fusion, bf16[512,2048]{1,0:T(8,128)(2,1)} %param.7, s32[512]{0:T(512)S(1)} %multiply_add_fusion), kind=kOutput, calls=%fused_computation.3 | convolution fusion | flops 2288910336 | bytes 6686720 | tf_op jit(solution)/shard_map/dot_general | solution.py:110
  10.2 5.0 %shard_map.94 = bf16[256,4,2176]{2,1,0:T(4,128)(2,1)} custom-call(bf16[1024,2176]{1,0:T(8,128)(2,1)} %convolution_convert_fusion.1.x_ref), custom_call_target="tpu_custom_call" | custom-call | tf_op jit(solution)/shard_map/pallas_call | solution.py:34
  15.1 16.5 %all-to-all-start = ((bf16[256,4,2176]{2,1,0:T(4,128)(2,1)}), bf16[256,4,2176]{2,1,0:T(4,128)(2,1)}, u32[]{:S(2)}, u32[]{:S(2)}) async-start(bf16[256,4,2176]{2,1,0:T(4,128)(2,1)} %shard_map.94), calls=%async_computation | async-start | bytes 8912896 | tf_op jit(solution)/shard_map/all_to_all | solution.py:113
  31.8 2.9 %gather_fusion = bf16[6,128,2048]{2,1,0:T(8,128)(2,1)S(1)} fusion(bf16[8,128,2048]{2,1,0:T(8,128)(2,1)} %bitcast.29, s32[1024]{0:T(1024)S(1)} %pad_clamp_fusion.1), kind=kCustom, calls=%fused_computation | custom fusion | bytes 6291480 | tf_op jit(solution)/shard_map/jit(_take)/gather | solution.py:127
  34.9 2.2 bitcast_select_fusion
  37.1 97.7 %all-to-all-done.x_ref = bf16[256,4,2176]{2,1,0:T(4,128)(2,1)} async-done(((bf16[256,4,2176]{2,1,0:T(4,128)(2,1)}), bf16[256,4,2176]{2,1,0:T(4,128)(2,1)}, u32[]{:S(2)}, u32[]{:S(2)}) %all-to-all-start) | async-done | bytes 4456480 | tf_op jit(solution)/shard_map/all_to_all | solution.py:113
  134.8 5.0 %shard_map.95 = bf16[1024,2176]{1,0:T(8,128)(2,1)} custom-call(bf16[256,4,2176]{2,1,0:T(4,128)(2,1)} %all-to-all-done.x_ref), custom_call_target="tpu_custom_call" | custom-call | tf_op jit(solution)/shard_map/pallas_call | solution.py:46
  139.7 1.4 add_reduce_fusion
  141.2 1.1 convert_reduce_fusion.1
  142.3 5.3 %fusion.30 = (f32[1024]{0:T(1024)S(1)}, f32[1024,768]{0,1:T(8,128)S(1)}) fusion(bf16[768,2048]{1,0:T(8,128)(2,1)S(1)} %copy-done, bf16[1024,2176]{1,0:T(8,128)(2,1)} %shard_map.95), kind=kOutput, calls=%fused_computation.77 | convolution fusion | flops 3222010880 | bytes 10489856 | tf_op jit(solution)/shard_map/dot_general | solution.py:129
  148.1 1.4 select_reduce_fusion
  149.9 5.7 %fusion.x_ref = bf16[1024,2176]{1,0:T(8,128)(2,1)} fusion(bf16[1024,768]{0,1:T(8,128)(2,1)S(1)} %get-tuple-element.5, pred[2176]{0:T(1024)(128)(4,1)S(1)} %iota_compare_fusion.7, bf16[768,2048]{1,0:T(8,128)(2,1)S(1)} %copy-done.1, bf16[1024]{0:T(1024)(128)(2,1)S(1)} %subtract_convert_fusion), kind=kOutput, calls=%fused_computation.4 | convolution fusion | flops 3427008512 | bytes 9179264 | tf_op jit(solution)/shard_map/dot_general | solution.py:136
  155.6 5.0 %shard_map.96 = bf16[256,4,2176]{2,1,0:T(4,128)(2,1)} custom-call(bf16[1024,2176]{1,0:T(8,128)(2,1)} %fusion.x_ref), custom_call_target="tpu_custom_call" | custom-call | tf_op jit(solution)/shard_map/pallas_call | solution.py:34
  160.6 7.7 %all-to-all-start.1 = ((bf16[256,4,2176]{2,1,0:T(4,128)(2,1)}), bf16[256,4,2176]{2,1,0:T(4,128)(2,1)}, u32[]{:S(2)}, u32[]{:S(2)}) async-start(bf16[256,4,2176]{2,1,0:T(4,128)(2,1)} %shard_map.96), calls=%async_computation.1 | async-start | bytes 8912896 | tf_op jit(solution)/shard_map/all_to_all | solution.py:159
  168.7 2.0 gather_fusion.1
  170.7 2.1 fusion.14
  172.8 8.2 %convolution_convert_fusion.2 = bf16[1024,2048]{1,0:T(8,128)(2,1)} fusion(bf16[1024,1024]{0,1:T(8,128)(2,1)S(1)} %fusion.14, bf16[1024,2176]{1,0:T(8,128)(2,1)} %shard_map.95), kind=kOutput, calls=%fused_computation.7 | convolution fusion | flops 4297064448 | bytes 10485760 | tf_op jit(solution)/shard_map/dot_general | solution.py:154
  181.0 90.5 %all-to-all-done.1.x_ref = bf16[256,4,2176]{2,1,0:T(4,128)(2,1)} async-done(((bf16[256,4,2176]{2,1,0:T(4,128)(2,1)}), bf16[256,4,2176]{2,1,0:T(4,128)(2,1)}, u32[]{:S(2)}, u32[]{:S(2)}) %all-to-all-start.1) | async-done | bytes 4456480 | tf_op jit(solution)/shard_map/all_to_all | solution.py:159
  271.6 5.0 %shard_map.97 = bf16[1024,2176]{1,0:T(8,128)(2,1)} custom-call(bf16[256,4,2176]{2,1,0:T(4,128)(2,1)} %all-to-all-done.1.x_ref), custom_call_target="tpu_custom_call" | custom-call | tf_op jit(solution)/shard_map/pallas_call | solution.py:46
  276.5 5.9 %fusion.7 = bf16[512,2048]{1,0:T(8,128)(2,1)} fusion(bf16[1024,2176]{1,0:T(8,128)(2,1)} %shard_map.97, s32[512]{0:T(512)S(1)} %multiply_add_fusion), kind=kOutput, calls=%fused_computation.17 | convolution fusion | flops 2149056512 | bytes 6293504 | tf_op jit(solution)/shard_map/dot_general | solution.py:162
  282.4 1.5 fusion.15
  (29 shorter events, 2.8 us)
Async XLA Ops:
  15.1 16.6 %copy-start.3 = (s32[256]{0:T(256)S(1)}, s32[256]{0:T(256)}, u32[]{:S(2)}) copy-start(s32[256]{0:T(256)} %param.10) | copy-start | bytes 3076
  15.1 16.6 %copy-start.2 = (s32[256,6]{0,1:T(8,128)S(1)}, s32[256,6]{0,1:T(8,128)}, u32[]{:S(2)}) copy-start(s32[256,6]{0,1:T(8,128)} %param.9) | copy-start | bytes 18436
  15.1 119.7 %all-to-all-start = ((bf16[256,4,2176]{2,1,0:T(4,128)(2,1)}), bf16[256,4,2176]{2,1,0:T(4,128)(2,1)}, u32[]{:S(2)}, u32[]{:S(2)}) async-start(bf16[256,4,2176]{2,1,0:T(4,128)(2,1)} %shard_map.94), calls=%async_computation | async-start | bytes 8912896 | tf_op jit(solution)/shard_map/all_to_all | solution.py:113
  37.1 105.2 %copy-start = (bf16[768,2048]{1,0:T(8,128)(2,1)S(1)}, bf16[768,2048]{1,0:T(8,128)(2,1)}, u32[]{:S(2)}) copy-start(bf16[768,2048]{1,0:T(8,128)(2,1)} %bitcast_select_fusion) | copy-start | bytes 9437188
  148.0 1.9 copy-start.1
  160.6 110.9 %all-to-all-start.1 = ((bf16[256,4,2176]{2,1,0:T(4,128)(2,1)}), bf16[256,4,2176]{2,1,0:T(4,128)(2,1)}, u32[]{:S(2)}, u32[]{:S(2)}) async-start(bf16[256,4,2176]{2,1,0:T(4,128)(2,1)} %shard_map.96), calls=%async_computation.1 | async-start | bytes 8912896 | tf_op jit(solution)/shard_map/all_to_all | solution.py:159

commit v3 on v2

--- a/solution.py
+++ b/solution.py
@@ -15,6 +15,17 @@
 SMOOTH = 0.1
 AXES = ("vocab", "fsdp")
 GROUPS_PER_STEP = 64
+
+
+def place_tokens(token_language, language_owner):
+    language = token_language[:, 0]
+    languages = language_owner.shape[0]
+    matches = language[:, None] == jnp.arange(languages, dtype=jnp.int32)[None, :]
+    slot_ids = jnp.sum(jnp.where(matches, language_owner[None, :], 0), axis=1)
+    positions = jnp.arange(language.shape[0], dtype=jnp.int32)
+    earlier = (language[:, None] == language[None, :]) & (positions[None, :] < positions[:, None])
+    rank_in_group = jnp.sum(earlier.astype(jnp.int32), axis=1)
+    return slot_ids * CAP + rank_in_group
 
 
 def _split_rows(x_ref, o_ref):
@@ -52,32 +63,64 @@
     )(x)
 
 
-def smoothed_loss(logits, targets, weights):
-    columns = logits.shape[1]
+def _middle(r_ref, cand_ref, back_ref, rows_ref, grads_ref):
+    x = r_ref[...]
+    x = x.reshape(x.shape[0] * x.shape[1], x.shape[2])
+    rows_ref[...] = x
+    n, width = x.shape
+    cand = cand_ref[...]
+    columns, features = cand.shape
+    logits = lax.dot_general(
+        x[:, :features], cand, (((1,), (1,)), ((), ())), preferred_element_type=jnp.float32
+    )
+    weights = x[:, features : features + 1].astype(jnp.float32)
+    targets = (
+        x[:, features + 1 : features + 2].astype(jnp.float32) * LABEL_SPLIT
+        + x[:, features + 2 : features + 3].astype(jnp.float32)
+    ).astype(jnp.int32)
     row_max = jnp.max(logits, axis=1, keepdims=True)
     shifted = logits - row_max
     log_probs = shifted - jnp.log(jnp.sum(jnp.exp(shifted), axis=1, keepdims=True))
-    onehot = (lax.broadcasted_iota(jnp.int32, logits.shape, 1) == targets[:, None]).astype(
-        jnp.float32
-    )
-    losses = -(1.0 - SMOOTH) * jnp.sum(onehot * log_probs, axis=1) - SMOOTH / columns * jnp.sum(
-        log_probs, axis=1
-    )
-    grads = weights.astype(jnp.float32)[:, None] * (
-        jnp.exp(log_probs) - (1.0 - SMOOTH) * onehot - SMOOTH / columns
-    )
-    return (losses.astype(jnp.bfloat16), grads.astype(jnp.bfloat16))
-
-
-def place_tokens(token_language, language_owner):
-    language = token_language[:, 0]
-    languages = language_owner.shape[0]
-    matches = language[:, None] == jnp.arange(languages, dtype=jnp.int32)[None, :]
-    slot_ids = jnp.sum(jnp.where(matches, language_owner[None, :], 0), axis=1)
-    positions = jnp.arange(language.shape[0], dtype=jnp.int32)
-    earlier = (language[:, None] == language[None, :]) & (positions[None, :] < positions[:, None])
-    rank_in_group = jnp.sum(earlier.astype(jnp.int32), axis=1)
-    return slot_ids * CAP + rank_in_group
+    onehot = (lax.broadcasted_iota(jnp.int32, logits.shape, 1) == targets).astype(jnp.float32)
+    losses = -(1.0 - SMOOTH) * jnp.sum(onehot * log_probs, axis=1, keepdims=True) - (
+        SMOOTH / columns
+    ) * jnp.sum(log_probs, axis=1, keepdims=True)
+    grads = (
+        weights * (jnp.exp(log_probs) - (1.0 - SMOOTH) * onehot - SMOOTH / columns)
+    ).astype(jnp.bfloat16)
+    grads_ref[...] = grads
+    row_grads = jnp.dot(grads, cand, preferred_element_type=jnp.float32).astype(jnp.bfloat16)
+    extras = jnp.where(
+        lax.broadcasted_iota(jnp.int32, (n, width - features), 1) == 0,
+        losses.astype(jnp.bfloat16),
+        jnp.zeros((), jnp.bfloat16),
+    )
+    back = jnp.concatenate([row_grads, extras], axis=1)
+    back_ref[...] = back.reshape(back_ref.shape)
+
+
+def middle(received, candidates):
+    groups, cap, width = received.shape
+    columns, features = candidates.shape
+    step = min(GROUPS_PER_STEP, groups)
+    return pl.pallas_call(
+        _middle,
+        grid=(groups // step,),
+        in_specs=[
+            pl.BlockSpec((step, cap, width), lambda i: (i, 0, 0)),
+            pl.BlockSpec((columns, features), lambda i: (0, 0)),
+        ],
+        out_specs=[
+            pl.BlockSpec((step, cap, width), lambda i: (i, 0, 0)),
+            pl.BlockSpec((step * cap, width), lambda i: (i, 0)),
+            pl.BlockSpec((step * cap, columns), lambda i: (i, 0)),
+        ],
+        out_shape=[
+            jax.ShapeDtypeStruct((groups, cap, width), received.dtype),
+            jax.ShapeDtypeStruct((groups * cap, width), received.dtype),
+            jax.ShapeDtypeStruct((groups * cap, columns), jnp.bfloat16),
+        ],
+    )(received, candidates)
 
 
 def shards(
@@ -86,7 +129,6 @@
     devices = lax.axis_size(AXES)
     tokens, features = hidden.shape
     places = devices * CAP
-    width = features + EXTRA
     assert head_weight.shape[0] == SB * BLOCK
 
     target_place = place_tokens(token_language, language_owner)
@@ -109,16 +151,7 @@
     packed = jnp.concatenate([hidden, extras], axis=1)
     send = jnp.dot(place_hot, packed, preferred_element_type=jnp.float32).astype(jnp.bfloat16)
 
-    received = from_groups(
-        lax.all_to_all(to_groups(send), AXES, split_axis=0, concat_axis=0, tiled=True)
-    )
-
-    token_rows = received[:, :features]
-    weights = received[:, features]
-    targets = (
-        received[:, features + 1].astype(jnp.int32) * LABEL_SPLIT
-        + received[:, features + 2].astype(jnp.int32)
-    )
+    received = lax.all_to_all(to_groups(send), AXES, split_axis=0, concat_axis=0, tiled=True)
 
     self_index = lax.axis_index(AXES)
     owned_mask = (language_owner == self_index).astype(jnp.int32)
@@ -126,19 +159,8 @@
     slab = head_weight.reshape(SB, BLOCK, features)
     candidates = jnp.take(slab, blocks, axis=0).reshape(LB * BLOCK, features)
 
-    logits = lax.dot_general(
-        token_rows, candidates, (((1,), (1,)), ((), ())), preferred_element_type=jnp.float32
-    )
-    losses, grads = smoothed_loss(logits, targets, weights)
-    cand_padded = jnp.concatenate(
-        [candidates, jnp.zeros((LB * BLOCK, EXTRA), jnp.bfloat16)], axis=1
-    )
-    row_grads = jnp.dot(grads, cand_padded, preferred_element_type=jnp.float32).astype(
-        jnp.bfloat16
-    )
-    back = jnp.where(
-        lax.broadcasted_iota(jnp.int32, row_grads.shape, 1) == features, losses[:, None], row_grads
-    )
+    back, token_rows, grads = middle(received, candidates)
+    returned = from_groups(lax.all_to_all(back, AXES, split_axis=0, concat_axis=0, tiled=True))
 
     block_hot = blocks[None, :] == jnp.arange(SB, dtype=jnp.int32)[:, None]
     listed = jnp.any(block_hot, axis=1)
@@ -152,12 +174,9 @@
         jnp.zeros((), jnp.bfloat16),
     ).reshape(places, SB * BLOCK)
     head_grad = lax.dot_general(
-        expanded, token_rows, (((0,), (0,)), ((), ())), preferred_element_type=jnp.float32
-    ).astype(jnp.bfloat16)
-
-    returned = from_groups(
-        lax.all_to_all(to_groups(back), AXES, split_axis=0, concat_axis=0, tiled=True)
-    )
+        expanded, token_rows[:, :features], (((0,), (0,)), ((), ())),
+        preferred_element_type=jnp.float32,
+    ).astype(jnp.bfloat16)
 
     hidden_grad = lax.dot_general(
         place_hot, returned[:, :features], (((0,), (0,)), ((), ())),

time: 285 us -> 274 us (0.961)
  matrix products: 32.5 us -> 21.4 us
  other arithmetic: 12.7 us -> 7.17 us
  Pallas kernels: 19.9 us -> 24.8 us
  local copies, waits for them, and re-layouts: 6.13 us -> 10.3 us
  waiting for transfers between devices: 188 us -> 185 us
    pallas_call x0 -> x1, Pallas kernels: none -> 14.7 us  [middle(): pl.pallas_call(_middle, grid=(groups // step,), in_specs=[pl.BlockSpec((s...]
    dot_general x3 -> x1, matrix products: 19.2 us -> 8.23 us  [shards(): lax.dot_general(expanded, token_rows[:, :features], (((0,), (0,)), ((), (...]
    pallas_call x2 -> x1, Pallas kernels: 10 us -> 5.03 us  [to_groups(): pl.pallas_call(_split_rows, grid=(groups // step,), in_specs=[pl.BlockSpe...]
    pallas_call x2 -> x1, Pallas kernels: 9.9 us -> 5.02 us  [from_groups(): pl.pallas_call(_join_rows, grid=(groups // step,), in_specs=[pl.BlockSpec...]
    all_to_all x1, waiting for transfers between devices: 90.5 us -> 87 us  [shards(): lax.all_to_all(back, AXES, split_axis=0, concat_axis=0, tiled=True)]
    gather x1 -> x2, local copies, waits for them, and re-layouts: 2 us -> 4.99 us  [shards(): jnp.take(grads_by_block, list_index, axis=1)]
  transfers between devices with their start and end apart: 2 -> 2, of which waited for: 2 -> 2; matrix products, arithmetic and copies ran while one was open for 6% -> 8% of each run, Pallas kernels for 0% -> 0%
where the time goes in v3:
time: 274 us; the launch traced here: 273 us
  waiting for transfers between devices  185 us (68%)
  Pallas kernels  24.8 us (9%)
  starting transfers between devices  24.2 us (9%)
  matrix products  21.4 us (8%)
  local copies, waits for them, and re-layouts  10.3 us (4%)
  other arithmetic  7.17 us (3%)
    all_to_all x1, waiting for transfers between devices, shards(): lax.all_to_all(to_groups(send), AXES, split_axis=0, concat_axis=0, tiled=...  97.7 us
    all_to_all x1, waiting for transfers between devices, shards(): lax.all_to_all(back, AXES, split_axis=0, concat_axis=0, tiled=True)  87 us
    all_to_all x1, starting transfers between devices, shards(): lax.all_to_all(to_groups(send), AXES, split_axis=0, concat_axis=0, tiled=...  16.5 us
    pallas_call x1, Pallas kernels, middle(): pl.pallas_call(_middle, grid=(groups // step,), in_specs=[pl.BlockSpec((s...  14.7 us
    dot_general x1, matrix products, shards(): lax.dot_general(expanded, token_rows[:, :features], (((0,), (0,)), ((), (...  8.23 us
    all_to_all x1, starting transfers between devices, shards(): lax.all_to_all(back, AXES, split_axis=0, concat_axis=0, tiled=True)  7.67 us
    dot_general x1, matrix products, shards(): lax.dot_general(place_hot, returned[:, :features], (((0,), (0,)), ((), ()...  5.91 us
    dot_general x1, matrix products, shards(): jnp.dot(place_hot, packed, preferred_element_type=jnp.float32)  5.84 us
  transfers between devices with their start and end apart: 2, of which 2 were waited for; matrix products, arithmetic and copies ran while one was open for 8% of the time, Pallas kernels for 0%

profile of v3, /device:TPU:1, one launch (start us, length us, event | category | flops | bytes accessed | tf_op | source)
XLA Modules:
  0.0 273.4 jit_solution(4748513520851474875)
XLA Ops:
  0.7 0.7 fusion.21
  1.3 1.0 convert_reduce_fusion
  2.4 0.9 select_reduce_fusion
  3.3 0.9 select_select_fusion
  4.3 5.8 %convolution_convert_fusion.x_ref = bf16[1024,2176]{1,0:T(8,128)(2,1)} fusion(bf16[512,128]{1,0:T(8,128)(2,1)S(1)} %select_select_fusion, bf16[512,2048]{1,0:T(8,128)(2,1)} %param.7, s32[512]{0:T(512)S(1)} %multiply_add_fusion), kind=kOutput, calls=%fused_computation.2 | convolution fusion | flops 2288910336 | bytes 6686720 | tf_op jit(solution)/shard_map/dot_general | solution.py:152
  10.1 5.0 %shard_map.94 = bf16[256,4,2176]{2,1,0:T(4,128)(2,1)} custom-call(bf16[1024,2176]{1,0:T(8,128)(2,1)} %convolution_convert_fusion.x_ref), custom_call_target="tpu_custom_call" | custom-call | tf_op jit(solution)/shard_map/pallas_call | solution.py:45
  15.1 16.5 %all-to-all-start = ((bf16[256,4,2176]{2,1,0:T(4,128)(2,1)}), bf16[256,4,2176]{2,1,0:T(4,128)(2,1)}, u32[]{:S(2)}, u32[]{:S(2)}) async-start(bf16[256,4,2176]{2,1,0:T(4,128)(2,1)} %shard_map.94), calls=%async_computation | async-start | bytes 8912896 | tf_op jit(solution)/shard_map/all_to_all | solution.py:154
  31.8 2.9 %gather_fusion = bf16[6,128,2048]{2,1,0:T(8,128)(2,1)S(1)} fusion(bf16[8,128,2048]{2,1,0:T(8,128)(2,1)} %bitcast.27, s32[1024]{0:T(1024)S(1)} %pad_clamp_fusion.1), kind=kCustom, calls=%fused_computation | custom fusion | bytes 6291480 | tf_op jit(solution)/shard_map/jit(_take)/gather | solution.py:160
  34.9 2.2 bitcast_select_fusion.cand_ref
  37.1 97.7 %all-to-all-done.r_ref = bf16[256,4,2176]{2,1,0:T(4,128)(2,1)} async-done(((bf16[256,4,2176]{2,1,0:T(4,128)(2,1)}), bf16[256,4,2176]{2,1,0:T(4,128)(2,1)}, u32[]{:S(2)}, u32[]{:S(2)}) %all-to-all-start) | async-done | bytes 4456480 | tf_op jit(solution)/shard_map/all_to_all | solution.py:154
  134.8 14.7 %shard_map.95 = (bf16[256,4,2176]{2,1,0:T(4,128)(2,1)}, bf16[1024,2176]{1,0:T(8,128)(2,1)}, bf16[1024,768]{1,0:T(8,128)(2,1)}) custom-call(bf16[256,4,2176]{2,1,0:T(4,128)(2,1)} %all-to-all-done.r_ref, bf16[768,2048]{1,0:T(8,128)(2,1)} %bitcast_select_fusion.cand_ref), custom_call_target="tpu_custom_call" | custom-call | tf_op jit(solution)/shard_map/pallas_call | solution.py:106
  149.5 7.7 %all-to-all-start.1 = ((bf16[256,4,2176]{2,1,0:T(4,128)(2,1)}), bf16[256,4,2176]{2,1,0:T(4,128)(2,1)}, u32[]{:S(2)}, u32[]{:S(2)}) async-start(bf16[256,4,2176]{2,1,0:T(4,128)(2,1)} %get-tuple-element.6), calls=%async_computation.1 | async-start | bytes 8912896 | tf_op jit(solution)/shard_map/all_to_all | solution.py:163
  157.2 0.1 fusion.20
  157.5 0.8 copy.15
  158.3 0.9 copy.16
  159.2 2.1 gather_fusion.1
  161.3 2.9 %copy.17 = bf16[1024,8,128]{0,2,1:T(8,128)(2,1)S(1)} copy(bf16[1024,8,128]{2,0,1:T(8,128)(2,1)} %bitcast.25) | data formatting | bytes 4194304 | tf_op jit(solution)/shard_map/jit(_take)/gather | solution.py:173
  164.2 1.0 fusion.13
  165.2 8.2 %fusion.4 = bf16[1024,2048]{1,0:T(8,128)(2,1)} fusion(bf16[1024,1024]{0,1:T(8,128)(2,1)S(1)} %fusion.13, bf16[1024,2176]{1,0:T(8,128)(2,1)} %get-tuple-element.8), kind=kOutput, calls=%fused_computation.7 | convolution fusion | flops 4297064448 | bytes 10485760 | tf_op jit(solution)/shard_map/dot_general | solution.py:176
  173.4 87.0 %all-to-all-done.1.x_ref = bf16[256,4,2176]{2,1,0:T(4,128)(2,1)} async-done(((bf16[256,4,2176]{2,1,0:T(4,128)(2,1)}), bf16[256,4,2176]{2,1,0:T(4,128)(2,1)}, u32[]{:S(2)}, u32[]{:S(2)}) %all-to-all-start.1) | async-done | bytes 4456480 | tf_op jit(solution)/shard_map/all_to_all | solution.py:163
  260.4 5.0 %shard_map.96 = bf16[1024,2176]{1,0:T(8,128)(2,1)} custom-call(bf16[256,4,2176]{2,1,0:T(4,128)(2,1)} %all-to-all-done.1.x_ref), custom_call_target="tpu_custom_call" | custom-call | tf_op jit(solution)/shard_map/pallas_call | solution.py:57
  265.4 5.9 %fusion.7 = bf16[512,2048]{1,0:T(8,128)(2,1)} fusion(bf16[1024,2176]{1,0:T(8,128)(2,1)} %shard_map.96, s32[512]{0:T(512)S(1)} %multiply_add_fusion), kind=kOutput, calls=%fused_computation.9 | convolution fusion | flops 2149056512 | bytes 6293504 | tf_op jit(solution)/shard_map/dot_general | solution.py:181
  271.3 1.5 fusion.14
  272.8 0.6 fusion.23
  (20 shorter events, 0.5 us)
Async XLA Ops:
  15.1 16.6 %copy-start.2 = (s32[256]{0:T(256)S(1)}, s32[256]{0:T(256)}, u32[]{:S(2)}) copy-start(s32[256]{0:T(256)} %param.10) | copy-start | bytes 3076
  15.1 16.6 %copy-start.1 = (s32[256,6]{0,1:T(8,128)S(1)}, s32[256,6]{0,1:T(8,128)}, u32[]{:S(2)}) copy-start(s32[256,6]{0,1:T(8,128)} %param.9) | copy-start | bytes 18436
  15.1 119.7 %all-to-all-start = ((bf16[256,4,2176]{2,1,0:T(4,128)(2,1)}), bf16[256,4,2176]{2,1,0:T(4,128)(2,1)}, u32[]{:S(2)}, u32[]{:S(2)}) async-start(bf16[256,4,2176]{2,1,0:T(4,128)(2,1)} %shard_map.94), calls=%async_computation | async-start | bytes 8912896 | tf_op jit(solution)/shard_map/all_to_all | solution.py:154
  149.5 8.0 %copy-start = (bf16[1024,768]{1,0:T(8,128)(2,1)S(1)}, bf16[1024,768]{1,0:T(8,128)(2,1)}, u32[]{:S(2)}) copy-start(bf16[1024,768]{1,0:T(8,128)(2,1)} %get-tuple-element.7) | copy-start | bytes 4718596
  149.5 110.9 %all-to-all-start.1 = ((bf16[256,4,2176]{2,1,0:T(4,128)(2,1)}), bf16[256,4,2176]{2,1,0:T(4,128)(2,1)}, u32[]{:S(2)}, u32[]{:S(2)}) async-start(bf16[256,4,2176]{2,1,0:T(4,128)(2,1)} %get-tuple-element.6), calls=%async_computation.1 | async-start | bytes 8912896 | tf_op jit(solution)/shard_map/all_to_all | solution.py:163

commit v4 on v3

--- a/solution.py
+++ b/solution.py
@@ -2,6 +2,7 @@
 import jax.numpy as jnp
 from jax import lax
 from jax.experimental import pallas as pl
+from jax.experimental.pallas import tpu as pltpu
 from jax.sharding import PartitionSpec as P
 
 D = 2048
@@ -28,39 +29,84 @@
     return slot_ids * CAP + rank_in_group
 
 
-def _split_rows(x_ref, o_ref):
-    x = x_ref[...]
-    o_ref[...] = x.reshape(o_ref.shape)
-
-
-def _join_rows(x_ref, o_ref):
-    x = x_ref[...]
-    o_ref[...] = x.reshape(o_ref.shape)
-
-
-def to_groups(x):
-    rows, width = x.shape
-    groups = rows // CAP
+def _place(target_ref, hidden_ref, extras_ref, o_ref):
+    step_rows = o_ref.shape[0] * o_ref.shape[1]
+    tokens = hidden_ref.shape[0]
+    first = pl.program_id(0) * step_rows
+    hot = (
+        lax.broadcasted_iota(jnp.int32, (step_rows, tokens), 0) + first == target_ref[...]
+    ).astype(jnp.bfloat16)
+    rows = jnp.dot(hot, hidden_ref[...], preferred_element_type=jnp.float32)
+    extra = jnp.dot(hot, extras_ref[...], preferred_element_type=jnp.float32)
+    out = jnp.concatenate([rows.astype(jnp.bfloat16), extra.astype(jnp.bfloat16)], axis=1)
+    o_ref[...] = out.reshape(o_ref.shape)
+
+
+def place(target_place, hidden, extras, groups):
+    tokens, features = hidden.shape
+    width = features + extras.shape[1]
     step = min(GROUPS_PER_STEP, groups)
     return pl.pallas_call(
-        _split_rows,
+        _place,
         grid=(groups // step,),
-        in_specs=[pl.BlockSpec((step * CAP, width), lambda i: (i, 0))],
+        in_specs=[
+            pl.BlockSpec((1, tokens), lambda i: (0, 0)),
+            pl.BlockSpec((tokens, features), lambda i: (0, 0)),
+            pl.BlockSpec((tokens, extras.shape[1]), lambda i: (0, 0)),
+        ],
         out_specs=pl.BlockSpec((step, CAP, width), lambda i: (i, 0, 0)),
-        out_shape=jax.ShapeDtypeStruct((groups, CAP, width), x.dtype),
-    )(x)
-
-
-def from_groups(x):
-    groups, cap, width = x.shape
+        out_shape=jax.ShapeDtypeStruct((groups, CAP, width), hidden.dtype),
+    )(target_place.reshape(1, tokens), hidden, extras)
+
+
+def _unplace(target_ref, r_ref, rows_ref, extra_ref, acc_ref):
+    i = pl.program_id(0)
+    x = r_ref[...]
+    x = x.reshape(x.shape[0] * x.shape[1], x.shape[2])
+    step_rows = x.shape[0]
+    tokens = target_ref.shape[0]
+    hot = (
+        lax.broadcasted_iota(jnp.int32, (tokens, step_rows), 1) + i * step_rows == target_ref[...]
+    ).astype(jnp.bfloat16)
+    part = jnp.dot(hot, x, preferred_element_type=jnp.float32)
+
+    @pl.when(i == 0)
+    def _():
+        acc_ref[...] = part
+
+    @pl.when(i > 0)
+    def _():
+        acc_ref[...] = acc_ref[...] + part
+
+    @pl.when(i == pl.num_programs(0) - 1)
+    def _():
+        features = rows_ref.shape[1]
+        total = acc_ref[...]
+        rows_ref[...] = total[:, :features].astype(rows_ref.dtype)
+        extra_ref[...] = total[:, features:].astype(extra_ref.dtype)
+
+
+def unplace(target_place, returned, features):
+    groups, cap, width = returned.shape
+    tokens = target_place.shape[0]
     step = min(GROUPS_PER_STEP, groups)
     return pl.pallas_call(
-        _join_rows,
+        _unplace,
         grid=(groups // step,),
-        in_specs=[pl.BlockSpec((step, cap, width), lambda i: (i, 0, 0))],
-        out_specs=pl.BlockSpec((step * cap, width), lambda i: (i, 0)),
-        out_shape=jax.ShapeDtypeStruct((groups * cap, width), x.dtype),
-    )(x)
+        in_specs=[
+            pl.BlockSpec((tokens, 1), lambda i: (0, 0)),
+            pl.BlockSpec((step, cap, width), lambda i: (i, 0, 0)),
+        ],
+        out_specs=[
+            pl.BlockSpec((tokens, features), lambda i: (0, 0)),
+            pl.BlockSpec((tokens, width - features), lambda i: (0, 0)),
+        ],
+        out_shape=[
+            jax.ShapeDtypeStruct((tokens, features), returned.dtype),
+            jax.ShapeDtypeStruct((tokens, width - features), returned.dtype),
+        ],
+        scratch_shapes=[pltpu.VMEM((tokens, width), jnp.float32)],
+    )(target_place.reshape(tokens, 1), returned)
 
 
 def _middle(r_ref, cand_ref, back_ref, rows_ref, grads_ref):
@@ -132,10 +178,6 @@
     assert head_weight.shape[0] == SB * BLOCK
 
     target_place = place_tokens(token_language, language_owner)
-    place_hot = (
-        lax.broadcasted_iota(jnp.int32, (places, tokens), 0) == target_place[None, :]
-    ).astype(jnp.bfloat16)
-
     extra_cols = lax.broadcasted_iota(jnp.int32, (tokens, EXTRA), 1)
     label_hi = (labels // LABEL_SPLIT).astype(jnp.bfloat16)
     label_lo = (labels % LABEL_SPLIT).astype(jnp.bfloat16)
@@ -148,10 +190,8 @@
             jnp.where(extra_cols == 2, label_lo[:, None], jnp.zeros((), jnp.bfloat16)),
         ),
     )
-    packed = jnp.concatenate([hidden, extras], axis=1)
-    send = jnp.dot(place_hot, packed, preferred_element_type=jnp.float32).astype(jnp.bfloat16)
-
-    received = lax.all_to_all(to_groups(send), AXES, split_axis=0, concat_axis=0, tiled=True)
+    send = place(target_place, hidden, extras, devices)
+    received = lax.all_to_all(send, AXES, split_axis=0, concat_axis=0, tiled=True)
 
     self_index = lax.axis_index(AXES)
     owned_mask = (language_owner == self_index).astype(jnp.int32)
@@ -160,7 +200,7 @@
     candidates = jnp.take(slab, blocks, axis=0).reshape(LB * BLOCK, features)
 
     back, token_rows, grads = middle(received, candidates)
-    returned = from_groups(lax.all_to_all(back, AXES, split_axis=0, concat_axis=0, tiled=True))
+    returned = lax.all_to_all(back, AXES, split_axis=0, concat_axis=0, tiled=True)
 
     block_hot = blocks[None, :] == jnp.arange(SB, dtype=jnp.int32)[:, None]
     listed = jnp.any(block_hot, axis=1)
@@ -178,14 +218,8 @@
         preferred_element_type=jnp.float32,
     ).astype(jnp.bfloat16)
 
-    hidden_grad = lax.dot_general(
-        place_hot, returned[:, :features], (((0,), (0,)), ((), ())),
-        preferred_element_type=jnp.float32,
-    ).astype(jnp.bfloat16)
-    token_loss = lax.dot_general(
-        place_hot, returned[:, features:], (((0,), (0,)), ((), ())),
-        preferred_element_type=jnp.float32,
-    )[:, 0].astype(jnp.bfloat16)
+    hidden_grad, returned_extras = unplace(target_place, returned, features)
+    token_loss = returned_extras[:, 0]
     return (hidden_grad, token_loss, head_grad)
 
 

time: 274 us -> 267 us (0.974)
  matrix products: 21.4 us -> 8.23 us
  Pallas kernels: 24.8 us -> 28.6 us
    dot_general x3 -> x0, matrix products: 13.2 us -> none  [the longest x1 5.91 us: shards(): lax.dot_general(place_hot, returned[:, :features], (((0,), (0,)), ((), ()...]
    pallas_call x2, Pallas kernels: 10 us -> 13.8 us  [the longest x1 7.76 us: unplace(): pl.pallas_call(_unplace, grid=(groups // step,), in_specs=[pl.BlockSpec((...]
where the time goes in v4:
time: 267 us; the launch traced here: 266 us
  waiting for transfers between devices  184 us (69%)
  Pallas kernels  28.6 us (11%)
  starting transfers between devices  24.2 us (9%)
  local copies, waits for them, and re-layouts  12.2 us (5%)
  other arithmetic  8.41 us (3%)
  matrix products  8.23 us (3%)
    all_to_all x1, waiting for transfers between devices, shards(): lax.all_to_all(send, AXES, split_axis=0, concat_axis=0, tiled=True)  97.7 us
    all_to_all x1, waiting for transfers between devices, shards(): lax.all_to_all(back, AXES, split_axis=0, concat_axis=0, tiled=True)  86.1 us
    all_to_all x1, starting transfers between devices, shards(): lax.all_to_all(send, AXES, split_axis=0, concat_axis=0, tiled=True)  16.5 us
    pallas_call x1, Pallas kernels, middle(): pl.pallas_call(_middle, grid=(groups // step,), in_specs=[pl.BlockSpec((s...  14.7 us
    dot_general x1, matrix products, shards(): lax.dot_general(expanded, token_rows[:, :features], (((0,), (0,)), ((), (...  8.23 us
    pallas_call x1, Pallas kernels, unplace(): pl.pallas_call(_unplace, grid=(groups // step,), in_specs=[pl.BlockSpec((...  7.76 us
    all_to_all x1, starting transfers between devices, shards(): lax.all_to_all(back, AXES, split_axis=0, concat_axis=0, tiled=True)  7.68 us
    pallas_call x1, Pallas kernels, place(): pl.pallas_call(_place, grid=(groups // step,), in_specs=[pl.BlockSpec((1,...  6.08 us
  transfers between devices with their start and end apart: 2, of which 2 were waited for; matrix products, arithmetic and copies ran while one was open for 8% of the time, Pallas kernels for 0%

profile of v4, /device:TPU:1, one launch (start us, length us, event | category | flops | bytes accessed | tf_op | source)
XLA Modules:
  0.0 266.2 jit_solution(11300496136115850420)
XLA Ops:
  0.7 0.7 fusion.8
  1.3 1.0 convert_reduce_fusion
  2.4 0.9 select_reduce_fusion
  3.3 0.6 multiply_add_fusion
  3.9 1.6 select_select_fusion.extras_ref
  5.5 6.1 %shard_map.94 = bf16[256,4,2176]{2,1,0:T(4,128)(2,1)} custom-call(s32[1,512]{1,0:T(1,128)} %bitcast.30, bf16[512,2048]{1,0:T(8,128)(2,1)} %hidden_ref.1, bf16[512,128]{1,0:T(8,128)(2,1)} %select_select_fusion.extras_ref), custom_call_target="tpu_custom_call" | custom-call | tf_op jit(solution)/shard_map/pallas_call | solution.py:49
  11.6 16.5 %all-to-all-start = ((bf16[256,4,2176]{2,1,0:T(4,128)(2,1)}), bf16[256,4,2176]{2,1,0:T(4,128)(2,1)}, u32[]{:S(2)}, u32[]{:S(2)}) async-start(bf16[256,4,2176]{2,1,0:T(4,128)(2,1)} %shard_map.94), calls=%async_computation | async-start | bytes 8912896 | tf_op jit(solution)/shard_map/all_to_all | solution.py:194
  28.2 0.1 multiply_reduce_fusion
  28.3 2.9 %gather_fusion = bf16[6,128,2048]{2,1,0:T(8,128)(2,1)S(1)} fusion(bf16[8,128,2048]{2,1,0:T(8,128)(2,1)} %bitcast.29, s32[1024]{0:T(1024)S(1)} %pad_clamp_fusion.1), kind=kCustom, calls=%fused_computation | custom fusion | bytes 6291480 | tf_op jit(solution)/shard_map/jit(_take)/gather | solution.py:200
  31.3 2.2 bitcast_select_fusion.cand_ref
  33.5 97.7 %all-to-all-done.r_ref = bf16[256,4,2176]{2,1,0:T(4,128)(2,1)} async-done(((bf16[256,4,2176]{2,1,0:T(4,128)(2,1)}), bf16[256,4,2176]{2,1,0:T(4,128)(2,1)}, u32[]{:S(2)}, u32[]{:S(2)}) %all-to-all-start) | async-done | bytes 4456480 | tf_op jit(solution)/shard_map/all_to_all | solution.py:194
  131.2 14.7 %shard_map.95 = (bf16[256,4,2176]{2,1,0:T(4,128)(2,1)}, bf16[1024,2176]{1,0:T(8,128)(2,1)}, bf16[1024,768]{1,0:T(8,128)(2,1)}) custom-call(bf16[256,4,2176]{2,1,0:T(4,128)(2,1)} %all-to-all-done.r_ref, bf16[768,2048]{1,0:T(8,128)(2,1)} %bitcast_select_fusion.cand_ref), custom_call_target="tpu_custom_call" | custom-call | tf_op jit(solution)/shard_map/pallas_call | solution.py:152
  146.0 7.7 %all-to-all-start.1 = ((bf16[256,4,2176]{2,1,0:T(4,128)(2,1)}), bf16[256,4,2176]{2,1,0:T(4,128)(2,1)}, u32[]{:S(2)}, u32[]{:S(2)}) async-start(bf16[256,4,2176]{2,1,0:T(4,128)(2,1)} %get-tuple-element.8), calls=%async_computation.1 | async-start | bytes 8912896 | tf_op jit(solution)/shard_map/all_to_all | solution.py:203
  153.6 0.9 copy.17.target_ref
  154.5 0.1 fusion.7
  154.9 0.8 copy.18
  155.6 0.9 copy.19
  156.5 2.1 gather_fusion.1
  158.7 2.9 %copy.20 = bf16[1024,8,128]{0,2,1:T(8,128)(2,1)S(1)} copy(bf16[1024,8,128]{2,0,1:T(8,128)(2,1)} %bitcast.27) | data formatting | bytes 4194304 | tf_op jit(solution)/shard_map/jit(_take)/gather | solution.py:213
  161.5 1.0 fusion.5
  162.5 8.2 %fusion.2 = bf16[1024,2048]{1,0:T(8,128)(2,1)} fusion(bf16[1024,1024]{0,1:T(8,128)(2,1)S(1)} %fusion.5, bf16[1024,2176]{1,0:T(8,128)(2,1)} %get-tuple-element.12), kind=kOutput, calls=%fused_computation.4 | convolution fusion | flops 4297064448 | bytes 10485760 | tf_op jit(solution)/shard_map/dot_general | solution.py:216
  170.7 86.1 %all-to-all-done.1.r_ref = bf16[256,4,2176]{2,1,0:T(4,128)(2,1)} async-done(((bf16[256,4,2176]{2,1,0:T(4,128)(2,1)}), bf16[256,4,2176]{2,1,0:T(4,128)(2,1)}, u32[]{:S(2)}, u32[]{:S(2)}) %all-to-all-start.1) | async-done | bytes 4456480 | tf_op jit(solution)/shard_map/all_to_all | solution.py:203
  256.8 7.8 %shard_map.96 = (bf16[512,2048]{1,0:T(8,128)(2,1)}, bf16[512,128]{1,0:T(8,128)(2,1)}) custom-call(s32[512,1]{1,0:T(8,128)} %copy.17.target_ref, bf16[256,4,2176]{2,1,0:T(4,128)(2,1)} %all-to-all-done.1.r_ref), custom_call_target="tpu_custom_call" | custom-call | tf_op jit(solution)/shard_map/pallas_call | solution.py:93
  264.6 1.6 slice_reduce_fusion
  (20 shorter events, 0.3 us)
Async XLA Ops:
  11.6 16.6 %copy-start.3 = (s32[256]{0:T(256)S(1)}, s32[256]{0:T(256)}, u32[]{:S(2)}) copy-start(s32[256]{0:T(256)} %param.10) | copy-start | bytes 3076
  11.6 16.6 %copy-start.2 = (s32[256,6]{0,1:T(8,128)S(1)}, s32[256,6]{0,1:T(8,128)}, u32[]{:S(2)}) copy-start(s32[256,6]{0,1:T(8,128)} %param.9) | copy-start | bytes 18436
  11.6 119.7 %all-to-all-start = ((bf16[256,4,2176]{2,1,0:T(4,128)(2,1)}), bf16[256,4,2176]{2,1,0:T(4,128)(2,1)}, u32[]{:S(2)}, u32[]{:S(2)}) async-start(bf16[256,4,2176]{2,1,0:T(4,128)(2,1)} %shard_map.94), calls=%async_computation | async-start | bytes 8912896 | tf_op jit(solution)/shard_map/all_to_all | solution.py:194
  145.9 7.7 %copy-start.1 = (s32[512]{0:T(512)S(1)}, s32[512]{0:T(512)}, u32[]{:S(2)}) copy-start(s32[512]{0:T(512)} %multiply_add_fusion) | copy-start | bytes 6148
  145.9 8.9 %copy-start = (bf16[1024,768]{1,0:T(8,128)(2,1)S(1)}, bf16[1024,768]{1,0:T(8,128)(2,1)}, u32[]{:S(2)}) copy-start(bf16[1024,768]{1,0:T(8,128)(2,1)} %get-tuple-element.11) | copy-start | bytes 4718596
  146.0 110.9 %all-to-all-start.1 = ((bf16[256,4,2176]{2,1,0:T(4,128)(2,1)}), bf16[256,4,2176]{2,1,0:T(4,128)(2,1)}, u32[]{:S(2)}, u32[]{:S(2)}) async-start(bf16[256,4,2176]{2,1,0:T(4,128)(2,1)} %get-tuple-element.8), calls=%async_computation.1 | async-start | bytes 8912896 | tf_op jit(solution)/shard_map/all_to_all | solution.py:203

commit v5 on v4

--- a/solution.py
+++ b/solution.py
@@ -2,7 +2,6 @@
 import jax.numpy as jnp
 from jax import lax
 from jax.experimental import pallas as pl
-from jax.experimental.pallas import tpu as pltpu
 from jax.sharding import PartitionSpec as P
 
 D = 2048
@@ -15,7 +14,7 @@
 
 SMOOTH = 0.1
 AXES = ("vocab", "fsdp")
-GROUPS_PER_STEP = 64
+GROUPS_PER_STEP = 32
 
 
 def place_tokens(token_language, language_owner):
@@ -59,43 +58,28 @@
     )(target_place.reshape(1, tokens), hidden, extras)
 
 
-def _unplace(target_ref, r_ref, rows_ref, extra_ref, acc_ref):
-    i = pl.program_id(0)
+def _unplace(target_ref, r_ref, rows_ref, extra_ref):
     x = r_ref[...]
     x = x.reshape(x.shape[0] * x.shape[1], x.shape[2])
-    step_rows = x.shape[0]
     tokens = target_ref.shape[0]
     hot = (
-        lax.broadcasted_iota(jnp.int32, (tokens, step_rows), 1) + i * step_rows == target_ref[...]
-    ).astype(jnp.bfloat16)
-    part = jnp.dot(hot, x, preferred_element_type=jnp.float32)
-
-    @pl.when(i == 0)
-    def _():
-        acc_ref[...] = part
-
-    @pl.when(i > 0)
-    def _():
-        acc_ref[...] = acc_ref[...] + part
-
-    @pl.when(i == pl.num_programs(0) - 1)
-    def _():
-        features = rows_ref.shape[1]
-        total = acc_ref[...]
-        rows_ref[...] = total[:, :features].astype(rows_ref.dtype)
-        extra_ref[...] = total[:, features:].astype(extra_ref.dtype)
+        lax.broadcasted_iota(jnp.int32, (tokens, x.shape[0]), 1) == target_ref[...]
+    ).astype(jnp.bfloat16)
+    total = jnp.dot(hot, x, preferred_element_type=jnp.float32)
+    features = rows_ref.shape[1]
+    rows_ref[...] = total[:, :features].astype(rows_ref.dtype)
+    extra_ref[...] = total[:, features:].astype(extra_ref.dtype)
 
 
 def unplace(target_place, returned, features):
     groups, cap, width = returned.shape
     tokens = target_place.shape[0]
-    step = min(GROUPS_PER_STEP, groups)
     return pl.pallas_call(
         _unplace,
-        grid=(groups // step,),
+        grid=(1,),
         in_specs=[
             pl.BlockSpec((tokens, 1), lambda i: (0, 0)),
-            pl.BlockSpec((step, cap, width), lambda i: (i, 0, 0)),
+            pl.BlockSpec((groups, cap, width), lambda i: (0, 0, 0)),
         ],
         out_specs=[
             pl.BlockSpec((tokens, features), lambda i: (0, 0)),
@@ -105,7 +89,6 @@
             jax.ShapeDtypeStruct((tokens, features), returned.dtype),
             jax.ShapeDtypeStruct((tokens, width - features), returned.dtype),
         ],
-        scratch_shapes=[pltpu.VMEM((tokens, width), jnp.float32)],
     )(target_place.reshape(tokens, 1), returned)
 
 

time: 267 us -> 275 us (1.030)
  Pallas kernels: 28.6 us -> 37.2 us
    pallas_call x1, Pallas kernels: 14.7 us -> 23.3 us  [middle(): pl.pallas_call(_middle, grid=(groups // step,), in_specs=[pl.BlockSpec((s...]
where the time goes in v5:
time: 275 us
  waiting for transfers between devices  184 us (67%)
  Pallas kernels  37.2 us (14%)
  starting transfers between devices  24.2 us (9%)
  local copies, waits for them, and re-layouts  12.2 us (4%)
  other arithmetic  8.41 us (3%)
  matrix products  8.23 us (3%)
    all_to_all x1, waiting for transfers between devices, shards(): lax.all_to_all(send, AXES, split_axis=0, concat_axis=0, tiled=True)  97.7 us
    all_to_all x1, waiting for transfers between devices, shards(): lax.all_to_all(back, AXES, split_axis=0, concat_axis=0, tiled=True)  86.1 us
    pallas_call x1, Pallas kernels, middle(): pl.pallas_call(_middle, grid=(groups // step,), in_specs=[pl.BlockSpec((s...  23.3 us
    all_to_all x1, starting transfers between devices, shards(): lax.all_to_all(send, AXES, split_axis=0, concat_axis=0, tiled=True)  16.5 us
    dot_general x1, matrix products, shards(): lax.dot_general(expanded, token_rows[:, :features], (((0,), (0,)), ((), (...  8.23 us
    all_to_all x1, starting transfers between devices, shards(): lax.all_to_all(back, AXES, split_axis=0, concat_axis=0, tiled=True)  7.68 us
    pallas_call x1, Pallas kernels, place(): pl.pallas_call(_place, grid=(groups // step,), in_specs=[pl.BlockSpec((1,...  7.38 us
    pallas_call x1, Pallas kernels, unplace(): pl.pallas_call(_unplace, grid=(1,), in_specs=[pl.BlockSpec((tokens, 1), l...  6.48 us
  transfers between devices with their start and end apart: 2, of which 2 were waited for; matrix products, arithmetic and copies ran while one was open for 8% of the time, Pallas kernels for 0%

profile of v5, /device:TPU:1, one launch (start us, length us, event | category | flops | bytes accessed | tf_op | source)
XLA Modules:
  0.0 274.8 jit_solution(10440587984532456911)
XLA Ops:
  0.7 0.7 fusion.8
  1.3 1.0 convert_reduce_fusion
  2.4 0.9 select_reduce_fusion
  3.3 0.6 multiply_add_fusion
  3.9 1.6 select_select_fusion.extras_ref
  5.5 7.4 %shard_map.94 = bf16[256,4,2176]{2,1,0:T(4,128)(2,1)} custom-call(s32[1,512]{1,0:T(1,128)} %bitcast.30, bf16[512,2048]{1,0:T(8,128)(2,1)} %hidden_ref.1, bf16[512,128]{1,0:T(8,128)(2,1)} %select_select_fusion.extras_ref), custom_call_target="tpu_custom_call" | custom-call | tf_op jit(solution)/shard_map/pallas_call | solution.py:48
  12.9 16.5 %all-to-all-start = ((bf16[256,4,2176]{2,1,0:T(4,128)(2,1)}), bf16[256,4,2176]{2,1,0:T(4,128)(2,1)}, u32[]{:S(2)}, u32[]{:S(2)}) async-start(bf16[256,4,2176]{2,1,0:T(4,128)(2,1)} %shard_map.94), calls=%async_computation | async-start | bytes 8912896 | tf_op jit(solution)/shard_map/all_to_all | solution.py:177
  29.4 0.1 multiply_reduce_fusion
  29.6 2.9 %gather_fusion = bf16[6,128,2048]{2,1,0:T(8,128)(2,1)S(1)} fusion(bf16[8,128,2048]{2,1,0:T(8,128)(2,1)} %bitcast.29, s32[1024]{0:T(1024)S(1)} %pad_clamp_fusion.1), kind=kCustom, calls=%fused_computation | custom fusion | bytes 6291480 | tf_op jit(solution)/shard_map/jit(_take)/gather | solution.py:183
  32.6 2.2 bitcast_select_fusion.cand_ref
  34.8 97.7 %all-to-all-done.r_ref = bf16[256,4,2176]{2,1,0:T(4,128)(2,1)} async-done(((bf16[256,4,2176]{2,1,0:T(4,128)(2,1)}), bf16[256,4,2176]{2,1,0:T(4,128)(2,1)}, u32[]{:S(2)}, u32[]{:S(2)}) %all-to-all-start) | async-done | bytes 4456480 | tf_op jit(solution)/shard_map/all_to_all | solution.py:177
  132.5 23.3 %shard_map.95 = (bf16[256,4,2176]{2,1,0:T(4,128)(2,1)}, bf16[1024,2176]{1,0:T(8,128)(2,1)}, bf16[1024,768]{1,0:T(8,128)(2,1)}) custom-call(bf16[256,4,2176]{2,1,0:T(4,128)(2,1)} %all-to-all-done.r_ref, bf16[768,2048]{1,0:T(8,128)(2,1)} %bitcast_select_fusion.cand_ref), custom_call_target="tpu_custom_call" | custom-call | tf_op jit(solution)/shard_map/pallas_call | solution.py:135
  155.8 7.7 %all-to-all-start.1 = ((bf16[256,4,2176]{2,1,0:T(4,128)(2,1)}), bf16[256,4,2176]{2,1,0:T(4,128)(2,1)}, u32[]{:S(2)}, u32[]{:S(2)}) async-start(bf16[256,4,2176]{2,1,0:T(4,128)(2,1)} %get-tuple-element.8), calls=%async_computation.1 | async-start | bytes 8912896 | tf_op jit(solution)/shard_map/all_to_all | solution.py:186
  163.5 0.9 copy.17.target_ref
  164.4 0.1 fusion.7
  164.7 0.8 copy.18
  165.5 0.9 copy.19
  166.4 2.1 gather_fusion.1
  168.5 2.9 %copy.20 = bf16[1024,8,128]{0,2,1:T(8,128)(2,1)S(1)} copy(bf16[1024,8,128]{2,0,1:T(8,128)(2,1)} %bitcast.27) | data formatting | bytes 4194304 | tf_op jit(solution)/shard_map/jit(_take)/gather | solution.py:196
  171.4 1.0 fusion.5
  172.4 8.2 %fusion.2 = bf16[1024,2048]{1,0:T(8,128)(2,1)} fusion(bf16[1024,1024]{0,1:T(8,128)(2,1)S(1)} %fusion.5, bf16[1024,2176]{1,0:T(8,128)(2,1)} %get-tuple-element.12), kind=kOutput, calls=%fused_computation.4 | convolution fusion | flops 4297064448 | bytes 10485760 | tf_op jit(solution)/shard_map/dot_general | solution.py:199
  180.6 86.1 %all-to-all-done.1.r_ref = bf16[256,4,2176]{2,1,0:T(4,128)(2,1)} async-done(((bf16[256,4,2176]{2,1,0:T(4,128)(2,1)}), bf16[256,4,2176]{2,1,0:T(4,128)(2,1)}, u32[]{:S(2)}, u32[]{:S(2)}) %all-to-all-start.1) | async-done | bytes 4456480 | tf_op jit(solution)/shard_map/all_to_all | solution.py:186
  266.7 6.5 %shard_map.96 = (bf16[512,2048]{1,0:T(8,128)(2,1)}, bf16[512,128]{1,0:T(8,128)(2,1)}) custom-call(s32[512,1]{1,0:T(8,128)} %copy.17.target_ref, bf16[256,4,2176]{2,1,0:T(4,128)(2,1)} %all-to-all-done.1.r_ref), custom_call_target="tpu_custom_call" | custom-call | tf_op jit(solution)/shard_map/pallas_call | solution.py:77
  273.2 1.6 slice_reduce_fusion
  (20 shorter events, 0.3 us)
Async XLA Ops:
  12.9 16.6 %copy-start.3 = (s32[256]{0:T(256)S(1)}, s32[256]{0:T(256)}, u32[]{:S(2)}) copy-start(s32[256]{0:T(256)} %param.10) | copy-start | bytes 3076
  12.9 16.6 %copy-start.2 = (s32[256,6]{0,1:T(8,128)S(1)}, s32[256,6]{0,1:T(8,128)}, u32[]{:S(2)}) copy-start(s32[256,6]{0,1:T(8,128)} %param.9) | copy-start | bytes 18436
  12.9 119.6 %all-to-all-start = ((bf16[256,4,2176]{2,1,0:T(4,128)(2,1)}), bf16[256,4,2176]{2,1,0:T(4,128)(2,1)}, u32[]{:S(2)}, u32[]{:S(2)}) async-start(bf16[256,4,2176]{2,1,0:T(4,128)(2,1)} %shard_map.94), calls=%async_computation | async-start | bytes 8912896 | tf_op jit(solution)/shard_map/all_to_all | solution.py:177
  155.8 7.7 %copy-start.1 = (s32[512]{0:T(512)S(1)}, s32[512]{0:T(512)}, u32[]{:S(2)}) copy-start(s32[512]{0:T(512)} %multiply_add_fusion) | copy-start | bytes 6148
  155.8 8.9 %copy-start = (bf16[1024,768]{1,0:T(8,128)(2,1)S(1)}, bf16[1024,768]{1,0:T(8,128)(2,1)}, u32[]{:S(2)}) copy-start(bf16[1024,768]{1,0:T(8,128)(2,1)} %get-tuple-element.11) | copy-start | bytes 4718596
  155.8 110.9 %all-to-all-start.1 = ((bf16[256,4,2176]{2,1,0:T(4,128)(2,1)}), bf16[256,4,2176]{2,1,0:T(4,128)(2,1)}, u32[]{:S(2)}, u32[]{:S(2)}) async-start(bf16[256,4,2176]{2,1,0:T(4,128)(2,1)} %get-tuple-element.8), calls=%async_computation.1 | async-start | bytes 8912896 | tf_op jit(solution)/shard_map/all_to_all | solution.py:186

commit v6 on v5

--- a/solution.py
+++ b/solution.py
@@ -14,7 +14,7 @@
 
 SMOOTH = 0.1
 AXES = ("vocab", "fsdp")
-GROUPS_PER_STEP = 32
+GROUPS_PER_STEP = 128
 
 
 def place_tokens(token_language, language_owner):

time: 275 us -> 265 us (0.964)
  Pallas kernels: 37.2 us -> 27 us
    pallas_call x1, Pallas kernels: 23.3 us -> 14.6 us  [middle(): pl.pallas_call(_middle, grid=(groups // step,), in_specs=[pl.BlockSpec((s...]
where the time goes in v6:
time: 265 us
  waiting for transfers between devices  184 us (69%)
  Pallas kernels  27 us (10%)
  starting transfers between devices  24.2 us (9%)
  local copies, waits for them, and re-layouts  12.2 us (5%)
  other arithmetic  8.41 us (3%)
  matrix products  8.23 us (3%)
    all_to_all x1, waiting for transfers between devices, shards(): lax.all_to_all(send, AXES, split_axis=0, concat_axis=0, tiled=True)  97.7 us
    all_to_all x1, waiting for transfers between devices, shards(): lax.all_to_all(back, AXES, split_axis=0, concat_axis=0, tiled=True)  86.1 us
    all_to_all x1, starting transfers between devices, shards(): lax.all_to_all(send, AXES, split_axis=0, concat_axis=0, tiled=True)  16.5 us
    pallas_call x1, Pallas kernels, middle(): pl.pallas_call(_middle, grid=(groups // step,), in_specs=[pl.BlockSpec((s...  14.6 us
    dot_general x1, matrix products, shards(): lax.dot_general(expanded, token_rows[:, :features], (((0,), (0,)), ((), (...  8.23 us
    all_to_all x1, starting transfers between devices, shards(): lax.all_to_all(back, AXES, split_axis=0, concat_axis=0, tiled=True)  7.67 us
    pallas_call x1, Pallas kernels, unplace(): pl.pallas_call(_unplace, grid=(1,), in_specs=[pl.BlockSpec((tokens, 1), l...  6.48 us
    pallas_call x1, Pallas kernels, place(): pl.pallas_call(_place, grid=(groups // step,), in_specs=[pl.BlockSpec((1,...  5.85 us
  transfers between devices with their start and end apart: 2, of which 2 were waited for; matrix products, arithmetic and copies ran while one was open for 8% of the time, Pallas kernels for 0%

profile of v6, /device:TPU:1, one launch (start us, length us, event | category | flops | bytes accessed | tf_op | source)
XLA Modules:
  0.0 264.6 jit_solution(3217655828622538993)
XLA Ops:
  0.7 0.7 fusion.8
  1.3 1.0 convert_reduce_fusion
  2.4 0.9 select_reduce_fusion
  3.3 0.6 multiply_add_fusion
  3.9 1.6 select_select_fusion.extras_ref
  5.5 5.9 %shard_map.94 = bf16[256,4,2176]{2,1,0:T(4,128)(2,1)} custom-call(s32[1,512]{1,0:T(1,128)} %bitcast.30, bf16[512,2048]{1,0:T(8,128)(2,1)} %hidden_ref.1, bf16[512,128]{1,0:T(8,128)(2,1)} %select_select_fusion.extras_ref), custom_call_target="tpu_custom_call" | custom-call | tf_op jit(solution)/shard_map/pallas_call | solution.py:48
  11.3 16.5 %all-to-all-start = ((bf16[256,4,2176]{2,1,0:T(4,128)(2,1)}), bf16[256,4,2176]{2,1,0:T(4,128)(2,1)}, u32[]{:S(2)}, u32[]{:S(2)}) async-start(bf16[256,4,2176]{2,1,0:T(4,128)(2,1)} %shard_map.94), calls=%async_computation | async-start | bytes 8912896 | tf_op jit(solution)/shard_map/all_to_all | solution.py:177
  27.9 0.1 multiply_reduce_fusion
  28.1 2.9 %gather_fusion = bf16[6,128,2048]{2,1,0:T(8,128)(2,1)S(1)} fusion(bf16[8,128,2048]{2,1,0:T(8,128)(2,1)} %bitcast.29, s32[1024]{0:T(1024)S(1)} %pad_clamp_fusion.1), kind=kCustom, calls=%fused_computation | custom fusion | bytes 6291480 | tf_op jit(solution)/shard_map/jit(_take)/gather | solution.py:183
  31.1 2.2 bitcast_select_fusion.cand_ref
  33.3 97.7 %all-to-all-done.r_ref = bf16[256,4,2176]{2,1,0:T(4,128)(2,1)} async-done(((bf16[256,4,2176]{2,1,0:T(4,128)(2,1)}), bf16[256,4,2176]{2,1,0:T(4,128)(2,1)}, u32[]{:S(2)}, u32[]{:S(2)}) %all-to-all-start) | async-done | bytes 4456480 | tf_op jit(solution)/shard_map/all_to_all | solution.py:177
  131.0 14.6 %shard_map.95 = (bf16[256,4,2176]{2,1,0:T(4,128)(2,1)}, bf16[1024,2176]{1,0:T(8,128)(2,1)}, bf16[1024,768]{1,0:T(8,128)(2,1)}) custom-call(bf16[256,4,2176]{2,1,0:T(4,128)(2,1)} %all-to-all-done.r_ref, bf16[768,2048]{1,0:T(8,128)(2,1)} %bitcast_select_fusion.cand_ref), custom_call_target="tpu_custom_call" | custom-call | tf_op jit(solution)/shard_map/pallas_call | solution.py:135
  145.6 7.7 %all-to-all-start.1 = ((bf16[256,4,2176]{2,1,0:T(4,128)(2,1)}), bf16[256,4,2176]{2,1,0:T(4,128)(2,1)}, u32[]{:S(2)}, u32[]{:S(2)}) async-start(bf16[256,4,2176]{2,1,0:T(4,128)(2,1)} %get-tuple-element.8), calls=%async_computation.1 | async-start | bytes 8912896 | tf_op jit(solution)/shard_map/all_to_all | solution.py:186
  153.3 0.9 copy.17.target_ref
  154.2 0.1 fusion.7
  154.5 0.8 copy.18
  155.3 0.9 copy.19
  156.2 2.1 gather_fusion.1
  158.3 2.9 %copy.20 = bf16[1024,8,128]{0,2,1:T(8,128)(2,1)S(1)} copy(bf16[1024,8,128]{2,0,1:T(8,128)(2,1)} %bitcast.27) | data formatting | bytes 4194304 | tf_op jit(solution)/shard_map/jit(_take)/gather | solution.py:196
  161.2 1.0 fusion.5
  162.2 8.2 %fusion.2 = bf16[1024,2048]{1,0:T(8,128)(2,1)} fusion(bf16[1024,1024]{0,1:T(8,128)(2,1)S(1)} %fusion.5, bf16[1024,2176]{1,0:T(8,128)(2,1)} %get-tuple-element.12), kind=kOutput, calls=%fused_computation.4 | convolution fusion | flops 4297064448 | bytes 10485760 | tf_op jit(solution)/shard_map/dot_general | solution.py:199
  170.4 86.1 %all-to-all-done.1.r_ref = bf16[256,4,2176]{2,1,0:T(4,128)(2,1)} async-done(((bf16[256,4,2176]{2,1,0:T(4,128)(2,1)}), bf16[256,4,2176]{2,1,0:T(4,128)(2,1)}, u32[]{:S(2)}, u32[]{:S(2)}) %all-to-all-start.1) | async-done | bytes 4456480 | tf_op jit(solution)/shard_map/all_to_all | solution.py:186
  256.5 6.5 %shard_map.96 = (bf16[512,2048]{1,0:T(8,128)(2,1)}, bf16[512,128]{1,0:T(8,128)(2,1)}) custom-call(s32[512,1]{1,0:T(8,128)} %copy.17.target_ref, bf16[256,4,2176]{2,1,0:T(4,128)(2,1)} %all-to-all-done.1.r_ref), custom_call_target="tpu_custom_call" | custom-call | tf_op jit(solution)/shard_map/pallas_call | solution.py:77
  263.0 1.6 slice_reduce_fusion
  (20 shorter events, 0.3 us)
Async XLA Ops:
  11.3 16.5 %copy-start.3 = (s32[256]{0:T(256)S(1)}, s32[256]{0:T(256)}, u32[]{:S(2)}) copy-start(s32[256]{0:T(256)} %param.10) | copy-start | bytes 3076
  11.3 16.6 %copy-start.2 = (s32[256,6]{0,1:T(8,128)S(1)}, s32[256,6]{0,1:T(8,128)}, u32[]{:S(2)}) copy-start(s32[256,6]{0,1:T(8,128)} %param.9) | copy-start | bytes 18436
  11.3 119.6 %all-to-all-start = ((bf16[256,4,2176]{2,1,0:T(4,128)(2,1)}), bf16[256,4,2176]{2,1,0:T(4,128)(2,1)}, u32[]{:S(2)}, u32[]{:S(2)}) async-start(bf16[256,4,2176]{2,1,0:T(4,128)(2,1)} %shard_map.94), calls=%async_computation | async-start | bytes 8912896 | tf_op jit(solution)/shard_map/all_to_all | solution.py:177
  145.6 7.7 %copy-start.1 = (s32[512]{0:T(512)S(1)}, s32[512]{0:T(512)}, u32[]{:S(2)}) copy-start(s32[512]{0:T(512)} %multiply_add_fusion) | copy-start | bytes 6148
  145.6 8.9 %copy-start = (bf16[1024,768]{1,0:T(8,128)(2,1)S(1)}, bf16[1024,768]{1,0:T(8,128)(2,1)}, u32[]{:S(2)}) copy-start(bf16[1024,768]{1,0:T(8,128)(2,1)} %get-tuple-element.11) | copy-start | bytes 4718596
  145.6 110.9 %all-to-all-start.1 = ((bf16[256,4,2176]{2,1,0:T(4,128)(2,1)}), bf16[256,4,2176]{2,1,0:T(4,128)(2,1)}, u32[]{:S(2)}, u32[]{:S(2)}) async-start(bf16[256,4,2176]{2,1,0:T(4,128)(2,1)} %get-tuple-element.8), calls=%async_computation.1 | async-start | bytes 8912896 | tf_op jit(solution)/shard_map/all_to_all | solution.py:186

commit v7 on v6

--- a/solution.py
+++ b/solution.py
@@ -17,79 +17,120 @@
 GROUPS_PER_STEP = 128
 
 
-def place_tokens(token_language, language_owner):
-    language = token_language[:, 0]
-    languages = language_owner.shape[0]
-    matches = language[:, None] == jnp.arange(languages, dtype=jnp.int32)[None, :]
-    slot_ids = jnp.sum(jnp.where(matches, language_owner[None, :], 0), axis=1)
-    positions = jnp.arange(language.shape[0], dtype=jnp.int32)
-    earlier = (language[:, None] == language[None, :]) & (positions[None, :] < positions[:, None])
-    rank_in_group = jnp.sum(earlier.astype(jnp.int32), axis=1)
-    return slot_ids * CAP + rank_in_group
-
-
-def _place(target_ref, hidden_ref, extras_ref, o_ref):
+def _place(lang_col_ref, lang_row_ref, owner_ref, labels_ref, weights_ref, hidden_ref, o_ref, target_ref):
+    tokens = hidden_ref.shape[0]
+    languages = owner_ref.shape[0]
+    lang_row = lang_row_ref[...]
+    earlier = (lang_col_ref[...] == lang_row) & (
+        lax.broadcasted_iota(jnp.int32, (tokens, tokens), 0)
+        < lax.broadcasted_iota(jnp.int32, (tokens, tokens), 1)
+    )
+    rank = jnp.sum(earlier.astype(jnp.int32), axis=0, keepdims=True)
+    slot = jnp.sum(
+        jnp.where(
+            lax.broadcasted_iota(jnp.int32, (languages, tokens), 0) == lang_row, owner_ref[...], 0
+        ),
+        axis=0,
+        keepdims=True,
+    )
+    target = slot * CAP + rank
+    target_ref[...] = target
+    labels = labels_ref[...]
+    kind = lax.broadcasted_iota(jnp.int32, (EXTRA, tokens), 0)
+    extras_t = jnp.where(
+        kind == 0,
+        weights_ref[...].astype(jnp.float32),
+        jnp.where(
+            kind == 1,
+            (labels // LABEL_SPLIT).astype(jnp.float32),
+            jnp.where(kind == 2, (labels % LABEL_SPLIT).astype(jnp.float32), 0.0),
+        ),
+    ).astype(jnp.bfloat16)
     step_rows = o_ref.shape[0] * o_ref.shape[1]
-    tokens = hidden_ref.shape[0]
     first = pl.program_id(0) * step_rows
-    hot = (
-        lax.broadcasted_iota(jnp.int32, (step_rows, tokens), 0) + first == target_ref[...]
-    ).astype(jnp.bfloat16)
+    hot = (lax.broadcasted_iota(jnp.int32, (step_rows, tokens), 0) + first == target).astype(
+        jnp.bfloat16
+    )
     rows = jnp.dot(hot, hidden_ref[...], preferred_element_type=jnp.float32)
-    extra = jnp.dot(hot, extras_ref[...], preferred_element_type=jnp.float32)
+    extra = lax.dot_general(
+        hot, extras_t, (((1,), (1,)), ((), ())), preferred_element_type=jnp.float32
+    )
     out = jnp.concatenate([rows.astype(jnp.bfloat16), extra.astype(jnp.bfloat16)], axis=1)
     o_ref[...] = out.reshape(o_ref.shape)
 
 
-def place(target_place, hidden, extras, groups):
+def place(token_language, language_owner, labels, loss_weight, hidden, groups):
     tokens, features = hidden.shape
-    width = features + extras.shape[1]
+    languages = language_owner.shape[0]
+    width = features + EXTRA
     step = min(GROUPS_PER_STEP, groups)
+    whole = lambda i: (0, 0)
     return pl.pallas_call(
         _place,
         grid=(groups // step,),
         in_specs=[
-            pl.BlockSpec((1, tokens), lambda i: (0, 0)),
-            pl.BlockSpec((tokens, features), lambda i: (0, 0)),
-            pl.BlockSpec((tokens, extras.shape[1]), lambda i: (0, 0)),
-        ],
-        out_specs=pl.BlockSpec((step, CAP, width), lambda i: (i, 0, 0)),
-        out_shape=jax.ShapeDtypeStruct((groups, CAP, width), hidden.dtype),
-    )(target_place.reshape(1, tokens), hidden, extras)
-
-
-def _unplace(target_ref, r_ref, rows_ref, extra_ref):
+            pl.BlockSpec((tokens, 1), whole),
+            pl.BlockSpec((1, tokens), whole),
+            pl.BlockSpec((languages, 1), whole),
+            pl.BlockSpec((1, tokens), whole),
+            pl.BlockSpec((1, tokens), whole),
+            pl.BlockSpec((tokens, features), whole),
+        ],
+        out_specs=[
+            pl.BlockSpec((step, CAP, width), lambda i: (i, 0, 0)),
+            pl.BlockSpec((1, tokens), whole),
+        ],
+        out_shape=[
+            jax.ShapeDtypeStruct((groups, CAP, width), hidden.dtype),
+            jax.ShapeDtypeStruct((1, tokens), jnp.int32),
+        ],
+    )(
+        token_language,
+        token_language.reshape(1, tokens),
+        language_owner.reshape(languages, 1),
+        labels.reshape(1, tokens),
+        loss_weight.reshape(1, tokens),
+        hidden,
+    )
+
+
+def _unplace(target_ref, r_ref, rows_ref, loss_ref):
     x = r_ref[...]
     x = x.reshape(x.shape[0] * x.shape[1], x.shape[2])
-    tokens = target_ref.shape[0]
-    hot = (
-        lax.broadcasted_iota(jnp.int32, (tokens, x.shape[0]), 1) == target_ref[...]
-    ).astype(jnp.bfloat16)
-    total = jnp.dot(hot, x, preferred_element_type=jnp.float32)
+    tokens = target_ref.shape[1]
     features = rows_ref.shape[1]
-    rows_ref[...] = total[:, :features].astype(rows_ref.dtype)
-    extra_ref[...] = total[:, features:].astype(extra_ref.dtype)
-
-
-def unplace(target_place, returned, features):
+    hot_t = (lax.broadcasted_iota(jnp.int32, (x.shape[0], tokens), 0) == target_ref[...]).astype(
+        jnp.bfloat16
+    )
+    rows = lax.dot_general(
+        hot_t, x[:, :features], (((0,), (0,)), ((), ())), preferred_element_type=jnp.float32
+    )
+    rows_ref[...] = rows.astype(rows_ref.dtype)
+    loss = lax.dot_general(
+        x[:, features:], hot_t, (((0,), (0,)), ((), ())), preferred_element_type=jnp.float32
+    )
+    loss_ref[...] = loss[0:1, :].astype(loss_ref.dtype)
+
+
+def unplace(target_row, returned, features):
     groups, cap, width = returned.shape
-    tokens = target_place.shape[0]
+    tokens = target_row.shape[1]
     return pl.pallas_call(
         _unplace,
         grid=(1,),
         in_specs=[
-            pl.BlockSpec((tokens, 1), lambda i: (0, 0)),
+            pl.BlockSpec((1, tokens), lambda i: (0, 0)),
             pl.BlockSpec((groups, cap, width), lambda i: (0, 0, 0)),
         ],
         out_specs=[
             pl.BlockSpec((tokens, features), lambda i: (0, 0)),
-            pl.BlockSpec((tokens, width - features), lambda i: (0, 0)),
+            pl.BlockSpec((1, tokens), lambda i: (0, 0)),
         ],
         out_shape=[
             jax.ShapeDtypeStruct((tokens, features), returned.dtype),
-            jax.ShapeDtypeStruct((tokens, width - features), returned.dtype),
-        ],
-    )(target_place.reshape(tokens, 1), returned)
+            jax.ShapeDtypeStruct((1, tokens), returned.dtype),
+        ],
+    )(target_row, returned)
 
 
 def _middle(r_ref, cand_ref, back_ref, rows_ref, grads_ref):
@@ -109,14 +150,15 @@
     ).astype(jnp.int32)
     row_max = jnp.max(logits, axis=1, keepdims=True)
     shifted = logits - row_max
-    log_probs = shifted - jnp.log(jnp.sum(jnp.exp(shifted), axis=1, keepdims=True))
+    exps = jnp.exp(shifted)
+    total = jnp.sum(exps, axis=1, keepdims=True)
+    log_probs = shifted - jnp.log(total)
     onehot = (lax.broadcasted_iota(jnp.int32, logits.shape, 1) == targets).astype(jnp.float32)
     losses = -(1.0 - SMOOTH) * jnp.sum(onehot * log_probs, axis=1, keepdims=True) - (
         SMOOTH / columns
     ) * jnp.sum(log_probs, axis=1, keepdims=True)
-    grads = (
-        weights * (jnp.exp(log_probs) - (1.0 - SMOOTH) * onehot - SMOOTH / columns)
-    ).astype(jnp.bfloat16)
+    probs = exps * (1.0 / total)
+    grads = (weights * (probs - (1.0 - SMOOTH) * onehot - SMOOTH / columns)).astype(jnp.bfloat16)
     grads_ref[...] = grads
     row_grads = jnp.dot(grads, cand, preferred_element_type=jnp.float32).astype(jnp.bfloat16)
     extras = jnp.where(
@@ -160,20 +202,7 @@
     places = devices * CAP
     assert head_weight.shape[0] == SB * BLOCK
 
-    target_place = place_tokens(token_language, language_owner)
-    extra_cols = lax.broadcasted_iota(jnp.int32, (tokens, EXTRA), 1)
-    label_hi = (labels // LABEL_SPLIT).astype(jnp.bfloat16)
-    label_lo = (labels % LABEL_SPLIT).astype(jnp.bfloat16)
-    extras = jnp.where(
-        extra_cols == 0,
-        loss_weight[:, None],
-        jnp.where(
-            extra_cols == 1,
-            label_hi[:, None],
-            jnp.where(extra_cols == 2, label_lo[:, None], jnp.zeros((), jnp.bfloat16)),
-        ),
-    )
-    send = place(target_place, hidden, extras, devices)
+    send, target_row = place(token_language, language_owner, labels, loss_weight, hidden, devices)
     received = lax.all_to_all(send, AXES, split_axis=0, concat_axis=0, tiled=True)
 
     self_index = lax.axis_index(AXES)
@@ -201,8 +230,8 @@
         preferred_element_type=jnp.float32,
     ).astype(jnp.bfloat16)
 
-    hidden_grad, returned_extras = unplace(target_place, returned, features)
-    token_loss = returned_extras[:, 0]
+    hidden_grad, loss_row = unplace(target_row, returned, features)
+    token_loss = loss_row.reshape(tokens)
     return (hidden_grad, token_loss, head_grad)
 
 

time: 265 us -> 264 us (level)
  other arithmetic: 8.41 us -> 4.82 us
    reshape x0 -> x2, local copies, waits for them, and re-layouts: none -> 2.75 us  [the longest x1 1.47 us: place(): language_owner.reshape(languages, 1)]
where the time goes in v7:
time: 264 us
  waiting for transfers between devices  185 us (70%)
  Pallas kernels  27 us (10%)
  starting transfers between devices  24.2 us (9%)
  local copies, waits for them, and re-layouts  14 us (5%)
  matrix products  8.23 us (3%)
  other arithmetic  4.82 us (2%)
    all_to_all x1, waiting for transfers between devices, shards(): lax.all_to_all(send, AXES, split_axis=0, concat_axis=0, tiled=True)  97.7 us
    all_to_all x1, waiting for transfers between devices, shards(): lax.all_to_all(back, AXES, split_axis=0, concat_axis=0, tiled=True)  87 us
    all_to_all x1, starting transfers between devices, shards(): lax.all_to_all(send, AXES, split_axis=0, concat_axis=0, tiled=True)  16.5 us
    pallas_call x1, Pallas kernels, middle(): pl.pallas_call(_middle, grid=(groups // step,), in_specs=[pl.BlockSpec((s...  14.4 us
    dot_general x1, matrix products, shards(): lax.dot_general(expanded, token_rows[:, :features], (((0,), (0,)), ((), (...  8.23 us
    all_to_all x1, starting transfers between devices, shards(): lax.all_to_all(back, AXES, split_axis=0, concat_axis=0, tiled=True)  7.67 us
    pallas_call x1, Pallas kernels, place(): pl.pallas_call(_place, grid=(groups // step,), in_specs=[pl.BlockSpec((to...  6.53 us
    pallas_call x1, Pallas kernels, unplace(): pl.pallas_call(_unplace, grid=(1,), in_specs=[pl.BlockSpec((1, tokens), l...  6.04 us
  transfers between devices with their start and end apart: 2, of which 2 were waited for; matrix products, arithmetic and copies ran while one was open for 8% of the time, Pallas kernels for 0%

profile of v7, /device:TPU:1, one launch (start us, length us, event | category | flops | bytes accessed | tf_op | source)
XLA Modules:
  0.0 263.7 jit_solution(6979388883605073530)
XLA Ops:
  0.6 1.5 copy.20.lang_col_ref
  2.2 1.5 copy.21.owner_ref
  3.6 1.3 reshape.76.weights_ref
  4.9 6.5 %shard_map.94 = (bf16[256,4,2176]{2,1,0:T(4,128)(2,1)}, s32[1,512]{1,0:T(1,128)}) custom-call(s32[512,1]{1,0:T(8,128)} %copy.20.lang_col_ref, s32[1,512]{1,0:T(1,128)} %bitcast.30, s32[256,1]{1,0:T(8,128)} %copy.21.owner_ref, s32[1,512]{1,0:T(1,128)} %bitcast.32, bf16[1,512]{1,0:T(2,128)(2,1)} %reshape.76.weights_ref, bf16[512,2048]{1,0:T(8,128)(2,1)} %hidden_ref.1), custom_call_target="tpu_custom_call" | custom-call | tf_op jit(solution)/shard_map/pallas_call | solution.py:68
  11.4 16.5 %all-to-all-start = ((bf16[256,4,2176]{2,1,0:T(4,128)(2,1)}), bf16[256,4,2176]{2,1,0:T(4,128)(2,1)}, u32[]{:S(2)}, u32[]{:S(2)}) async-start(bf16[256,4,2176]{2,1,0:T(4,128)(2,1)} %get-tuple-element.11), calls=%async_computation | async-start | bytes 8912896 | tf_op jit(solution)/shard_map/all_to_all | solution.py:206
  28.0 0.1 multiply_reduce_fusion
  28.2 2.9 %gather_fusion = bf16[6,128,2048]{2,1,0:T(8,128)(2,1)S(1)} fusion(bf16[8,128,2048]{2,1,0:T(8,128)(2,1)} %bitcast.29, s32[1024]{0:T(1024)S(1)} %pad_clamp_fusion.1), kind=kCustom, calls=%fused_computation | custom fusion | bytes 6291480 | tf_op jit(solution)/shard_map/jit(_take)/gather | solution.py:212
  31.1 0.1 broadcast_bitcast_fusion.2
  31.2 2.2 bitcast_select_fusion.cand_ref
  33.4 97.7 %all-to-all-done.r_ref = bf16[256,4,2176]{2,1,0:T(4,128)(2,1)} async-done(((bf16[256,4,2176]{2,1,0:T(4,128)(2,1)}), bf16[256,4,2176]{2,1,0:T(4,128)(2,1)}, u32[]{:S(2)}, u32[]{:S(2)}) %all-to-all-start) | async-done | bytes 4456480 | tf_op jit(solution)/shard_map/all_to_all | solution.py:206
  131.1 14.4 %shard_map.95 = (bf16[256,4,2176]{2,1,0:T(4,128)(2,1)}, bf16[1024,2176]{1,0:T(8,128)(2,1)}, bf16[1024,768]{1,0:T(8,128)(2,1)}) custom-call(bf16[256,4,2176]{2,1,0:T(4,128)(2,1)} %all-to-all-done.r_ref, bf16[768,2048]{1,0:T(8,128)(2,1)} %bitcast_select_fusion.cand_ref), custom_call_target="tpu_custom_call" | custom-call | tf_op jit(solution)/shard_map/pallas_call | solution.py:177
  145.5 7.7 %all-to-all-start.1 = ((bf16[256,4,2176]{2,1,0:T(4,128)(2,1)}), bf16[256,4,2176]{2,1,0:T(4,128)(2,1)}, u32[]{:S(2)}, u32[]{:S(2)}) async-start(bf16[256,4,2176]{2,1,0:T(4,128)(2,1)} %get-tuple-element.12), calls=%async_computation.1 | async-start | bytes 8912896 | tf_op jit(solution)/shard_map/all_to_all | solution.py:215
  153.2 0.1 fusion.6
  153.3 0.1 select_reduce_fusion
  153.5 0.1 broadcast_bitcast_fusion
  153.5 0.8 copy.22
  154.3 0.9 copy.23
  155.2 2.1 gather_fusion.1
  157.3 2.9 %copy.24 = bf16[1024,8,128]{0,2,1:T(8,128)(2,1)S(1)} copy(bf16[1024,8,128]{2,0,1:T(8,128)(2,1)} %bitcast.27) | data formatting | bytes 4194304 | tf_op jit(solution)/shard_map/jit(_take)/gather | solution.py:225
  160.2 1.0 fusion.5
  161.2 8.2 %fusion.2 = bf16[1024,2048]{1,0:T(8,128)(2,1)} fusion(bf16[1024,1024]{0,1:T(8,128)(2,1)S(1)} %fusion.5, bf16[1024,2176]{1,0:T(8,128)(2,1)} %get-tuple-element.16), kind=kOutput, calls=%fused_computation.4 | convolution fusion | flops 4297064448 | bytes 10485760 | tf_op jit(solution)/shard_map/dot_general | solution.py:228
  169.4 87.0 %all-to-all-done.1.r_ref = bf16[256,4,2176]{2,1,0:T(4,128)(2,1)} async-done(((bf16[256,4,2176]{2,1,0:T(4,128)(2,1)}), bf16[256,4,2176]{2,1,0:T(4,128)(2,1)}, u32[]{:S(2)}, u32[]{:S(2)}) %all-to-all-start.1) | async-done | bytes 4456480 | tf_op jit(solution)/shard_map/all_to_all | solution.py:215
  256.4 6.0 %shard_map.96 = (bf16[512,2048]{1,0:T(8,128)(2,1)}, bf16[1,512]{1,0:T(2,128)(2,1)}) custom-call(s32[1,512]{1,0:T(1,128)} %get-tuple-element.10.target_ref, bf16[256,4,2176]{2,1,0:T(4,128)(2,1)} %all-to-all-done.1.r_ref), custom_call_target="tpu_custom_call" | custom-call | tf_op jit(solution)/shard_map/pallas_call | solution.py:118
  262.4 1.3 reduce
  (13 shorter events, 0.1 us)
Async XLA Ops:
  11.4 16.6 %copy-start.2 = (s32[256]{0:T(256)S(1)}, s32[256]{0:T(256)}, u32[]{:S(2)}) copy-start(s32[256]{0:T(256)} %param.10) | copy-start | bytes 3076
  11.4 16.6 %copy-start.1 = (s32[256,6]{0,1:T(8,128)S(1)}, s32[256,6]{0,1:T(8,128)}, u32[]{:S(2)}) copy-start(s32[256,6]{0,1:T(8,128)} %param.9) | copy-start | bytes 18436
  11.4 119.7 %all-to-all-start = ((bf16[256,4,2176]{2,1,0:T(4,128)(2,1)}), bf16[256,4,2176]{2,1,0:T(4,128)(2,1)}, u32[]{:S(2)}, u32[]{:S(2)}) async-start(bf16[256,4,2176]{2,1,0:T(4,128)(2,1)} %get-tuple-element.11), calls=%async_computation | async-start | bytes 8912896 | tf_op jit(solution)/shard_map/all_to_all | solution.py:206
  145.5 8.0 %copy-start = (bf16[1024,768]{1,0:T(8,128)(2,1)S(1)}, bf16[1024,768]{1,0:T(8,128)(2,1)}, u32[]{:S(2)}) copy-start(bf16[1024,768]{1,0:T(8,128)(2,1)} %get-tuple-element.15) | copy-start | bytes 4718596
  145.5 110.9 %all-to-all-start.1 = ((bf16[256,4,2176]{2,1,0:T(4,128)(2,1)}), bf16[256,4,2176]{2,1,0:T(4,128)(2,1)}, u32[]{:S(2)}, u32[]{:S(2)}) async-start(bf16[256,4,2176]{2,1,0:T(4,128)(2,1)} %get-tuple-element.12), calls=%async_computation.1 | async-start | bytes 8912896 | tf_op jit(solution)/shard_map/all_to_all | solution.py:215

commit v8 on v7

--- a/solution.py
+++ b/solution.py
@@ -17,29 +17,29 @@
 GROUPS_PER_STEP = 128
 
 
-def _place(lang_col_ref, lang_row_ref, owner_ref, labels_ref, weights_ref, hidden_ref, o_ref, target_ref):
+def _place(lang_ref, owner_ref, labels_ref, weights_ref, hidden_ref, o_ref, target_ref):
     tokens = hidden_ref.shape[0]
     languages = owner_ref.shape[0]
-    lang_row = lang_row_ref[...]
-    earlier = (lang_col_ref[...] == lang_row) & (
-        lax.broadcasted_iota(jnp.int32, (tokens, tokens), 0)
-        < lax.broadcasted_iota(jnp.int32, (tokens, tokens), 1)
-    )
-    rank = jnp.sum(earlier.astype(jnp.int32), axis=0, keepdims=True)
-    slot = jnp.sum(
-        jnp.where(
-            lax.broadcasted_iota(jnp.int32, (languages, tokens), 0) == lang_row, owner_ref[...], 0
-        ),
-        axis=0,
-        keepdims=True,
-    )
-    target = slot * CAP + rank
+    lang = lang_ref[...].reshape(1, tokens)
+    owner = owner_ref[...].reshape(1, languages)
+    is_lang = (lax.broadcasted_iota(jnp.int32, (languages, tokens), 0) == lang).astype(
+        jnp.bfloat16
+    )
+    same = lax.dot_general(
+        is_lang, is_lang, (((0,), (0,)), ((), ())), preferred_element_type=jnp.float32
+    )
+    before = lax.broadcasted_iota(jnp.int32, (tokens, tokens), 0) < lax.broadcasted_iota(
+        jnp.int32, (tokens, tokens), 1
+    )
+    rank = jnp.sum(jnp.where(before, same, 0.0), axis=0, keepdims=True)
+    slot = jnp.dot(owner.astype(jnp.bfloat16), is_lang, preferred_element_type=jnp.float32)
+    target = (slot * CAP + rank).astype(jnp.int32)
     target_ref[...] = target
-    labels = labels_ref[...]
+    labels = labels_ref[...].reshape(1, tokens)
     kind = lax.broadcasted_iota(jnp.int32, (EXTRA, tokens), 0)
     extras_t = jnp.where(
         kind == 0,
-        weights_ref[...].astype(jnp.float32),
+        weights_ref[...].reshape(1, tokens).astype(jnp.float32),
         jnp.where(
             kind == 1,
             (labels // LABEL_SPLIT).astype(jnp.float32),
@@ -64,34 +64,26 @@
     languages = language_owner.shape[0]
     width = features + EXTRA
     step = min(GROUPS_PER_STEP, groups)
-    whole = lambda i: (0, 0)
+    whole = lambda i: (0,)
     return pl.pallas_call(
         _place,
         grid=(groups // step,),
         in_specs=[
-            pl.BlockSpec((tokens, 1), whole),
-            pl.BlockSpec((1, tokens), whole),
-            pl.BlockSpec((languages, 1), whole),
-            pl.BlockSpec((1, tokens), whole),
-            pl.BlockSpec((1, tokens), whole),
-            pl.BlockSpec((tokens, features), whole),
+            pl.BlockSpec((tokens,), whole),
+            pl.BlockSpec((languages,), whole),
+            pl.BlockSpec((tokens,), whole),
+            pl.BlockSpec((tokens,), whole),
+            pl.BlockSpec((tokens, features), lambda i: (0, 0)),
         ],
         out_specs=[
             pl.BlockSpec((step, CAP, width), lambda i: (i, 0, 0)),
-            pl.BlockSpec((1, tokens), whole),
+            pl.BlockSpec((1, tokens), lambda i: (0, 0)),
         ],
         out_shape=[
             jax.ShapeDtypeStruct((groups, CAP, width), hidden.dtype),
             jax.ShapeDtypeStruct((1, tokens), jnp.int32),
         ],
-    )(
-        token_language,
-        token_language.reshape(1, tokens),
-        language_owner.reshape(languages, 1),
-        labels.reshape(1, tokens),
-        loss_weight.reshape(1, tokens),
-        hidden,
-    )
+    )(token_language.reshape(tokens), language_owner, labels, loss_weight, hidden)
 
 
 def _unplace(target_ref, r_ref, rows_ref, loss_ref):
@@ -109,7 +101,7 @@
     loss = lax.dot_general(
         x[:, features:], hot_t, (((0,), (0,)), ((), ())), preferred_element_type=jnp.float32
     )
-    loss_ref[...] = loss[0:1, :].astype(loss_ref.dtype)
+    loss_ref[...] = loss[0:1, :].astype(loss_ref.dtype).reshape(loss_ref.shape)
 
 
 def unplace(target_row, returned, features):
@@ -124,11 +116,11 @@
         ],
         out_specs=[
             pl.BlockSpec((tokens, features), lambda i: (0, 0)),
-            pl.BlockSpec((1, tokens), lambda i: (0, 0)),
+            pl.BlockSpec((tokens,), lambda i: (0,)),
         ],
         out_shape=[
             jax.ShapeDtypeStruct((tokens, features), returned.dtype),
-            jax.ShapeDtypeStruct((1, tokens), returned.dtype),
+            jax.ShapeDtypeStruct((tokens,), returned.dtype),
         ],
     )(target_row, returned)
 
@@ -230,8 +222,7 @@
         preferred_element_type=jnp.float32,
     ).astype(jnp.bfloat16)
 
-    hidden_grad, loss_row = unplace(target_row, returned, features)
-    token_loss = loss_row.reshape(tokens)
+    hidden_grad, token_loss = unplace(target_row, returned, features)
     return (hidden_grad, token_loss, head_grad)
 
 

time: 264 us -> 259 us (0.981)
  local copies, waits for them, and re-layouts: 14 us -> 9.74 us
    reshape x2 -> x0, local copies, waits for them, and re-layouts: 2.75 us -> none  [the longest x1 1.47 us: place(): language_owner.reshape(languages, 1)]
where the time goes in v8:
time: 259 us; the launch traced here: 258 us
  waiting for transfers between devices  185 us (71%)
  Pallas kernels  27.3 us (11%)
  starting transfers between devices  24.2 us (9%)
  local copies, waits for them, and re-layouts  9.74 us (4%)
  matrix products  8.23 us (3%)
  other arithmetic  3.57 us (1%)
    all_to_all x1, waiting for transfers between devices, shards(): lax.all_to_all(send, AXES, split_axis=0, concat_axis=0, tiled=True)  97.7 us
    all_to_all x1, waiting for transfers between devices, shards(): lax.all_to_all(back, AXES, split_axis=0, concat_axis=0, tiled=True)  87 us
    all_to_all x1, starting transfers between devices, shards(): lax.all_to_all(send, AXES, split_axis=0, concat_axis=0, tiled=True)  16.5 us
    pallas_call x1, Pallas kernels, middle(): pl.pallas_call(_middle, grid=(groups // step,), in_specs=[pl.BlockSpec((s...  14.4 us
    dot_general x1, matrix products, shards(): lax.dot_general(expanded, token_rows[:, :features], (((0,), (0,)), ((), (...  8.23 us
    all_to_all x1, starting transfers between devices, shards(): lax.all_to_all(back, AXES, split_axis=0, concat_axis=0, tiled=True)  7.67 us
    pallas_call x1, Pallas kernels, place(): pl.pallas_call(_place, grid=(groups // step,), in_specs=[pl.BlockSpec((to...  6.81 us
    pallas_call x1, Pallas kernels, unplace(): pl.pallas_call(_unplace, grid=(1,), in_specs=[pl.BlockSpec((1, tokens), l...  6.04 us
  transfers between devices with their start and end apart: 2, of which 2 were waited for; matrix products, arithmetic and copies ran while one was open for 8% of the time, Pallas kernels for 0%

profile of v8, /device:TPU:1, one launch (start us, length us, event | category | flops | bytes accessed | tf_op | source)
XLA Modules:
  0.0 258.4 jit_solution(17418054221923072931)
XLA Ops:
  0.6 6.8 %shard_map.94 = (bf16[256,4,2176]{2,1,0:T(4,128)(2,1)}, s32[1,512]{1,0:T(1,128)}) custom-call(s32[512]{0:T(512)} %bitcast.28, s32[256]{0:T(256)} %owner_ref.1, s32[512]{0:T(512)} %labels_ref.1, bf16[512]{0:T(512)(128)(2,1)} %weights_ref.1, bf16[512,2048]{1,0:T(8,128)(2,1)} %hidden_ref.1), custom_call_target="tpu_custom_call" | custom-call | tf_op jit(solution)/shard_map/pallas_call | solution.py:68
  7.4 0.0 copy-start.2
  7.4 16.5 %all-to-all-start = ((bf16[256,4,2176]{2,1,0:T(4,128)(2,1)}), bf16[256,4,2176]{2,1,0:T(4,128)(2,1)}, u32[]{:S(2)}, u32[]{:S(2)}) async-start(bf16[256,4,2176]{2,1,0:T(4,128)(2,1)} %get-tuple-element.11), calls=%async_computation | async-start | bytes 8912896 | tf_op jit(solution)/shard_map/all_to_all | solution.py:198
  24.0 0.0 copy-done.2
  24.0 0.0 copy-done.1
  24.0 0.1 multiply_reduce_fusion
  24.2 2.9 %gather_fusion = bf16[6,128,2048]{2,1,0:T(8,128)(2,1)S(1)} fusion(bf16[8,128,2048]{2,1,0:T(8,128)(2,1)} %bitcast.27, s32[1024]{0:T(1024)S(1)} %pad_clamp_fusion.1), kind=kCustom, calls=%fused_computation | custom fusion | bytes 6291480 | tf_op jit(solution)/shard_map/jit(_take)/gather | solution.py:204
  27.1 0.1 broadcast_bitcast_fusion.2
  27.2 2.2 bitcast_select_fusion.cand_ref
  29.4 97.7 %all-to-all-done.r_ref = bf16[256,4,2176]{2,1,0:T(4,128)(2,1)} async-done(((bf16[256,4,2176]{2,1,0:T(4,128)(2,1)}), bf16[256,4,2176]{2,1,0:T(4,128)(2,1)}, u32[]{:S(2)}, u32[]{:S(2)}) %all-to-all-start) | async-done | bytes 4456480 | tf_op jit(solution)/shard_map/all_to_all | solution.py:198
  127.1 14.4 %shard_map.95 = (bf16[256,4,2176]{2,1,0:T(4,128)(2,1)}, bf16[1024,2176]{1,0:T(8,128)(2,1)}, bf16[1024,768]{1,0:T(8,128)(2,1)}) custom-call(bf16[256,4,2176]{2,1,0:T(4,128)(2,1)} %all-to-all-done.r_ref, bf16[768,2048]{1,0:T(8,128)(2,1)} %bitcast_select_fusion.cand_ref), custom_call_target="tpu_custom_call" | custom-call | tf_op jit(solution)/shard_map/pallas_call | solution.py:169
  141.5 7.7 %all-to-all-start.1 = ((bf16[256,4,2176]{2,1,0:T(4,128)(2,1)}), bf16[256,4,2176]{2,1,0:T(4,128)(2,1)}, u32[]{:S(2)}, u32[]{:S(2)}) async-start(bf16[256,4,2176]{2,1,0:T(4,128)(2,1)} %get-tuple-element.12), calls=%async_computation.1 | async-start | bytes 8912896 | tf_op jit(solution)/shard_map/all_to_all | solution.py:207
  149.2 0.1 fusion.6
  149.3 0.1 select_reduce_fusion
  149.5 0.1 broadcast_bitcast_fusion
  149.5 0.0 copy-done
  149.5 0.8 copy.15
  150.3 0.9 copy.16
  151.2 2.1 gather_fusion.1
  153.4 2.9 %copy.17 = bf16[1024,8,128]{0,2,1:T(8,128)(2,1)S(1)} copy(bf16[1024,8,128]{2,0,1:T(8,128)(2,1)} %bitcast.25) | data formatting | bytes 4194304 | tf_op jit(solution)/shard_map/jit(_take)/gather | solution.py:217
  156.2 1.0 fusion.5
  157.2 8.2 %fusion.2 = bf16[1024,2048]{1,0:T(8,128)(2,1)} fusion(bf16[1024,1024]{0,1:T(8,128)(2,1)S(1)} %fusion.5, bf16[1024,2176]{1,0:T(8,128)(2,1)} %get-tuple-element.16), kind=kOutput, calls=%fused_computation.4 | convolution fusion | flops 4297064448 | bytes 10485760 | tf_op jit(solution)/shard_map/dot_general | solution.py:220
  165.4 87.0 %all-to-all-done.1.r_ref = bf16[256,4,2176]{2,1,0:T(4,128)(2,1)} async-done(((bf16[256,4,2176]{2,1,0:T(4,128)(2,1)}), bf16[256,4,2176]{2,1,0:T(4,128)(2,1)}, u32[]{:S(2)}, u32[]{:S(2)}) %all-to-all-start.1) | async-done | bytes 4456480 | tf_op jit(solution)/shard_map/all_to_all | solution.py:207
  252.4 6.0 %shard_map.96 = (bf16[512,2048]{1,0:T(8,128)(2,1)}, bf16[512]{0:T(512)(128)(2,1)}) custom-call(s32[1,512]{1,0:T(1,128)} %get-tuple-element.10.target_ref, bf16[256,4,2176]{2,1,0:T(4,128)(2,1)} %all-to-all-done.1.r_ref), custom_call_target="tpu_custom_call" | custom-call | tf_op jit(solution)/shard_map/pallas_call | solution.py:110
  (9 shorter events, 0.1 us)
Async XLA Ops:
  7.4 16.6 %copy-start.2 = (s32[256]{0:T(256)S(1)}, s32[256]{0:T(256)}, u32[]{:S(2)}) copy-start(s32[256]{0:T(256)} %owner_ref.1) | copy-start | bytes 3076
  7.4 16.6 %copy-start.1 = (s32[256,6]{0,1:T(8,128)S(1)}, s32[256,6]{0,1:T(8,128)}, u32[]{:S(2)}) copy-start(s32[256,6]{0,1:T(8,128)} %param.9) | copy-start | bytes 18436
  7.4 119.7 %all-to-all-start = ((bf16[256,4,2176]{2,1,0:T(4,128)(2,1)}), bf16[256,4,2176]{2,1,0:T(4,128)(2,1)}, u32[]{:S(2)}, u32[]{:S(2)}) async-start(bf16[256,4,2176]{2,1,0:T(4,128)(2,1)} %get-tuple-element.11), calls=%async_computation | async-start | bytes 8912896 | tf_op jit(solution)/shard_map/all_to_all | solution.py:198
  141.5 8.0 %copy-start = (bf16[1024,768]{1,0:T(8,128)(2,1)S(1)}, bf16[1024,768]{1,0:T(8,128)(2,1)}, u32[]{:S(2)}) copy-start(bf16[1024,768]{1,0:T(8,128)(2,1)} %get-tuple-element.15) | copy-start | bytes 4718596
  141.5 110.9 %all-to-all-start.1 = ((bf16[256,4,2176]{2,1,0:T(4,128)(2,1)}), bf16[256,4,2176]{2,1,0:T(4,128)(2,1)}, u32[]{:S(2)}, u32[]{:S(2)}) async-start(bf16[256,4,2176]{2,1,0:T(4,128)(2,1)} %get-tuple-element.12), calls=%async_computation.1 | async-start | bytes 8912896 | tf_op jit(solution)/shard_map/all_to_all | solution.py:207

commit v9 on v8

--- a/solution.py
+++ b/solution.py
@@ -125,10 +125,9 @@
     )(target_row, returned)
 
 
-def _middle(r_ref, cand_ref, back_ref, rows_ref, grads_ref):
+def _middle(r_ref, cand_ref, back_ref, grads_ref):
     x = r_ref[...]
     x = x.reshape(x.shape[0] * x.shape[1], x.shape[2])
-    rows_ref[...] = x
     n, width = x.shape
     cand = cand_ref[...]
     columns, features = cand.shape
@@ -175,12 +174,10 @@
         ],
         out_specs=[
             pl.BlockSpec((step, cap, width), lambda i: (i, 0, 0)),
-            pl.BlockSpec((step * cap, width), lambda i: (i, 0)),
             pl.BlockSpec((step * cap, columns), lambda i: (i, 0)),
         ],
         out_shape=[
             jax.ShapeDtypeStruct((groups, cap, width), received.dtype),
-            jax.ShapeDtypeStruct((groups * cap, width), received.dtype),
             jax.ShapeDtypeStruct((groups * cap, columns), jnp.bfloat16),
         ],
     )(received, candidates)
@@ -203,8 +200,10 @@
     slab = head_weight.reshape(SB, BLOCK, features)
     candidates = jnp.take(slab, blocks, axis=0).reshape(LB * BLOCK, features)
 
-    back, token_rows, grads = middle(received, candidates)
+    back, grads = middle(received, candidates)
     returned = lax.all_to_all(back, AXES, split_axis=0, concat_axis=0, tiled=True)
+    received, grads = lax.optimization_barrier((received, grads))
+    token_rows = received.reshape(places, received.shape[2])
 
     block_hot = blocks[None, :] == jnp.arange(SB, dtype=jnp.int32)[:, None]
     listed = jnp.any(block_hot, axis=1)

time: 259 us -> 259 us (level)
  local copies, waits for them, and re-layouts: 9.74 us -> 16.8 us
  waiting for transfers between devices: 185 us -> 178 us
    reshape x0 -> x1, local copies, waits for them, and re-layouts: none -> 7.06 us  [shards(): token_rows = received.reshape(places, received.shape[2])]
    all_to_all x1, waiting for transfers between devices: 87 us -> 79.9 us  [shards(): lax.all_to_all(back, AXES, split_axis=0, concat_axis=0, tiled=True)]
  transfers between devices with their start and end apart: 2 -> 2, of which waited for: 2 -> 2; matrix products, arithmetic and copies ran while one was open for 8% -> 11% of each run, Pallas kernels for 0% -> 0%
where the time goes in v9:
time: 259 us; the launch traced here: 258 us
  waiting for transfers between devices  178 us (69%)
  Pallas kernels  27.2 us (11%)
  starting transfers between devices  24.2 us (9%)
  local copies, waits for them, and re-layouts  16.8 us (6%)
  matrix products  8.23 us (3%)
  other arithmetic  3.55 us (1%)
    all_to_all x1, waiting for transfers between devices, shards(): lax.all_to_all(send, AXES, split_axis=0, concat_axis=0, tiled=True)  97.7 us
    all_to_all x1, waiting for transfers between devices, shards(): lax.all_to_all(back, AXES, split_axis=0, concat_axis=0, tiled=True)  79.9 us
    all_to_all x1, starting transfers between devices, shards(): lax.all_to_all(send, AXES, split_axis=0, concat_axis=0, tiled=True)  16.5 us
    pallas_call x1, Pallas kernels, middle(): pl.pallas_call(_middle, grid=(groups // step,), in_specs=[pl.BlockSpec((s...  14.4 us
    dot_general x1, matrix products, shards(): lax.dot_general(expanded, token_rows[:, :features], (((0,), (0,)), ((), (...  8.23 us
    all_to_all x1, starting transfers between devices, shards(): lax.all_to_all(back, AXES, split_axis=0, concat_axis=0, tiled=True)  7.67 us
    reshape x1, local copies, waits for them, and re-layouts, shards(): token_rows = received.reshape(places, received.shape[2])  7.06 us
    pallas_call x1, Pallas kernels, place(): pl.pallas_call(_place, grid=(groups // step,), in_specs=[pl.BlockSpec((to...  6.74 us
  transfers between devices with their start and end apart: 2, of which 2 were waited for; matrix products, arithmetic and copies ran while one was open for 11% of the time, Pallas kernels for 0%

profile of v9, /device:TPU:1, one launch (start us, length us, event | category | flops | bytes accessed | tf_op | source)
XLA Modules:
  0.0 258.4 jit_solution(11246137788490522019)
XLA Ops:
  0.6 6.7 %shard_map.94 = (bf16[256,4,2176]{2,1,0:T(4,128)(2,1)}, s32[1,512]{1,0:T(1,128)}) custom-call(s32[512]{0:T(512)} %bitcast.28, s32[256]{0:T(256)} %owner_ref.1, s32[512]{0:T(512)} %labels_ref.1, bf16[512]{0:T(512)(128)(2,1)} %weights_ref.1, bf16[512,2048]{1,0:T(8,128)(2,1)} %hidden_ref.1), custom_call_target="tpu_custom_call" | custom-call | tf_op jit(solution)/shard_map/pallas_call | solution.py:68
  7.4 16.5 %all-to-all-start = ((bf16[256,4,2176]{2,1,0:T(4,128)(2,1)}), bf16[256,4,2176]{2,1,0:T(4,128)(2,1)}, u32[]{:S(2)}, u32[]{:S(2)}) async-start(bf16[256,4,2176]{2,1,0:T(4,128)(2,1)} %get-tuple-element.12), calls=%async_computation | async-start | bytes 8912896 | tf_op jit(solution)/shard_map/all_to_all | solution.py:195
  23.9 0.0 copy-done.2
  23.9 0.0 copy-done.1
  24.0 0.1 multiply_reduce_fusion
  24.1 2.9 %gather_fusion = bf16[6,128,2048]{2,1,0:T(8,128)(2,1)S(1)} fusion(bf16[8,128,2048]{2,1,0:T(8,128)(2,1)} %bitcast.27, s32[1024]{0:T(1024)S(1)} %pad_clamp_fusion.1), kind=kCustom, calls=%fused_computation | custom fusion | bytes 6291480 | tf_op jit(solution)/shard_map/jit(_take)/gather | solution.py:201
  27.1 0.1 broadcast_bitcast_fusion.2
  27.1 2.2 bitcast_select_fusion.cand_ref
  29.3 97.7 %all-to-all-done.r_ref = bf16[256,4,2176]{2,1,0:T(4,128)(2,1)} async-done(((bf16[256,4,2176]{2,1,0:T(4,128)(2,1)}), bf16[256,4,2176]{2,1,0:T(4,128)(2,1)}, u32[]{:S(2)}, u32[]{:S(2)}) %all-to-all-start) | async-done | bytes 4456480 | tf_op jit(solution)/shard_map/all_to_all | solution.py:195
  127.0 14.4 %shard_map.95 = (bf16[256,4,2176]{2,1,0:T(4,128)(2,1)}, bf16[1024,768]{1,0:T(8,128)(2,1)}) custom-call(bf16[256,4,2176]{2,1,0:T(4,128)(2,1)} %all-to-all-done.r_ref, bf16[768,2048]{1,0:T(8,128)(2,1)} %bitcast_select_fusion.cand_ref), custom_call_target="tpu_custom_call" | custom-call | tf_op jit(solution)/shard_map/pallas_call | solution.py:168
  141.5 7.7 %all-to-all-start.1 = ((bf16[256,4,2176]{2,1,0:T(4,128)(2,1)}), bf16[256,4,2176]{2,1,0:T(4,128)(2,1)}, u32[]{:S(2)}, u32[]{:S(2)}) async-start(bf16[256,4,2176]{2,1,0:T(4,128)(2,1)} %get-tuple-element.13), calls=%async_computation.1 | async-start | bytes 8912896 | tf_op jit(solution)/shard_map/all_to_all | solution.py:204
  149.2 0.1 fusion.6
  149.3 0.1 select_reduce_fusion
  149.4 0.1 broadcast_bitcast_fusion
  149.5 0.0 copy-done
  149.5 0.8 copy.15
  150.3 0.9 copy.16
  151.2 2.1 gather_fusion.1
  153.3 2.9 %copy.17 = bf16[1024,8,128]{0,2,1:T(8,128)(2,1)S(1)} copy(bf16[1024,8,128]{2,0,1:T(8,128)(2,1)} %bitcast.25) | data formatting | bytes 4194304 | tf_op jit(solution)/shard_map/jit(_take)/gather | solution.py:216
  156.2 7.1 %reshape.67 = bf16[1024,2176]{1,0:T(8,128)(2,1)} reshape(bf16[256,4,2176]{2,1,0:T(4,128)(2,1)} %all-to-all-done.r_ref) | data formatting | bytes 8912896 | tf_op jit(solution)/shard_map/reshape | solution.py:206
  163.2 1.0 fusion.5
  164.2 8.2 %fusion.2 = bf16[1024,2048]{1,0:T(8,128)(2,1)} fusion(bf16[1024,1024]{0,1:T(8,128)(2,1)S(1)} %fusion.5, bf16[1024,2176]{1,0:T(8,128)(2,1)} %reshape.67), kind=kOutput, calls=%fused_computation.4 | convolution fusion | flops 4297064448 | bytes 10485760 | tf_op jit(solution)/shard_map/dot_general | solution.py:219
  172.4 79.9 %all-to-all-done.1.r_ref = bf16[256,4,2176]{2,1,0:T(4,128)(2,1)} async-done(((bf16[256,4,2176]{2,1,0:T(4,128)(2,1)}), bf16[256,4,2176]{2,1,0:T(4,128)(2,1)}, u32[]{:S(2)}, u32[]{:S(2)}) %all-to-all-start.1) | async-done | bytes 4456480 | tf_op jit(solution)/shard_map/all_to_all | solution.py:204
  252.4 6.0 %shard_map.96 = (bf16[512,2048]{1,0:T(8,128)(2,1)}, bf16[512]{0:T(512)(128)(2,1)}) custom-call(s32[1,512]{1,0:T(1,128)} %get-tuple-element.11.target_ref, bf16[256,4,2176]{2,1,0:T(4,128)(2,1)} %all-to-all-done.1.r_ref), custom_call_target="tpu_custom_call" | custom-call | tf_op jit(solution)/shard_map/pallas_call | solution.py:110
  (10 shorter events, 0.1 us)
Async XLA Ops:
  7.4 16.6 %copy-start.2 = (s32[256]{0:T(256)S(1)}, s32[256]{0:T(256)}, u32[]{:S(2)}) copy-start(s32[256]{0:T(256)} %owner_ref.1) | copy-start | bytes 3076
  7.4 16.6 %copy-start.1 = (s32[256,6]{0,1:T(8,128)S(1)}, s32[256,6]{0,1:T(8,128)}, u32[]{:S(2)}) copy-start(s32[256,6]{0,1:T(8,128)} %param.9) | copy-start | bytes 18436
  7.4 119.7 %all-to-all-start = ((bf16[256,4,2176]{2,1,0:T(4,128)(2,1)}), bf16[256,4,2176]{2,1,0:T(4,128)(2,1)}, u32[]{:S(2)}, u32[]{:S(2)}) async-start(bf16[256,4,2176]{2,1,0:T(4,128)(2,1)} %get-tuple-element.12), calls=%async_computation | async-start | bytes 8912896 | tf_op jit(solution)/shard_map/all_to_all | solution.py:195
  141.5 8.0 %copy-start = (bf16[1024,768]{1,0:T(8,128)(2,1)S(1)}, bf16[1024,768]{1,0:T(8,128)(2,1)}, u32[]{:S(2)}) copy-start(bf16[1024,768]{1,0:T(8,128)(2,1)} %get-tuple-element.17) | copy-start | bytes 4718596
  141.5 110.9 %all-to-all-start.1 = ((bf16[256,4,2176]{2,1,0:T(4,128)(2,1)}), bf16[256,4,2176]{2,1,0:T(4,128)(2,1)}, u32[]{:S(2)}, u32[]{:S(2)}) async-start(bf16[256,4,2176]{2,1,0:T(4,128)(2,1)} %get-tuple-element.13), calls=%async_computation.1 | async-start | bytes 8912896 | tf_op jit(solution)/shard_map/all_to_all | solution.py:204

commit v10 on v8

--- a/solution.py
+++ b/solution.py
@@ -2,6 +2,7 @@
 import jax.numpy as jnp
 from jax import lax
 from jax.experimental import pallas as pl
+from jax.experimental.pallas import tpu as pltpu
 from jax.sharding import PartitionSpec as P
 
 D = 2048
@@ -17,43 +18,46 @@
 GROUPS_PER_STEP = 128
 
 
-def _place(lang_ref, owner_ref, labels_ref, weights_ref, hidden_ref, o_ref, target_ref):
+def _place(lang_ref, owner_ref, labels_ref, weights_ref, hidden_ref, o_ref, target_ref, extras_ref):
     tokens = hidden_ref.shape[0]
     languages = owner_ref.shape[0]
-    lang = lang_ref[...].reshape(1, tokens)
-    owner = owner_ref[...].reshape(1, languages)
-    is_lang = (lax.broadcasted_iota(jnp.int32, (languages, tokens), 0) == lang).astype(
-        jnp.bfloat16
-    )
-    same = lax.dot_general(
-        is_lang, is_lang, (((0,), (0,)), ((), ())), preferred_element_type=jnp.float32
-    )
-    before = lax.broadcasted_iota(jnp.int32, (tokens, tokens), 0) < lax.broadcasted_iota(
-        jnp.int32, (tokens, tokens), 1
-    )
-    rank = jnp.sum(jnp.where(before, same, 0.0), axis=0, keepdims=True)
-    slot = jnp.dot(owner.astype(jnp.bfloat16), is_lang, preferred_element_type=jnp.float32)
-    target = (slot * CAP + rank).astype(jnp.int32)
-    target_ref[...] = target
-    labels = labels_ref[...].reshape(1, tokens)
-    kind = lax.broadcasted_iota(jnp.int32, (EXTRA, tokens), 0)
-    extras_t = jnp.where(
-        kind == 0,
-        weights_ref[...].reshape(1, tokens).astype(jnp.float32),
-        jnp.where(
-            kind == 1,
-            (labels // LABEL_SPLIT).astype(jnp.float32),
-            jnp.where(kind == 2, (labels % LABEL_SPLIT).astype(jnp.float32), 0.0),
-        ),
-    ).astype(jnp.bfloat16)
+
+    @pl.when(pl.program_id(0) == 0)
+    def _():
+        lang = lang_ref[...].reshape(1, tokens)
+        owner = owner_ref[...].reshape(1, languages)
+        is_lang = (lax.broadcasted_iota(jnp.int32, (languages, tokens), 0) == lang).astype(
+            jnp.bfloat16
+        )
+        same = lax.dot_general(
+            is_lang, is_lang, (((0,), (0,)), ((), ())), preferred_element_type=jnp.float32
+        )
+        before = lax.broadcasted_iota(jnp.int32, (tokens, tokens), 0) < lax.broadcasted_iota(
+            jnp.int32, (tokens, tokens), 1
+        )
+        rank = jnp.sum(jnp.where(before, same, 0.0), axis=0, keepdims=True)
+        slot = jnp.dot(owner.astype(jnp.bfloat16), is_lang, preferred_element_type=jnp.float32)
+        target_ref[...] = (slot * CAP + rank).astype(jnp.int32)
+        labels = labels_ref[...].reshape(1, tokens)
+        kind = lax.broadcasted_iota(jnp.int32, (EXTRA, tokens), 0)
+        extras_ref[...] = jnp.where(
+            kind == 0,
+            weights_ref[...].reshape(1, tokens).astype(jnp.float32),
+            jnp.where(
+                kind == 1,
+                (labels // LABEL_SPLIT).astype(jnp.float32),
+                jnp.where(kind == 2, (labels % LABEL_SPLIT).astype(jnp.float32), 0.0),
+            ),
+        ).astype(jnp.bfloat16)
+
     step_rows = o_ref.shape[0] * o_ref.shape[1]
     first = pl.program_id(0) * step_rows
-    hot = (lax.broadcasted_iota(jnp.int32, (step_rows, tokens), 0) + first == target).astype(
-        jnp.bfloat16
-    )
+    hot = (
+        lax.broadcasted_iota(jnp.int32, (step_rows, tokens), 0) + first == target_ref[...]
+    ).astype(jnp.bfloat16)
     rows = jnp.dot(hot, hidden_ref[...], preferred_element_type=jnp.float32)
     extra = lax.dot_general(
-        hot, extras_t, (((1,), (1,)), ((), ())), preferred_element_type=jnp.float32
+        hot, extras_ref[...], (((1,), (1,)), ((), ())), preferred_element_type=jnp.float32
     )
     out = jnp.concatenate([rows.astype(jnp.bfloat16), extra.astype(jnp.bfloat16)], axis=1)
     o_ref[...] = out.reshape(o_ref.shape)
@@ -83,6 +87,7 @@
             jax.ShapeDtypeStruct((groups, CAP, width), hidden.dtype),
             jax.ShapeDtypeStruct((1, tokens), jnp.int32),
         ],
+        scratch_shapes=[pltpu.VMEM((EXTRA, tokens), jnp.bfloat16)],
     )(token_language.reshape(tokens), language_owner, labels, loss_weight, hidden)
 
 

time: 259 us -> 258 us (level)
  no operation moved by 1% of the time
where the time goes in v10:
time: 258 us
  waiting for transfers between devices  185 us (72%)
  Pallas kernels  26.8 us (10%)
  starting transfers between devices  24.2 us (9%)
  local copies, waits for them, and re-layouts  9.74 us (4%)
  matrix products  8.23 us (3%)
  other arithmetic  3.57 us (1%)
    all_to_all x1, waiting for transfers between devices, shards(): lax.all_to_all(send, AXES, split_axis=0, concat_axis=0, tiled=True)  97.7 us
    all_to_all x1, waiting for transfers between devices, shards(): lax.all_to_all(back, AXES, split_axis=0, concat_axis=0, tiled=True)  87 us
    all_to_all x1, starting transfers between devices, shards(): lax.all_to_all(send, AXES, split_axis=0, concat_axis=0, tiled=True)  16.5 us
    pallas_call x1, Pallas kernels, middle(): pl.pallas_call(_middle, grid=(groups // step,), in_specs=[pl.BlockSpec((s...  14.4 us
    dot_general x1, matrix products, shards(): lax.dot_general(expanded, token_rows[:, :features], (((0,), (0,)), ((), (...  8.23 us
    all_to_all x1, starting transfers between devices, shards(): lax.all_to_all(back, AXES, split_axis=0, concat_axis=0, tiled=True)  7.67 us
    pallas_call x1, Pallas kernels, place(): pl.pallas_call(_place, grid=(groups // step,), in_specs=[pl.BlockSpec((to...  6.35 us
    pallas_call x1, Pallas kernels, unplace(): pl.pallas_call(_unplace, grid=(1,), in_specs=[pl.BlockSpec((1, tokens), l...  6.04 us
  transfers between devices with their start and end apart: 2, of which 2 were waited for; matrix products, arithmetic and copies ran while one was open for 8% of the time, Pallas kernels for 0%

profile of v10, /device:TPU:1, one launch (start us, length us, event | category | flops | bytes accessed | tf_op | source)
XLA Modules:
  0.0 258.0 jit_solution(831109677976091047)
XLA Ops:
  0.6 6.3 %shard_map.94 = (bf16[256,4,2176]{2,1,0:T(4,128)(2,1)}, s32[1,512]{1,0:T(1,128)}) custom-call(s32[512]{0:T(512)} %bitcast.28, s32[256]{0:T(256)} %owner_ref.1, s32[512]{0:T(512)} %labels_ref.1, bf16[512]{0:T(512)(128)(2,1)} %weights_ref.1, bf16[512,2048]{1,0:T(8,128)(2,1)} %hidden_ref.1), custom_call_target="tpu_custom_call" | custom-call | tf_op jit(solution)/shard_map/pallas_call | solution.py:72
  7.0 0.0 copy-start.1
  7.0 16.5 %all-to-all-start = ((bf16[256,4,2176]{2,1,0:T(4,128)(2,1)}), bf16[256,4,2176]{2,1,0:T(4,128)(2,1)}, u32[]{:S(2)}, u32[]{:S(2)}) async-start(bf16[256,4,2176]{2,1,0:T(4,128)(2,1)} %get-tuple-element.11), calls=%async_computation | async-start | bytes 8912896 | tf_op jit(solution)/shard_map/all_to_all | solution.py:203
  23.5 0.0 copy-done.2
  23.6 0.0 copy-done.1
  23.6 0.1 multiply_reduce_fusion
  23.7 2.9 %gather_fusion = bf16[6,128,2048]{2,1,0:T(8,128)(2,1)S(1)} fusion(bf16[8,128,2048]{2,1,0:T(8,128)(2,1)} %bitcast.27, s32[1024]{0:T(1024)S(1)} %pad_clamp_fusion.1), kind=kCustom, calls=%fused_computation | custom fusion | bytes 6291480 | tf_op jit(solution)/shard_map/jit(_take)/gather | solution.py:209
  26.7 0.1 broadcast_bitcast_fusion.2
  26.7 2.2 bitcast_select_fusion.cand_ref
  28.9 97.7 %all-to-all-done.r_ref = bf16[256,4,2176]{2,1,0:T(4,128)(2,1)} async-done(((bf16[256,4,2176]{2,1,0:T(4,128)(2,1)}), bf16[256,4,2176]{2,1,0:T(4,128)(2,1)}, u32[]{:S(2)}, u32[]{:S(2)}) %all-to-all-start) | async-done | bytes 4456480 | tf_op jit(solution)/shard_map/all_to_all | solution.py:203
  126.6 14.4 %shard_map.95 = (bf16[256,4,2176]{2,1,0:T(4,128)(2,1)}, bf16[1024,2176]{1,0:T(8,128)(2,1)}, bf16[1024,768]{1,0:T(8,128)(2,1)}) custom-call(bf16[256,4,2176]{2,1,0:T(4,128)(2,1)} %all-to-all-done.r_ref, bf16[768,2048]{1,0:T(8,128)(2,1)} %bitcast_select_fusion.cand_ref), custom_call_target="tpu_custom_call" | custom-call | tf_op jit(solution)/shard_map/pallas_call | solution.py:174
  141.1 7.7 %all-to-all-start.1 = ((bf16[256,4,2176]{2,1,0:T(4,128)(2,1)}), bf16[256,4,2176]{2,1,0:T(4,128)(2,1)}, u32[]{:S(2)}, u32[]{:S(2)}) async-start(bf16[256,4,2176]{2,1,0:T(4,128)(2,1)} %get-tuple-element.12), calls=%async_computation.1 | async-start | bytes 8912896 | tf_op jit(solution)/shard_map/all_to_all | solution.py:212
  148.7 0.1 fusion.6
  148.9 0.1 select_reduce_fusion
  149.0 0.1 broadcast_bitcast_fusion
  149.1 0.0 copy-done
  149.1 0.8 copy.15
  149.9 0.9 copy.16
  150.8 2.1 gather_fusion.1
  152.9 2.9 %copy.17 = bf16[1024,8,128]{0,2,1:T(8,128)(2,1)S(1)} copy(bf16[1024,8,128]{2,0,1:T(8,128)(2,1)} %bitcast.25) | data formatting | bytes 4194304 | tf_op jit(solution)/shard_map/jit(_take)/gather | solution.py:222
  155.8 1.0 fusion.5
  156.7 8.2 %fusion.2 = bf16[1024,2048]{1,0:T(8,128)(2,1)} fusion(bf16[1024,1024]{0,1:T(8,128)(2,1)S(1)} %fusion.5, bf16[1024,2176]{1,0:T(8,128)(2,1)} %get-tuple-element.16), kind=kOutput, calls=%fused_computation.4 | convolution fusion | flops 4297064448 | bytes 10485760 | tf_op jit(solution)/shard_map/dot_general | solution.py:225
  165.0 87.0 %all-to-all-done.1.r_ref = bf16[256,4,2176]{2,1,0:T(4,128)(2,1)} async-done(((bf16[256,4,2176]{2,1,0:T(4,128)(2,1)}), bf16[256,4,2176]{2,1,0:T(4,128)(2,1)}, u32[]{:S(2)}, u32[]{:S(2)}) %all-to-all-start.1) | async-done | bytes 4456480 | tf_op jit(solution)/shard_map/all_to_all | solution.py:212
  252.0 6.0 %shard_map.96 = (bf16[512,2048]{1,0:T(8,128)(2,1)}, bf16[512]{0:T(512)(128)(2,1)}) custom-call(s32[1,512]{1,0:T(1,128)} %get-tuple-element.10.target_ref, bf16[256,4,2176]{2,1,0:T(4,128)(2,1)} %all-to-all-done.1.r_ref), custom_call_target="tpu_custom_call" | custom-call | tf_op jit(solution)/shard_map/pallas_call | solution.py:115
  (9 shorter events, 0.1 us)
Async XLA Ops:
  7.0 16.6 %copy-start.2 = (s32[256]{0:T(256)S(1)}, s32[256]{0:T(256)}, u32[]{:S(2)}) copy-start(s32[256]{0:T(256)} %owner_ref.1) | copy-start | bytes 3076
  7.0 16.6 %copy-start.1 = (s32[256,6]{0,1:T(8,128)S(1)}, s32[256,6]{0,1:T(8,128)}, u32[]{:S(2)}) copy-start(s32[256,6]{0,1:T(8,128)} %param.9) | copy-start | bytes 18436
  7.0 119.7 %all-to-all-start = ((bf16[256,4,2176]{2,1,0:T(4,128)(2,1)}), bf16[256,4,2176]{2,1,0:T(4,128)(2,1)}, u32[]{:S(2)}, u32[]{:S(2)}) async-start(bf16[256,4,2176]{2,1,0:T(4,128)(2,1)} %get-tuple-element.11), calls=%async_computation | async-start | bytes 8912896 | tf_op jit(solution)/shard_map/all_to_all | solution.py:203
  141.1 8.0 %copy-start = (bf16[1024,768]{1,0:T(8,128)(2,1)S(1)}, bf16[1024,768]{1,0:T(8,128)(2,1)}, u32[]{:S(2)}) copy-start(bf16[1024,768]{1,0:T(8,128)(2,1)} %get-tuple-element.15) | copy-start | bytes 4718596
  141.1 110.9 %all-to-all-start.1 = ((bf16[256,4,2176]{2,1,0:T(4,128)(2,1)}), bf16[256,4,2176]{2,1,0:T(4,128)(2,1)}, u32[]{:S(2)}, u32[]{:S(2)}) async-start(bf16[256,4,2176]{2,1,0:T(4,128)(2,1)} %get-tuple-element.12), calls=%async_computation.1 | async-start | bytes 8912896 | tf_op jit(solution)/shard_map/all_to_all | solution.py:212

commit v11 on v10

--- a/solution.py
+++ b/solution.py
@@ -18,7 +18,10 @@
 GROUPS_PER_STEP = 128
 
 
-def _place(lang_ref, owner_ref, labels_ref, weights_ref, hidden_ref, o_ref, target_ref, extras_ref):
+def _place(
+    lang_ref, owner_ref, labels_ref, weights_ref, hidden_ref, o_ref, target_ref, column_ref,
+    extras_ref,
+):
     tokens = hidden_ref.shape[0]
     languages = owner_ref.shape[0]
 
@@ -38,6 +41,14 @@
         rank = jnp.sum(jnp.where(before, same, 0.0), axis=0, keepdims=True)
         slot = jnp.dot(owner.astype(jnp.bfloat16), is_lang, preferred_element_type=jnp.float32)
         target_ref[...] = (slot * CAP + rank).astype(jnp.int32)
+        rank_column = jnp.sum(jnp.where(before, 0.0, same) - jnp.where(
+            lax.broadcasted_iota(jnp.int32, (tokens, tokens), 0)
+            == lax.broadcasted_iota(jnp.int32, (tokens, tokens), 1), same, 0.0), axis=1, keepdims=True)
+        slot_column = lax.dot_general(
+            is_lang, owner.astype(jnp.bfloat16), (((0,), (1,)), ((), ())),
+            preferred_element_type=jnp.float32,
+        )
+        column_ref[...] = (slot_column * CAP + rank_column).astype(jnp.int32)
         labels = labels_ref[...].reshape(1, tokens)
         kind = lax.broadcasted_iota(jnp.int32, (EXTRA, tokens), 0)
         extras_ref[...] = jnp.where(
@@ -82,34 +93,37 @@
         out_specs=[
             pl.BlockSpec((step, CAP, width), lambda i: (i, 0, 0)),
             pl.BlockSpec((1, tokens), lambda i: (0, 0)),
+            pl.BlockSpec((tokens, 1), lambda i: (0, 0)),
         ],
         out_shape=[
             jax.ShapeDtypeStruct((groups, CAP, width), hidden.dtype),
             jax.ShapeDtypeStruct((1, tokens), jnp.int32),
+            jax.ShapeDtypeStruct((tokens, 1), jnp.int32),
         ],
         scratch_shapes=[pltpu.VMEM((EXTRA, tokens), jnp.bfloat16)],
     )(token_language.reshape(tokens), language_owner, labels, loss_weight, hidden)
 
 
-def _unplace(target_ref, r_ref, rows_ref, loss_ref):
+def _unplace(target_ref, column_ref, r_ref, rows_ref, loss_ref):
     x = r_ref[...]
     x = x.reshape(x.shape[0] * x.shape[1], x.shape[2])
     tokens = target_ref.shape[1]
     features = rows_ref.shape[1]
+    hot = (
+        lax.broadcasted_iota(jnp.int32, (tokens, x.shape[0]), 1) == column_ref[...]
+    ).astype(jnp.bfloat16)
+    rows = jnp.dot(hot, x[:, :features], preferred_element_type=jnp.float32)
+    rows_ref[...] = rows.astype(rows_ref.dtype)
     hot_t = (lax.broadcasted_iota(jnp.int32, (x.shape[0], tokens), 0) == target_ref[...]).astype(
         jnp.bfloat16
     )
-    rows = lax.dot_general(
-        hot_t, x[:, :features], (((0,), (0,)), ((), ())), preferred_element_type=jnp.float32
-    )
-    rows_ref[...] = rows.astype(rows_ref.dtype)
     loss = lax.dot_general(
         x[:, features:], hot_t, (((0,), (0,)), ((), ())), preferred_element_type=jnp.float32
     )
     loss_ref[...] = loss[0:1, :].astype(loss_ref.dtype).reshape(loss_ref.shape)
 
 
-def unplace(target_row, returned, features):
+def unplace(target_row, target_column, returned, features):
     groups, cap, width = returned.shape
     tokens = target_row.shape[1]
     return pl.pallas_call(
@@ -117,6 +131,7 @@
         grid=(1,),
         in_specs=[
             pl.BlockSpec((1, tokens), lambda i: (0, 0)),
+            pl.BlockSpec((tokens, 1), lambda i: (0, 0)),
             pl.BlockSpec((groups, cap, width), lambda i: (0, 0, 0)),
         ],
         out_specs=[
@@ -127,7 +142,7 @@
             jax.ShapeDtypeStruct((tokens, features), returned.dtype),
             jax.ShapeDtypeStruct((tokens,), returned.dtype),
         ],
-    )(target_row, returned)
+    )(target_row, target_column, returned)
 
 
 def _middle(r_ref, cand_ref, back_ref, rows_ref, grads_ref):
@@ -199,7 +214,7 @@
     places = devices * CAP
     assert head_weight.shape[0] == SB * BLOCK
 
-    send, target_row = place(token_language, language_owner, labels, loss_weight, hidden, devices)
+    send, target_row, target_column = place(token_language, language_owner, labels, loss_weight, hidden, devices)
     received = lax.all_to_all(send, AXES, split_axis=0, concat_axis=0, tiled=True)
 
     self_index = lax.axis_index(AXES)
@@ -227,7 +242,7 @@
         preferred_element_type=jnp.float32,
     ).astype(jnp.bfloat16)
 
-    hidden_grad, token_loss = unplace(target_row, returned, features)
+    hidden_grad, token_loss = unplace(target_row, target_column, returned, features)
     return (hidden_grad, token_loss, head_grad)
 
 

time: 258 us -> 259 us (level)
  no operation moved by 1% of the time
where the time goes in v11:
time: 259 us; the launch traced here: 258 us
  waiting for transfers between devices  185 us (71%)
  Pallas kernels  27 us (10%)
  starting transfers between devices  24.2 us (9%)
  local copies, waits for them, and re-layouts  9.74 us (4%)
  matrix products  8.23 us (3%)
  other arithmetic  3.57 us (1%)
    all_to_all x1, waiting for transfers between devices, shards(): lax.all_to_all(send, AXES, split_axis=0, concat_axis=0, tiled=True)  97.7 us
    all_to_all x1, waiting for transfers between devices, shards(): lax.all_to_all(back, AXES, split_axis=0, concat_axis=0, tiled=True)  87 us
    all_to_all x1, starting transfers between devices, shards(): lax.all_to_all(send, AXES, split_axis=0, concat_axis=0, tiled=True)  16.5 us
    pallas_call x1, Pallas kernels, middle(): pl.pallas_call(_middle, grid=(groups // step,), in_specs=[pl.BlockSpec((s...  14.4 us
    dot_general x1, matrix products, shards(): lax.dot_general(expanded, token_rows[:, :features], (((0,), (0,)), ((), (...  8.23 us
    all_to_all x1, starting transfers between devices, shards(): lax.all_to_all(back, AXES, split_axis=0, concat_axis=0, tiled=True)  7.67 us
    pallas_call x1, Pallas kernels, place(): pl.pallas_call(_place, grid=(groups // step,), in_specs=[pl.BlockSpec((to...  6.46 us
    pallas_call x1, Pallas kernels, unplace(): pl.pallas_call(_unplace, grid=(1,), in_specs=[pl.BlockSpec((1, tokens), l...  6.13 us
  transfers between devices with their start and end apart: 2, of which 2 were waited for; matrix products, arithmetic and copies ran while one was open for 8% of the time, Pallas kernels for 0%

profile of v11, /device:TPU:1, one launch (start us, length us, event | category | flops | bytes accessed | tf_op | source)
XLA Modules:
  0.0 258.2 jit_solution(6121764080462092083)
XLA Ops:
  0.6 6.5 %shard_map.94 = (bf16[256,4,2176]{2,1,0:T(4,128)(2,1)}, s32[1,512]{1,0:T(1,128)}, s32[512,1]{1,0:T(8,128)}) custom-call(s32[512]{0:T(512)} %bitcast.28, s32[256]{0:T(256)} %owner_ref.1, s32[512]{0:T(512)} %labels_ref.1, bf16[512]{0:T(512)(128)(2,1)} %weights_ref.1, bf16[512,2048]{1,0:T(8,128)(2,1)} %hidden_ref.1), custom_call_target="tpu_custom_call" | custom-call | tf_op jit(solution)/shard_map/pallas_call | solution.py:83
  7.1 0.0 copy-start.2
  7.1 16.5 %all-to-all-start = ((bf16[256,4,2176]{2,1,0:T(4,128)(2,1)}), bf16[256,4,2176]{2,1,0:T(4,128)(2,1)}, u32[]{:S(2)}, u32[]{:S(2)}) async-start(bf16[256,4,2176]{2,1,0:T(4,128)(2,1)} %get-tuple-element.13), calls=%async_computation | async-start | bytes 8912896 | tf_op jit(solution)/shard_map/all_to_all | solution.py:218
  23.7 0.0 copy-done.2
  23.7 0.0 copy-done.1
  23.7 0.1 multiply_reduce_fusion
  23.8 2.9 %gather_fusion = bf16[6,128,2048]{2,1,0:T(8,128)(2,1)S(1)} fusion(bf16[8,128,2048]{2,1,0:T(8,128)(2,1)} %bitcast.27, s32[1024]{0:T(1024)S(1)} %pad_clamp_fusion.1), kind=kCustom, calls=%fused_computation | custom fusion | bytes 6291480 | tf_op jit(solution)/shard_map/jit(_take)/gather | solution.py:224
  26.8 0.1 broadcast_bitcast_fusion.2
  26.9 2.2 bitcast_select_fusion.cand_ref
  29.1 97.7 %all-to-all-done.r_ref = bf16[256,4,2176]{2,1,0:T(4,128)(2,1)} async-done(((bf16[256,4,2176]{2,1,0:T(4,128)(2,1)}), bf16[256,4,2176]{2,1,0:T(4,128)(2,1)}, u32[]{:S(2)}, u32[]{:S(2)}) %all-to-all-start) | async-done | bytes 4456480 | tf_op jit(solution)/shard_map/all_to_all | solution.py:218
  126.8 14.4 %shard_map.95 = (bf16[256,4,2176]{2,1,0:T(4,128)(2,1)}, bf16[1024,2176]{1,0:T(8,128)(2,1)}, bf16[1024,768]{1,0:T(8,128)(2,1)}) custom-call(bf16[256,4,2176]{2,1,0:T(4,128)(2,1)} %all-to-all-done.r_ref, bf16[768,2048]{1,0:T(8,128)(2,1)} %bitcast_select_fusion.cand_ref), custom_call_target="tpu_custom_call" | custom-call | tf_op jit(solution)/shard_map/pallas_call | solution.py:189
  141.2 7.7 %all-to-all-start.1 = ((bf16[256,4,2176]{2,1,0:T(4,128)(2,1)}), bf16[256,4,2176]{2,1,0:T(4,128)(2,1)}, u32[]{:S(2)}, u32[]{:S(2)}) async-start(bf16[256,4,2176]{2,1,0:T(4,128)(2,1)} %get-tuple-element.14), calls=%async_computation.1 | async-start | bytes 8912896 | tf_op jit(solution)/shard_map/all_to_all | solution.py:227
  148.9 0.1 fusion.6
  149.0 0.1 select_reduce_fusion
  149.1 0.1 broadcast_bitcast_fusion
  149.2 0.0 copy-done
  149.2 0.8 copy.15
  150.0 0.9 copy.16
  150.9 2.1 gather_fusion.1
  153.0 2.9 %copy.17 = bf16[1024,8,128]{0,2,1:T(8,128)(2,1)S(1)} copy(bf16[1024,8,128]{2,0,1:T(8,128)(2,1)} %bitcast.25) | data formatting | bytes 4194304 | tf_op jit(solution)/shard_map/jit(_take)/gather | solution.py:237
  155.9 1.0 fusion.5
  156.8 8.2 %fusion.2 = bf16[1024,2048]{1,0:T(8,128)(2,1)} fusion(bf16[1024,1024]{0,1:T(8,128)(2,1)S(1)} %fusion.5, bf16[1024,2176]{1,0:T(8,128)(2,1)} %get-tuple-element.18), kind=kOutput, calls=%fused_computation.4 | convolution fusion | flops 4297064448 | bytes 10485760 | tf_op jit(solution)/shard_map/dot_general | solution.py:240
  165.1 87.0 %all-to-all-done.1.r_ref = bf16[256,4,2176]{2,1,0:T(4,128)(2,1)} async-done(((bf16[256,4,2176]{2,1,0:T(4,128)(2,1)}), bf16[256,4,2176]{2,1,0:T(4,128)(2,1)}, u32[]{:S(2)}, u32[]{:S(2)}) %all-to-all-start.1) | async-done | bytes 4456480 | tf_op jit(solution)/shard_map/all_to_all | solution.py:227
  252.1 6.1 %shard_map.96 = (bf16[512,2048]{1,0:T(8,128)(2,1)}, bf16[512]{0:T(512)(128)(2,1)}) custom-call(s32[1,512]{1,0:T(1,128)} %get-tuple-element.11.target_ref, s32[512,1]{1,0:T(8,128)} %get-tuple-element.12.column_ref, bf16[256,4,2176]{2,1,0:T(4,128)(2,1)} %all-to-all-done.1.r_ref), custom_call_target="tpu_custom_call" | custom-call | tf_op jit(solution)/shard_map/pallas_call | solution.py:129
  (9 shorter events, 0.1 us)
Async XLA Ops:
  7.1 16.6 %copy-start.2 = (s32[256]{0:T(256)S(1)}, s32[256]{0:T(256)}, u32[]{:S(2)}) copy-start(s32[256]{0:T(256)} %owner_ref.1) | copy-start | bytes 3076
  7.1 16.6 %copy-start.1 = (s32[256,6]{0,1:T(8,128)S(1)}, s32[256,6]{0,1:T(8,128)}, u32[]{:S(2)}) copy-start(s32[256,6]{0,1:T(8,128)} %param.9) | copy-start | bytes 18436
  7.1 119.7 %all-to-all-start = ((bf16[256,4,2176]{2,1,0:T(4,128)(2,1)}), bf16[256,4,2176]{2,1,0:T(4,128)(2,1)}, u32[]{:S(2)}, u32[]{:S(2)}) async-start(bf16[256,4,2176]{2,1,0:T(4,128)(2,1)} %get-tuple-element.13), calls=%async_computation | async-start | bytes 8912896 | tf_op jit(solution)/shard_map/all_to_all | solution.py:218
  141.2 8.0 %copy-start = (bf16[1024,768]{1,0:T(8,128)(2,1)S(1)}, bf16[1024,768]{1,0:T(8,128)(2,1)}, u32[]{:S(2)}) copy-start(bf16[1024,768]{1,0:T(8,128)(2,1)} %get-tuple-element.17) | copy-start | bytes 4718596
  141.2 110.9 %all-to-all-start.1 = ((bf16[256,4,2176]{2,1,0:T(4,128)(2,1)}), bf16[256,4,2176]{2,1,0:T(4,128)(2,1)}, u32[]{:S(2)}, u32[]{:S(2)}) async-start(bf16[256,4,2176]{2,1,0:T(4,128)(2,1)} %get-tuple-element.14), calls=%async_computation.1 | async-start | bytes 8912896 | tf_op jit(solution)/shard_map/all_to_all | solution.py:227

commit v12 on v10

--- a/solution.py
+++ b/solution.py
@@ -92,32 +92,44 @@
 
 
 def _unplace(target_ref, r_ref, rows_ref, loss_ref):
+    i = pl.program_id(0)
     x = r_ref[...]
     x = x.reshape(x.shape[0] * x.shape[1], x.shape[2])
     tokens = target_ref.shape[1]
     features = rows_ref.shape[1]
-    hot_t = (lax.broadcasted_iota(jnp.int32, (x.shape[0], tokens), 0) == target_ref[...]).astype(
-        jnp.bfloat16
-    )
+    hot_t = (
+        lax.broadcasted_iota(jnp.int32, (x.shape[0], tokens), 0) + i * x.shape[0]
+        == target_ref[...]
+    ).astype(jnp.bfloat16)
     rows = lax.dot_general(
         hot_t, x[:, :features], (((0,), (0,)), ((), ())), preferred_element_type=jnp.float32
-    )
-    rows_ref[...] = rows.astype(rows_ref.dtype)
+    ).astype(rows_ref.dtype)
     loss = lax.dot_general(
         x[:, features:], hot_t, (((0,), (0,)), ((), ())), preferred_element_type=jnp.float32
     )
-    loss_ref[...] = loss[0:1, :].astype(loss_ref.dtype).reshape(loss_ref.shape)
+    loss = loss[0:1, :].astype(loss_ref.dtype).reshape(loss_ref.shape)
+
+    @pl.when(i == 0)
+    def _():
+        rows_ref[...] = rows
+        loss_ref[...] = loss
+
+    @pl.when(i > 0)
+    def _():
+        rows_ref[...] = rows_ref[...] + rows
+        loss_ref[...] = loss_ref[...] + loss
 
 
 def unplace(target_row, returned, features):
     groups, cap, width = returned.shape
     tokens = target_row.shape[1]
+    step = groups // 2
     return pl.pallas_call(
         _unplace,
-        grid=(1,),
+        grid=(groups // step,),
         in_specs=[
             pl.BlockSpec((1, tokens), lambda i: (0, 0)),
-            pl.BlockSpec((groups, cap, width), lambda i: (0, 0, 0)),
+            pl.BlockSpec((step, cap, width), lambda i: (i, 0, 0)),
         ],
         out_specs=[
             pl.BlockSpec((tokens, features), lambda i: (0, 0)),

time: 258 us -> 259 us (level)
  no operation moved by 1% of the time
where the time goes in v12:
time: 259 us; the launch traced here: 258 us
  waiting for transfers between devices  185 us (71%)
  Pallas kernels  26.9 us (10%)
  starting transfers between devices  24.2 us (9%)
  local copies, waits for them, and re-layouts  9.74 us (4%)
  matrix products  8.23 us (3%)
  other arithmetic  3.57 us (1%)
    all_to_all x1, waiting for transfers between devices, shards(): lax.all_to_all(send, AXES, split_axis=0, concat_axis=0, tiled=True)  97.7 us
    all_to_all x1, waiting for transfers between devices, shards(): lax.all_to_all(back, AXES, split_axis=0, concat_axis=0, tiled=True)  87 us
    all_to_all x1, starting transfers between devices, shards(): lax.all_to_all(send, AXES, split_axis=0, concat_axis=0, tiled=True)  16.5 us
    pallas_call x1, Pallas kernels, middle(): pl.pallas_call(_middle, grid=(groups // step,), in_specs=[pl.BlockSpec((s...  14.4 us
    dot_general x1, matrix products, shards(): lax.dot_general(expanded, token_rows[:, :features], (((0,), (0,)), ((), (...  8.23 us
    all_to_all x1, starting transfers between devices, shards(): lax.all_to_all(back, AXES, split_axis=0, concat_axis=0, tiled=True)  7.67 us
    pallas_call x1, Pallas kernels, place(): pl.pallas_call(_place, grid=(groups // step,), in_specs=[pl.BlockSpec((to...  6.35 us
    pallas_call x1, Pallas kernels, unplace(): pl.pallas_call(_unplace, grid=(groups // step,), in_specs=[pl.BlockSpec((...  6.18 us
  transfers between devices with their start and end apart: 2, of which 2 were waited for; matrix products, arithmetic and copies ran while one was open for 8% of the time, Pallas kernels for 0%

profile of v12, /device:TPU:1, one launch (start us, length us, event | category | flops | bytes accessed | tf_op | source)
XLA Modules:
  0.0 258.1 jit_solution(7633919528385586407)
XLA Ops:
  0.6 6.3 %shard_map.94 = (bf16[256,4,2176]{2,1,0:T(4,128)(2,1)}, s32[1,512]{1,0:T(1,128)}) custom-call(s32[512]{0:T(512)} %bitcast.28, s32[256]{0:T(256)} %owner_ref.1, s32[512]{0:T(512)} %labels_ref.1, bf16[512]{0:T(512)(128)(2,1)} %weights_ref.1, bf16[512,2048]{1,0:T(8,128)(2,1)} %hidden_ref.1), custom_call_target="tpu_custom_call" | custom-call | tf_op jit(solution)/shard_map/pallas_call | solution.py:72
  7.0 0.0 copy-start.2
  7.0 16.5 %all-to-all-start = ((bf16[256,4,2176]{2,1,0:T(4,128)(2,1)}), bf16[256,4,2176]{2,1,0:T(4,128)(2,1)}, u32[]{:S(2)}, u32[]{:S(2)}) async-start(bf16[256,4,2176]{2,1,0:T(4,128)(2,1)} %get-tuple-element.11), calls=%async_computation | async-start | bytes 8912896 | tf_op jit(solution)/shard_map/all_to_all | solution.py:215
  23.5 0.0 copy-done.2
  23.6 0.0 copy-done.1
  23.6 0.1 multiply_reduce_fusion
  23.7 2.9 %gather_fusion = bf16[6,128,2048]{2,1,0:T(8,128)(2,1)S(1)} fusion(bf16[8,128,2048]{2,1,0:T(8,128)(2,1)} %bitcast.27, s32[1024]{0:T(1024)S(1)} %pad_clamp_fusion.1), kind=kCustom, calls=%fused_computation | custom fusion | bytes 6291480 | tf_op jit(solution)/shard_map/jit(_take)/gather | solution.py:221
  26.7 0.1 broadcast_bitcast_fusion.2
  26.7 2.2 bitcast_select_fusion.cand_ref
  28.9 97.7 %all-to-all-done.r_ref = bf16[256,4,2176]{2,1,0:T(4,128)(2,1)} async-done(((bf16[256,4,2176]{2,1,0:T(4,128)(2,1)}), bf16[256,4,2176]{2,1,0:T(4,128)(2,1)}, u32[]{:S(2)}, u32[]{:S(2)}) %all-to-all-start) | async-done | bytes 4456480 | tf_op jit(solution)/shard_map/all_to_all | solution.py:215
  126.6 14.4 %shard_map.95 = (bf16[256,4,2176]{2,1,0:T(4,128)(2,1)}, bf16[1024,2176]{1,0:T(8,128)(2,1)}, bf16[1024,768]{1,0:T(8,128)(2,1)}) custom-call(bf16[256,4,2176]{2,1,0:T(4,128)(2,1)} %all-to-all-done.r_ref, bf16[768,2048]{1,0:T(8,128)(2,1)} %bitcast_select_fusion.cand_ref), custom_call_target="tpu_custom_call" | custom-call | tf_op jit(solution)/shard_map/pallas_call | solution.py:186
  141.1 7.7 %all-to-all-start.1 = ((bf16[256,4,2176]{2,1,0:T(4,128)(2,1)}), bf16[256,4,2176]{2,1,0:T(4,128)(2,1)}, u32[]{:S(2)}, u32[]{:S(2)}) async-start(bf16[256,4,2176]{2,1,0:T(4,128)(2,1)} %get-tuple-element.12), calls=%async_computation.1 | async-start | bytes 8912896 | tf_op jit(solution)/shard_map/all_to_all | solution.py:224
  148.7 0.1 fusion.6
  148.9 0.1 select_reduce_fusion
  149.0 0.1 broadcast_bitcast_fusion
  149.1 0.0 copy-done
  149.1 0.8 copy.15
  149.9 0.9 copy.16
  150.8 2.1 gather_fusion.1
  152.9 2.9 %copy.17 = bf16[1024,8,128]{0,2,1:T(8,128)(2,1)S(1)} copy(bf16[1024,8,128]{2,0,1:T(8,128)(2,1)} %bitcast.25) | data formatting | bytes 4194304 | tf_op jit(solution)/shard_map/jit(_take)/gather | solution.py:234
  155.8 1.0 fusion.5
  156.7 8.2 %fusion.2 = bf16[1024,2048]{1,0:T(8,128)(2,1)} fusion(bf16[1024,1024]{0,1:T(8,128)(2,1)S(1)} %fusion.5, bf16[1024,2176]{1,0:T(8,128)(2,1)} %get-tuple-element.16), kind=kOutput, calls=%fused_computation.4 | convolution fusion | flops 4297064448 | bytes 10485760 | tf_op jit(solution)/shard_map/dot_general | solution.py:237
  165.0 87.0 %all-to-all-done.1.r_ref = bf16[256,4,2176]{2,1,0:T(4,128)(2,1)} async-done(((bf16[256,4,2176]{2,1,0:T(4,128)(2,1)}), bf16[256,4,2176]{2,1,0:T(4,128)(2,1)}, u32[]{:S(2)}, u32[]{:S(2)}) %all-to-all-start.1) | async-done | bytes 4456480 | tf_op jit(solution)/shard_map/all_to_all | solution.py:224
  252.0 6.2 %shard_map.96 = (bf16[512,2048]{1,0:T(8,128)(2,1)}, bf16[512]{0:T(512)(128)(2,1)}) custom-call(s32[1,512]{1,0:T(1,128)} %get-tuple-element.10.target_ref, bf16[256,4,2176]{2,1,0:T(4,128)(2,1)} %all-to-all-done.1.r_ref), custom_call_target="tpu_custom_call" | custom-call | tf_op jit(solution)/shard_map/pallas_call | solution.py:127
  (9 shorter events, 0.1 us)
Async XLA Ops:
  7.0 16.6 %copy-start.2 = (s32[256]{0:T(256)S(1)}, s32[256]{0:T(256)}, u32[]{:S(2)}) copy-start(s32[256]{0:T(256)} %owner_ref.1) | copy-start | bytes 3076
  7.0 16.6 %copy-start.1 = (s32[256,6]{0,1:T(8,128)S(1)}, s32[256,6]{0,1:T(8,128)}, u32[]{:S(2)}) copy-start(s32[256,6]{0,1:T(8,128)} %param.9) | copy-start | bytes 18436
  7.0 119.7 %all-to-all-start = ((bf16[256,4,2176]{2,1,0:T(4,128)(2,1)}), bf16[256,4,2176]{2,1,0:T(4,128)(2,1)}, u32[]{:S(2)}, u32[]{:S(2)}) async-start(bf16[256,4,2176]{2,1,0:T(4,128)(2,1)} %get-tuple-element.11), calls=%async_computation | async-start | bytes 8912896 | tf_op jit(solution)/shard_map/all_to_all | solution.py:215
  141.1 8.0 %copy-start = (bf16[1024,768]{1,0:T(8,128)(2,1)S(1)}, bf16[1024,768]{1,0:T(8,128)(2,1)}, u32[]{:S(2)}) copy-start(bf16[1024,768]{1,0:T(8,128)(2,1)} %get-tuple-element.15) | copy-start | bytes 4718596
  141.1 110.9 %all-to-all-start.1 = ((bf16[256,4,2176]{2,1,0:T(4,128)(2,1)}), bf16[256,4,2176]{2,1,0:T(4,128)(2,1)}, u32[]{:S(2)}, u32[]{:S(2)}) async-start(bf16[256,4,2176]{2,1,0:T(4,128)(2,1)} %get-tuple-element.12), calls=%async_computation.1 | async-start | bytes 8912896 | tf_op jit(solution)/shard_map/all_to_all | solution.py:224

commit v13 on v10

--- a/solution.py
+++ b/solution.py
@@ -67,7 +67,7 @@
     tokens, features = hidden.shape
     languages = language_owner.shape[0]
     width = features + EXTRA
-    step = min(GROUPS_PER_STEP, groups)
+    step = groups
     whole = lambda i: (0,)
     return pl.pallas_call(
         _place,

time: 258 us -> 259 us (level)
  no operation moved by 1% of the time
where the time goes in v13:
time: 259 us; the launch traced here: 258 us
  waiting for transfers between devices  185 us (71%)
  Pallas kernels  27.2 us (11%)
  starting transfers between devices  24.2 us (9%)
  local copies, waits for them, and re-layouts  9.74 us (4%)
  matrix products  8.23 us (3%)
  other arithmetic  3.57 us (1%)
    all_to_all x1, waiting for transfers between devices, shards(): lax.all_to_all(send, AXES, split_axis=0, concat_axis=0, tiled=True)  97.7 us
    all_to_all x1, waiting for transfers between devices, shards(): lax.all_to_all(back, AXES, split_axis=0, concat_axis=0, tiled=True)  87 us
    all_to_all x1, starting transfers between devices, shards(): lax.all_to_all(send, AXES, split_axis=0, concat_axis=0, tiled=True)  16.5 us
    pallas_call x1, Pallas kernels, middle(): pl.pallas_call(_middle, grid=(groups // step,), in_specs=[pl.BlockSpec((s...  14.4 us
    dot_general x1, matrix products, shards(): lax.dot_general(expanded, token_rows[:, :features], (((0,), (0,)), ((), (...  8.23 us
    all_to_all x1, starting transfers between devices, shards(): lax.all_to_all(back, AXES, split_axis=0, concat_axis=0, tiled=True)  7.67 us
    pallas_call x1, Pallas kernels, place(): pl.pallas_call(_place, grid=(groups // step,), in_specs=[pl.BlockSpec((to...  6.75 us
    pallas_call x1, Pallas kernels, unplace(): pl.pallas_call(_unplace, grid=(1,), in_specs=[pl.BlockSpec((1, tokens), l...  6.04 us
  transfers between devices with their start and end apart: 2, of which 2 were waited for; matrix products, arithmetic and copies ran while one was open for 8% of the time, Pallas kernels for 0%

profile of v13, /device:TPU:1, one launch (start us, length us, event | category | flops | bytes accessed | tf_op | source)
XLA Modules:
  0.0 258.4 jit_solution(16932773806237247101)
XLA Ops:
  0.6 6.7 %shard_map.94 = (bf16[256,4,2176]{2,1,0:T(4,128)(2,1)}, s32[1,512]{1,0:T(1,128)}) custom-call(s32[512]{0:T(512)} %bitcast.28, s32[256]{0:T(256)} %owner_ref.1, s32[512]{0:T(512)} %labels_ref.1, bf16[512]{0:T(512)(128)(2,1)} %weights_ref.1, bf16[512,2048]{1,0:T(8,128)(2,1)} %hidden_ref.1), custom_call_target="tpu_custom_call" | custom-call | tf_op jit(solution)/shard_map/pallas_call | solution.py:72
  7.4 0.0 copy-start.2
  7.4 16.5 %all-to-all-start = ((bf16[256,4,2176]{2,1,0:T(4,128)(2,1)}), bf16[256,4,2176]{2,1,0:T(4,128)(2,1)}, u32[]{:S(2)}, u32[]{:S(2)}) async-start(bf16[256,4,2176]{2,1,0:T(4,128)(2,1)} %get-tuple-element.11), calls=%async_computation | async-start | bytes 8912896 | tf_op jit(solution)/shard_map/all_to_all | solution.py:203
  23.9 0.0 copy-done.2
  23.9 0.0 copy-done.1
  24.0 0.1 multiply_reduce_fusion
  24.1 2.9 %gather_fusion = bf16[6,128,2048]{2,1,0:T(8,128)(2,1)S(1)} fusion(bf16[8,128,2048]{2,1,0:T(8,128)(2,1)} %bitcast.27, s32[1024]{0:T(1024)S(1)} %pad_clamp_fusion.1), kind=kCustom, calls=%fused_computation | custom fusion | bytes 6291480 | tf_op jit(solution)/shard_map/jit(_take)/gather | solution.py:209
  27.1 0.1 broadcast_bitcast_fusion.2
  27.1 2.2 bitcast_select_fusion.cand_ref
  29.3 97.7 %all-to-all-done.r_ref = bf16[256,4,2176]{2,1,0:T(4,128)(2,1)} async-done(((bf16[256,4,2176]{2,1,0:T(4,128)(2,1)}), bf16[256,4,2176]{2,1,0:T(4,128)(2,1)}, u32[]{:S(2)}, u32[]{:S(2)}) %all-to-all-start) | async-done | bytes 4456480 | tf_op jit(solution)/shard_map/all_to_all | solution.py:203
  127.0 14.4 %shard_map.95 = (bf16[256,4,2176]{2,1,0:T(4,128)(2,1)}, bf16[1024,2176]{1,0:T(8,128)(2,1)}, bf16[1024,768]{1,0:T(8,128)(2,1)}) custom-call(bf16[256,4,2176]{2,1,0:T(4,128)(2,1)} %all-to-all-done.r_ref, bf16[768,2048]{1,0:T(8,128)(2,1)} %bitcast_select_fusion.cand_ref), custom_call_target="tpu_custom_call" | custom-call | tf_op jit(solution)/shard_map/pallas_call | solution.py:174
  141.5 7.7 %all-to-all-start.1 = ((bf16[256,4,2176]{2,1,0:T(4,128)(2,1)}), bf16[256,4,2176]{2,1,0:T(4,128)(2,1)}, u32[]{:S(2)}, u32[]{:S(2)}) async-start(bf16[256,4,2176]{2,1,0:T(4,128)(2,1)} %get-tuple-element.12), calls=%async_computation.1 | async-start | bytes 8912896 | tf_op jit(solution)/shard_map/all_to_all | solution.py:212
  149.1 0.1 fusion.6
  149.3 0.1 select_reduce_fusion
  149.4 0.1 broadcast_bitcast_fusion
  149.5 0.0 copy-done
  149.5 0.8 copy.15
  150.2 0.9 copy.16
  151.1 2.1 gather_fusion.1
  153.3 2.9 %copy.17 = bf16[1024,8,128]{0,2,1:T(8,128)(2,1)S(1)} copy(bf16[1024,8,128]{2,0,1:T(8,128)(2,1)} %bitcast.25) | data formatting | bytes 4194304 | tf_op jit(solution)/shard_map/jit(_take)/gather | solution.py:222
  156.1 1.0 fusion.5
  157.1 8.2 %fusion.2 = bf16[1024,2048]{1,0:T(8,128)(2,1)} fusion(bf16[1024,1024]{0,1:T(8,128)(2,1)S(1)} %fusion.5, bf16[1024,2176]{1,0:T(8,128)(2,1)} %get-tuple-element.16), kind=kOutput, calls=%fused_computation.4 | convolution fusion | flops 4297064448 | bytes 10485760 | tf_op jit(solution)/shard_map/dot_general | solution.py:225
  165.3 87.0 %all-to-all-done.1.r_ref = bf16[256,4,2176]{2,1,0:T(4,128)(2,1)} async-done(((bf16[256,4,2176]{2,1,0:T(4,128)(2,1)}), bf16[256,4,2176]{2,1,0:T(4,128)(2,1)}, u32[]{:S(2)}, u32[]{:S(2)}) %all-to-all-start.1) | async-done | bytes 4456480 | tf_op jit(solution)/shard_map/all_to_all | solution.py:212
  252.3 6.0 %shard_map.96 = (bf16[512,2048]{1,0:T(8,128)(2,1)}, bf16[512]{0:T(512)(128)(2,1)}) custom-call(s32[1,512]{1,0:T(1,128)} %get-tuple-element.10.target_ref, bf16[256,4,2176]{2,1,0:T(4,128)(2,1)} %all-to-all-done.1.r_ref), custom_call_target="tpu_custom_call" | custom-call | tf_op jit(solution)/shard_map/pallas_call | solution.py:115
  (9 shorter events, 0.1 us)
Async XLA Ops:
  7.4 16.5 %copy-start.2 = (s32[256]{0:T(256)S(1)}, s32[256]{0:T(256)}, u32[]{:S(2)}) copy-start(s32[256]{0:T(256)} %owner_ref.1) | copy-start | bytes 3076
  7.4 16.6 %copy-start.1 = (s32[256,6]{0,1:T(8,128)S(1)}, s32[256,6]{0,1:T(8,128)}, u32[]{:S(2)}) copy-start(s32[256,6]{0,1:T(8,128)} %param.9) | copy-start | bytes 18436
  7.4 119.6 %all-to-all-start = ((bf16[256,4,2176]{2,1,0:T(4,128)(2,1)}), bf16[256,4,2176]{2,1,0:T(4,128)(2,1)}, u32[]{:S(2)}, u32[]{:S(2)}) async-start(bf16[256,4,2176]{2,1,0:T(4,128)(2,1)} %get-tuple-element.11), calls=%async_computation | async-start | bytes 8912896 | tf_op jit(solution)/shard_map/all_to_all | solution.py:203
  141.5 8.0 %copy-start = (bf16[1024,768]{1,0:T(8,128)(2,1)S(1)}, bf16[1024,768]{1,0:T(8,128)(2,1)}, u32[]{:S(2)}) copy-start(bf16[1024,768]{1,0:T(8,128)(2,1)} %get-tuple-element.15) | copy-start | bytes 4718596
  141.5 110.9 %all-to-all-start.1 = ((bf16[256,4,2176]{2,1,0:T(4,128)(2,1)}), bf16[256,4,2176]{2,1,0:T(4,128)(2,1)}, u32[]{:S(2)}, u32[]{:S(2)}) async-start(bf16[256,4,2176]{2,1,0:T(4,128)(2,1)} %get-tuple-element.12), calls=%async_computation.1 | async-start | bytes 8912896 | tf_op jit(solution)/shard_map/all_to_all | solution.py:212
